TPU v7x, 512 devices: a whole 4x8x8 slice. The times are simulated.
512 devices in a mesh: section: 16 (over y, core), seq: 32 (over x, z).
Axes of the slice: x: 4, y: 8, z: 8, core: 2. Of those that a mesh axis runs over, the one named last changes fastest.
Arguments:
- queries: bfloat16 [16, 4096, 4096], P('section', 'seq'), may hold values from -15 to 15, as said below
- keys: bfloat16 [16, 4096, 512], P('section', 'seq'), may hold values from -6 to 6, as said below
- values: bfloat16 [16, 4096, 512], P('section', 'seq'), may hold values from -6 to 6
- cache_keys: bfloat16 [16, 32, 512, 128], P('section', 'seq'), may hold values from -6 to 6
- cache_values: bfloat16 [16, 32, 512, 128], P('section', 'seq'), may hold values from -6 to 6
- vertical: int32 [16, 32, 32], P('section', 'seq'), may hold values from 0 to 63, as said below
- vertical_count: int32 [16, 32], P('section', 'seq'), may hold values from 1 to 32, as said below
- slash: int32 [16, 32, 11], P('section', 'seq'), may hold values from 1 to 127, as said below
Outputs:
- attended: bfloat16 [16, 4096, 4096], P('section', 'seq')
Inputs may be any that keep to these rules, and one draw needn't show every extreme that they name: queries within the range in both draws. keys within the range in both draws. `vertical`: for each layer and head, the 32 entries are distinct cached block indices. `vertical_count`: in every layer some head uses all 32 slots. `slash`: for each layer and head, the 11 offsets are distinct.
All inputs are finite; a program needn't handle non-finite values.
Results may differ from a plain program's by a relative error of at most 0.011.
Values may be sent and summed in bfloat16 or wider, within the bound.
No kernel may reach another device: no remote copies, remote signals or barrier semaphores. Data moves between devices by JAX's collectives and lax.ppermute only.
A program may use at most 64 MiB of HBM per device.

v0:
```python
import math

import jax
import jax.numpy as jnp
from jax import lax
from jax.sharding import PartitionSpec as P

HEAD_SIZE = 128
GROUP = 8
BLK = 64
TILE = 4
NVMAX = 32
NS = 11
CACHE = 4096


big_negative = -1e30


def from_partner(value, axis, distance):
    mask = 2**distance
    pairs = [(source, source ^ mask) for source in range(lax.axis_size(axis))]
    return lax.ppermute(value, axis, pairs)


def from_behind(x, axis, by):
    peers = lax.axis_size(axis)
    return lax.ppermute(x, axis, [(i, (i + by) % peers) for i in range(peers)])


def online_update(carry, scores, allowed, contract):
    top, total, accum = carry
    masked = jnp.where(allowed, scores, big_negative)
    new_top = jnp.maximum(top, jnp.max(masked, axis=-1))
    factor = jnp.exp(top - new_top)
    attention_weight = jnp.where(allowed, jnp.exp(scores - new_top[..., None]), 0.0)
    total = total * factor + jnp.sum(attention_weight, axis=-1)
    accum = accum * factor[..., None] + contract(attention_weight.astype(jnp.bfloat16))
    return (new_top, total, accum)


def vertical_run(query_matrix, verts, count, first_tile, last_tile, all_kv, carry):
    softmax_scale = 1.0 / math.sqrt(HEAD_SIZE)
    span = TILE * BLK
    slot_ids = jnp.arange(TILE, dtype=jnp.int32)
    block_view = all_kv.reshape(all_kv.shape[0] // BLK, BLK, 2 * HEAD_SIZE)

    def step(tile, state):
        picked = lax.dynamic_slice_in_dim(verts, tile * TILE, TILE)
        kv_tile = jnp.take(block_view, picked, axis=0).reshape(span, 2 * HEAD_SIZE)
        key_tile = kv_tile[:, :HEAD_SIZE]
        value_tile = kv_tile[:, HEAD_SIZE:]
        live = jnp.repeat(tile * TILE + slot_ids < count, BLK)
        scores = (
            lax.dot_general(
                query_matrix, key_tile, (((1,), (1,)), ((), ())), preferred_element_type=jnp.float32
            )
            * softmax_scale
        )

        def contract(attention_weight):
            return jnp.dot(attention_weight, value_tile, preferred_element_type=jnp.float32)

        return online_update(state, scores, live[None, :], contract)

    return lax.fori_loop(first_tile, last_tile, step, carry)


def slash_run(query_matrix, verts, count, slashes, all_kv, carry):
    softmax_scale = 1.0 / math.sqrt(HEAD_SIZE)
    prefill_stretch = query_matrix.shape[0]
    ncb = CACHE // BLK
    nqb = prefill_stretch // BLK
    per = math.gcd(nqb, max(1, 512 // BLK))
    rounds = nqb // per
    width = (NS + 1) * BLK
    inner = jnp.arange(BLK, dtype=jnp.int32)
    offsets = jnp.concatenate([jnp.zeros((1,), jnp.int32), slashes])
    blocks = ncb + jnp.arange(nqb, dtype=jnp.int32)[:, None] - offsets[None, :]
    used = jnp.arange(NVMAX, dtype=jnp.int32)[None, None, :] < count
    listed = jnp.any((blocks[:, :, None] == verts[None, None, :]) & used, axis=2)
    valid = (blocks >= 0) & jnp.logical_not(listed)
    column = jnp.arange(width, dtype=jnp.int32)
    causal = (column[None, :] >= BLK) | ((column % BLK)[None, :] <= inner[:, None])
    padded = jnp.concatenate(
        [jnp.zeros((prefill_stretch, 2 * HEAD_SIZE), all_kv.dtype), all_kv], axis=0
    )
    starts = (nqb + ncb - offsets) * BLK
    top, total, accum = carry

    def one_round(items):
        round_id, local_query_share, valid_part, top_part, total_part, accum_part = items
        base = round_id * (per * BLK)

        def cut(start_row):
            return lax.dynamic_slice_in_dim(padded, start_row + base, per * BLK, 0)

        slabs = jax.vmap(cut)(starts)
        shares = (
            slabs.reshape(NS + 1, per, BLK, 2 * HEAD_SIZE)
            .transpose(1, 0, 2, 3)
            .reshape(per, width, 2 * HEAD_SIZE)
        )
        local_key_share = shares[:, :, :HEAD_SIZE]
        local_value_share = shares[:, :, HEAD_SIZE:]
        scores = (
            jnp.einsum(
                "cra,cma->crm",
                local_query_share,
                local_key_share,
                preferred_element_type=jnp.float32,
            )
            * softmax_scale
        )
        allowed = jnp.repeat(valid_part, BLK, axis=1)[:, None, :] & causal[None, :, :]

        def contract(attention_weight):
            return jnp.einsum(
                "owu,out->owt",
                attention_weight,
                local_value_share,
                preferred_element_type=jnp.float32,
            )

        return online_update((top_part, total_part, accum_part), scores, allowed, contract)

    items = (
        jnp.arange(rounds, dtype=jnp.int32),
        query_matrix.reshape(rounds, per, BLK, HEAD_SIZE),
        valid.reshape(rounds, per, NS + 1),
        top.reshape(rounds, per, BLK),
        total.reshape(rounds, per, BLK),
        accum.reshape(rounds, per, BLK, HEAD_SIZE),
    )
    new_top, new_total, new_accum = lax.map(one_round, items)
    return (
        new_top.reshape(prefill_stretch),
        new_total.reshape(prefill_stretch),
        new_accum.reshape(prefill_stretch, HEAD_SIZE),
    )


def assemble(piece, bits, rank):
    for bit in range(bits):
        other = from_partner(piece, "seq", bit)
        upper = rank // 2**bit % 2 == 1
        lower_half = jnp.where(upper, other, piece)
        upper_half = jnp.where(upper, piece, other)
        piece = jnp.concatenate([lower_half, upper_half], axis=0)
    return piece


def per_device(queries, keys, values, cache_keys, cache_values, vertical, vertical_count, slash):
    query_rows, key_rows, value_rows = from_behind((queries, keys, values), "section", 1)
    tok = query_rows.shape[1]
    heads = lax.axis_size("seq")
    kv_heads = key_rows.shape[2] // HEAD_SIZE
    prefill_stretch = tok * heads
    bits = GROUP.bit_length() - 1
    rank = lax.axis_index("seq")
    q_rows = query_rows[0].reshape(tok, heads, HEAD_SIZE)
    kv_rows = jnp.concatenate(
        [
            key_rows[0].reshape(tok, kv_heads, HEAD_SIZE),
            value_rows[0].reshape(tok, kv_heads, HEAD_SIZE),
        ],
        axis=2,
    )
    cache_part = jnp.concatenate([cache_keys[0, 0], cache_values[0, 0]], axis=1)
    spread = jnp.broadcast_to(
        kv_rows[:, :, None, :], (tok, kv_heads, GROUP, 2 * HEAD_SIZE)
    ).reshape(tok, heads, 2 * HEAD_SIZE)
    mine = lax.all_to_all(
        jnp.concatenate([q_rows, spread], axis=2), "seq", split_axis=1, concat_axis=0, tiled=True
    )
    own_query = mine[:, 0, :HEAD_SIZE]
    stretch_kv = mine[:, 0, HEAD_SIZE:]
    cache_kv = assemble(cache_part, bits, rank)
    all_kv = jnp.concatenate([cache_kv, stretch_kv], axis=0)
    verts = vertical[0, 0]
    count = vertical_count[0, 0]
    slashes = slash[0, 0]
    tiles = (count + TILE - 1) // TILE
    start = (
        jnp.full((prefill_stretch,), big_negative, jnp.float32),
        jnp.zeros((prefill_stretch,), jnp.float32),
        jnp.zeros((prefill_stretch, HEAD_SIZE), jnp.float32),
    )
    carry = vertical_run(own_query, verts, count, 0, tiles, all_kv, start)
    top, total, accum = slash_run(own_query, verts, count, slashes, all_kv, carry)
    result = (accum / total[:, None]).astype(jnp.bfloat16)
    back = lax.all_to_all(
        result.reshape(prefill_stretch, 1, HEAD_SIZE),
        "seq",
        split_axis=0,
        concat_axis=1,
        tiled=True,
    )
    return back.reshape(1, tok, heads * HEAD_SIZE)


def solution(mesh):
    return jax.shard_map(
        per_device,
        mesh=mesh,
        in_specs=(
            P("section", "seq", None),
            P("section", "seq", None),
            P("section", "seq", None),
            P("section", "seq", None, None),
            P("section", "seq", None, None),
            P("section", "seq", None),
            P("section", "seq"),
            P("section", "seq", None),
        ),
        out_specs=P("section", "seq", None),
        check_vma=False,
    )
```

profile of v0, /device:TPU:88, one launch (start us, length us, event | category | flops | bytes accessed | tf_op | source)
XLA Modules:
  0.0 735.1 jit_solution(6897072906691366801)
XLA Ops:
  0.0 2.9 collective-permute-start.4
  2.9 12.9 %collective-permute-done.4 = bf16[1,128,512]{2,1,0:T(8,128)(2,1)S(1)} collective-permute-done((bf16[1,128,512]{2,1,0:T(8,128)(2,1)}, bf16[1,128,512]{2,1,0:T(8,128)(2,1)S(1)}, u32[]{:S(2)}, u32[]{:S(2)}) %collective-permute-start.4) | collective-permute-done | bytes 131104 | tf_op jit(solution)/shard_map/ppermute | solution.py:28
  20.5 12.8 %all-to-all-start = ((bf16[128,32,384]{2,0,1:T(8,128)(2,1)}), bf16[128,32,384]{2,0,1:T(8,128)(2,1)S(1)}, u32[]{:S(2)}, u32[]{:S(2)}) async-start(bf16[128,32,384]{2,0,1:T(8,128)(2,1)} %pad_maximum_fusion.2), calls=%async_computation | async-start | bytes 6291456 | tf_op jit(solution)/shard_map/all_to_all | solution.py:173
  36.3 72.7 %collective-permute-done = bf16[512,256]{1,0:T(8,128)(2,1)} collective-permute-done((bf16[512,256]{1,0:T(8,128)(2,1)}, bf16[512,256]{1,0:T(8,128)(2,1)}, u32[]{:S(2)}, u32[]{:S(2)}) %collective-permute-start) | collective-permute-done | bytes 262176 | tf_op jit(solution)/shard_map/ppermute | solution.py:23
  111.6 3.6 collective-permute-start.1
  115.9 22.2 %collective-permute-done.1 = bf16[1024,256]{1,0:T(8,128)(2,1)} collective-permute-done((bf16[1024,256]{1,0:T(8,128)(2,1)}, bf16[1024,256]{1,0:T(8,128)(2,1)}, u32[]{:S(2)}, u32[]{:S(2)}) %collective-permute-start.1) | collective-permute-done | bytes 524320 | tf_op jit(solution)/shard_map/ppermute | solution.py:23
  141.3 5.0 collective-permute-start.2
  147.1 25.4 %collective-permute-done.2 = bf16[2048,256]{1,0:T(8,128)(2,1)} collective-permute-done((bf16[2048,256]{1,0:T(8,128)(2,1)}, bf16[2048,256]{1,0:T(8,128)(2,1)}, u32[]{:S(2)}, u32[]{:S(2)}) %collective-permute-start.2) | collective-permute-done | bytes 1048608 | tf_op jit(solution)/shard_map/ppermute | solution.py:23
  172.5 3.3 broadcast_select_fusion.1
  182.4 25.5 %pad_maximum_fusion = bf16[12288,256]{1,0:T(8,128)(2,1)} fusion(bf16[4096,256]{1,0:T(8,128)(2,1)S(1)} %slice_bitcast_fusion, bf16[2048,256]{1,0:T(8,128)(2,1)S(1)} %copy-done.2, bf16[2048,256]{1,0:T(8,128)(2,1)S(1)} %copy-done.1, bf16[12288]{0:T(1024)(128)(2,1)S(1)} %pad.3.clone), kind=kLoop, calls=%fused_computation.59 | loop fusion | flops 25165824 | bytes 10510336 | tf_op jit(solution)/shard_map/concatenate | solution.py:85
  209.4 74.1 %while.31 = (s32[]{:T(128)}, f32[4096]{0:T(1024)S(1)}, f32[4096]{0:T(1024)S(1)}, f32[4096,128]{1,0:T(8,128)}, s32[]{:T(128)}, /*index=5*/s32[]{:T(128)}, s32[32]...) while((s32[]{:T(128)}, f32[4096]{0:T(1024)S(1)}, ...), condition=%wide.region_4.5_spmd.clone, body=%wide.region_1.4_spmd.clone.sunk | while | flops 547431424 | bytes 18750728 | solution.py:66
  214.9 3.8 convolution_add_fusion.2
  224.2 3.8 convolution_add_fusion.2
  228.6 2.7 gather_fusion
  233.4 3.8 convolution_add_fusion.2
  242.7 3.8 convolution_add_fusion.2
  251.9 3.8 convolution_add_fusion.2
  261.2 3.8 convolution_add_fusion.2
  270.4 3.8 convolution_add_fusion.2
  279.7 3.8 convolution_add_fusion.2
  283.6 353.2 %while.33 = (s32[]{:T(128)}, f32[8,8,64]{2,1,0:T(8,128)S(1)}, f32[8,8,64,128]{3,2,1,0:T(8,128)}, f32[8,8,64]{2,1,0:T(8,128)S(1)}, f32[8,8,64]{2,1,0:T(8,128)S(1)...) while((s32[]{:T(128)}, f32[8,8,64]{2,1,0:T(8,128)S(1)}, ...), condition=%wide.region_8.9_spmd.clone, body=%wide.region_5.8_spmd.clone.sunk | while | flops 206276656 | bytes 15618658 | solution.py:135
  284.9 35.9 %while.34 = (s32[]{:T(128)}, bf16[12288,256]{1,0:T(8,128)(2,1)}, s32[12,2]{0,1:T(2,128)S(1)}, bf16[12,512,256]{2,1,0:T(8,128)(2,1)}, s32[]{:T(128)}) while((s32[]{:T(128)}, bf16[12288,256]{1,0:T(8,128)(2,1)}, s32[12,2]{0,1:T(2,128)S(1)}, bf16[12,512,256]{2,1,0:T(8,128)(2,1)}, s32[]{:T(128)}) %tuple.75), condition=%wide.while_cond, body=%wide.while_body.sunk | while | flops 2 | bytes 525401 | solution.py:96
  329.0 35.9 %while.34 = (s32[]{:T(128)}, bf16[12288,256]{1,0:T(8,128)(2,1)}, s32[12,2]{0,1:T(2,128)S(1)}, bf16[12,512,256]{2,1,0:T(8,128)(2,1)}, s32[]{:T(128)}) while((s32[]{:T(128)}, bf16[12288,256]{1,0:T(8,128)(2,1)}, s32[12,2]{0,1:T(2,128)S(1)}, bf16[12,512,256]{2,1,0:T(8,128)(2,1)}, s32[]{:T(128)}) %tuple.75), condition=%wide.while_cond, body=%wide.while_body.sunk | while | flops 2 | bytes 525401 | solution.py:96
  373.2 35.9 %while.34 = (s32[]{:T(128)}, bf16[12288,256]{1,0:T(8,128)(2,1)}, s32[12,2]{0,1:T(2,128)S(1)}, bf16[12,512,256]{2,1,0:T(8,128)(2,1)}, s32[]{:T(128)}) while((s32[]{:T(128)}, bf16[12288,256]{1,0:T(8,128)(2,1)}, s32[12,2]{0,1:T(2,128)S(1)}, bf16[12,512,256]{2,1,0:T(8,128)(2,1)}, s32[]{:T(128)}) %tuple.75), condition=%wide.while_cond, body=%wide.while_body.sunk | while | flops 2 | bytes 525401 | solution.py:96
  417.4 35.9 %while.34 = (s32[]{:T(128)}, bf16[12288,256]{1,0:T(8,128)(2,1)}, s32[12,2]{0,1:T(2,128)S(1)}, bf16[12,512,256]{2,1,0:T(8,128)(2,1)}, s32[]{:T(128)}) while((s32[]{:T(128)}, bf16[12288,256]{1,0:T(8,128)(2,1)}, s32[12,2]{0,1:T(2,128)S(1)}, bf16[12,512,256]{2,1,0:T(8,128)(2,1)}, s32[]{:T(128)}) %tuple.75), condition=%wide.while_cond, body=%wide.while_body.sunk | while | flops 2 | bytes 525401 | solution.py:96
  461.5 35.9 %while.34 = (s32[]{:T(128)}, bf16[12288,256]{1,0:T(8,128)(2,1)}, s32[12,2]{0,1:T(2,128)S(1)}, bf16[12,512,256]{2,1,0:T(8,128)(2,1)}, s32[]{:T(128)}) while((s32[]{:T(128)}, bf16[12288,256]{1,0:T(8,128)(2,1)}, s32[12,2]{0,1:T(2,128)S(1)}, bf16[12,512,256]{2,1,0:T(8,128)(2,1)}, s32[]{:T(128)}) %tuple.75), condition=%wide.while_cond, body=%wide.while_body.sunk | while | flops 2 | bytes 525401 | solution.py:96
  505.6 35.9 %while.34 = (s32[]{:T(128)}, bf16[12288,256]{1,0:T(8,128)(2,1)}, s32[12,2]{0,1:T(2,128)S(1)}, bf16[12,512,256]{2,1,0:T(8,128)(2,1)}, s32[]{:T(128)}) while((s32[]{:T(128)}, bf16[12288,256]{1,0:T(8,128)(2,1)}, s32[12,2]{0,1:T(2,128)S(1)}, bf16[12,512,256]{2,1,0:T(8,128)(2,1)}, s32[]{:T(128)}) %tuple.75), condition=%wide.while_cond, body=%wide.while_body.sunk | while | flops 2 | bytes 525401 | solution.py:96
  549.8 35.9 %while.34 = (s32[]{:T(128)}, bf16[12288,256]{1,0:T(8,128)(2,1)}, s32[12,2]{0,1:T(2,128)S(1)}, bf16[12,512,256]{2,1,0:T(8,128)(2,1)}, s32[]{:T(128)}) while((s32[]{:T(128)}, bf16[12288,256]{1,0:T(8,128)(2,1)}, s32[12,2]{0,1:T(2,128)S(1)}, bf16[12,512,256]{2,1,0:T(8,128)(2,1)}, s32[]{:T(128)}) %tuple.75), condition=%wide.while_cond, body=%wide.while_body.sunk | while | flops 2 | bytes 525401 | solution.py:96
  593.9 35.9 %while.34 = (s32[]{:T(128)}, bf16[12288,256]{1,0:T(8,128)(2,1)}, s32[12,2]{0,1:T(2,128)S(1)}, bf16[12,512,256]{2,1,0:T(8,128)(2,1)}, s32[]{:T(128)}) while((s32[]{:T(128)}, bf16[12288,256]{1,0:T(8,128)(2,1)}, s32[12,2]{0,1:T(2,128)S(1)}, bf16[12,512,256]{2,1,0:T(8,128)(2,1)}, s32[]{:T(128)}) %tuple.75), condition=%wide.while_cond, body=%wide.while_body.sunk | while | flops 2 | bytes 525401 | solution.py:96
  636.9 12.9 %divide_convert_fusion = bf16[4096,1,128]{2,1,0:T(2,128)(2,1)S(1)} fusion(f32[4096,1,128]{2,1,0:T(1,128)} %bitcast.108, f32[4096]{0:T(1024)S(1)} %div.49), kind=kLoop, calls=%fused_computation.63 | loop fusion | flops 1048576 | bytes 3162112 | tf_op jit(solution)/shard_map/convert_element_type | solution.py:191
  650.3 22.4 %reduce.2 = bf16[4096,128]{1,0:T(8,128)(2,1)S(1)} reduce(bf16[4096,1,128]{2,1,0:T(2,128)(2,1)S(1)} %divide_convert_fusion, bf16[]{:T(256)} %broadcast.190), dimensions={1}, to_apply=%divide_convert_fusion.reduce_sub_computation | reduce | bytes 2097154 | tf_op jit(solution)/shard_map/convert_element_type | solution.py:191
  673.0 58.9 %all_to_all.33 = bf16[32,2,8192]{2,1,0:T(2,128)(2,1)S(1)} all-to-all(bf16[32,2,8192]{2,1,0:T(2,128)(2,1)S(1)} %reshape.228), channel_id=1, replica_groups=mesh['section'=16,'seq'=32] {'seq'}, dimensions={0} | all-to-all | bytes 2097152 | tf_op jit(solution)/shard_map/all_to_all | solution.py:192
  (574 shorter events, 414.1 us)
Async XLA Ops:
  0.0 17.5 %collective-permute-start.3 = (bf16[1,128,4096]{2,1,0:T(8,128)(2,1)}, bf16[1,128,4096]{2,1,0:T(8,128)(2,1)S(1)}, u32[]{:S(2)}, u32[]{:S(2)}) collective-permute-start(bf16[1,128,4096]{2,1,0:T(8,128)(2,1)} %param.12), channel_id=1, source_target_pairs={{0,32},{32,64},{64,96},{96,128},{128,160},{160,192},{192,224},{224... | collective-permute-start | bytes 3145736 | tf_op jit(solution)/shard_map/ppermute | solution.py:28
  0.0 15.8 %collective-permute-start.4 = (bf16[1,128,512]{2,1,0:T(8,128)(2,1)}, bf16[1,128,512]{2,1,0:T(8,128)(2,1)S(1)}, u32[]{:S(2)}, u32[]{:S(2)}) collective-permute-start(bf16[1,128,512]{2,1,0:T(8,128)(2,1)} %param.13), channel_id=1, source_target_pairs={{0,32},{32,64},{64,96},{96,128},{128,160},{160,192},{192,224},{224... | collective-permute-start | bytes 393224 | tf_op jit(solution)/shard_map/ppermute | solution.py:28
  2.9 14.3 %collective-permute-start.5 = (bf16[1,128,512]{2,1,0:T(8,128)(2,1)}, bf16[1,128,512]{2,1,0:T(8,128)(2,1)S(1)}, u32[]{:S(2)}, u32[]{:S(2)}) collective-permute-start(bf16[1,128,512]{2,1,0:T(8,128)(2,1)} %param.14), channel_id=1, source_target_pairs={{0,32},{32,64},{64,96},{96,128},{128,160},{160,192},{192,224},{224... | collective-permute-start | bytes 393224 | tf_op jit(solution)/shard_map/ppermute | solution.py:28
  20.5 12.8 %copy-start.6 = (bf16[1,1,512,128]{3,2,1,0:T(8,128)(2,1)S(1)}, bf16[1,1,512,128]{3,2,1,0:T(8,128)(2,1)}, u32[]{:S(2)}) copy-start(bf16[1,1,512,128]{3,2,1,0:T(8,128)(2,1)} %param.16) | copy-start | bytes 393220
  20.5 12.8 %copy-start.7 = (bf16[1,1,512,128]{3,2,1,0:T(8,128)(2,1)S(1)}, bf16[1,1,512,128]{3,2,1,0:T(8,128)(2,1)}, u32[]{:S(2)}) copy-start(bf16[1,1,512,128]{3,2,1,0:T(8,128)(2,1)} %param.15) | copy-start | bytes 393220
  20.5 155.3 %all-to-all-start = ((bf16[128,32,384]{2,0,1:T(8,128)(2,1)}), bf16[128,32,384]{2,0,1:T(8,128)(2,1)S(1)}, u32[]{:S(2)}, u32[]{:S(2)}) async-start(bf16[128,32,384]{2,0,1:T(8,128)(2,1)} %pad_maximum_fusion.2), calls=%async_computation | async-start | bytes 6291456 | tf_op jit(solution)/shard_map/all_to_all | solution.py:173
  34.1 74.9 %collective-permute-start = (bf16[512,256]{1,0:T(8,128)(2,1)}, bf16[512,256]{1,0:T(8,128)(2,1)}, u32[]{:S(2)}, u32[]{:S(2)}) collective-permute-start(bf16[512,256]{1,0:T(8,128)(2,1)} %pad_maximum_fusion.5), channel_id=1, source_target_pairs={{0,1},{1,0},{2,3},{3,2},{4,5},{5,4},{6,7},{7,6},{8,9},{9,8},{10,11... | collective-permute-start | bytes 786440 | tf_op jit(solution)/shard_map/ppermute | solution.py:23
  36.2 110.2 %copy-start.9 = (s32[1,1,11]{2,1,0:T(1,128)S(1)}, s32[1,1,11]{2,1,0:T(1,128)}, u32[]{:S(2)}) copy-start(s32[1,1,11]{2,1,0:T(1,128)} %param.19) | copy-start | bytes 136
  36.2 110.3 %copy-start.8 = (s32[1,1,32]{2,1,0:T(1,128)S(1)}, s32[1,1,32]{2,1,0:T(1,128)}, u32[]{:S(2)}) copy-start(s32[1,1,32]{2,1,0:T(1,128)} %param.17) | copy-start | bytes 388
  110.0 0.7 copy-start.5
  111.6 26.5 %collective-permute-start.1 = (bf16[1024,256]{1,0:T(8,128)(2,1)}, bf16[1024,256]{1,0:T(8,128)(2,1)}, u32[]{:S(2)}, u32[]{:S(2)}) collective-permute-start(bf16[1024,256]{1,0:T(8,128)(2,1)} %pad_maximum_fusion.4), channel_id=1, source_target_pairs={{0,2},{1,3},{2,0},{3,1},{4,6},{5,7},{6,4},{7,5},{8,10},{9,11},{10,... | collective-permute-start | bytes 1572872 | tf_op jit(solution)/shard_map/ppermute | solution.py:23
  139.4 0.8 copy-start.3
  139.4 1.8 copy-start.4
  141.3 31.2 %collective-permute-start.2 = (bf16[2048,256]{1,0:T(8,128)(2,1)}, bf16[2048,256]{1,0:T(8,128)(2,1)}, u32[]{:S(2)}, u32[]{:S(2)}) collective-permute-start(bf16[2048,256]{1,0:T(8,128)(2,1)} %pad_maximum_fusion.3), channel_id=1, source_target_pairs={{0,4},{1,5},{2,6},{3,7},{4,0},{5,1},{6,2},{7,3},{8,12},{9,13},{10,... | collective-permute-start | bytes 3145736 | tf_op jit(solution)/shard_map/ppermute | solution.py:23
  175.8 1.6 copy-start
  177.5 2.7 copy-start.1
  177.5 2.7 copy-start.2
where the time goes:
time: 741 us; the launch traced here: 735 us
  local copies, waits for them, and re-layouts  348 us (47%)
  waiting for transfers between devices  135 us (18%)
  other arithmetic  92.2 us (12%)
  matrix products  67.7 us (9%)
  blocking collectives  58.9 us (8%)
  starting transfers between devices  26.5 us (4%)
    gather x288, local copies, waits for them, and re-layouts  287 us
    ppermute x3, waiting for transfers between devices, from_partner(): return lax.ppermute(value, axis, pairs)  120 us
    all_to_all x1, blocking collectives, per_device(): lax.all_to_all(result.reshape(prefill_stretch, 1, HEAD_SIZE), 'seq', spli...  58.9 us
    convert_element_type x2, other arithmetic, per_device(): result = (accum / total[:, None]).astype(jnp.bfloat16)  35.3 us
    dot_general x8, matrix products, contract(): jnp.dot(attention_weight, value_tile, preferred_element_type=jnp.float32)  30.1 us
    concatenate x1, other arithmetic, slash_run(): jnp.concatenate([jnp.zeros((prefill_stretch, 2 * HEAD_SIZE), all_kv.dtype...  25.5 us
    gather x8, local copies, waits for them, and re-layouts, step(): kv_tile = jnp.take(block_view, picked, axis=0).reshape(span, 2 * HEAD_SIZE)  21.9 us
    dot_general x8, matrix products, contract(): jnp.einsum('owu,out->owt', attention_weight, local_value_share, preferred...  18.5 us
  transfers between devices with their start and end apart: 7, of which 5 were waited for; matrix products, arithmetic and copies ran while one was open for 1% of the time, Pallas kernels for 0%

commit v1 on v0

v1 whole, which is shorter than its diff:
```python
import math

import jax
import jax.numpy as jnp
from jax import lax
from jax.experimental import pallas as pl
from jax.experimental.pallas import tpu as pltpu
from jax.sharding import Mesh
from jax.sharding import PartitionSpec as P

HEAD_SIZE = 128
GROUP = 8
BLK = 64
NVMAX = 32
NS = 11
CACHE = 4096
TQ = 256

big_negative = -1e30


def from_behind(x, axis, by):
    peers = lax.axis_size(axis)
    return lax.ppermute(x, axis, [(i, (i + by) % peers) for i in range(peers)])


def attention_kernel(verts_ref, count_ref, sblk_ref, q_ref, k_ref, v_ref, smask_ref, o_ref,
                     kvert, vvert, kslash, vslash):
    nb = TQ // BLK
    nd = NS + 1
    width = nd * BLK
    nvc = NVMAX * BLK
    tile = pl.program_id(0)
    softmax_scale = 1.0 / math.sqrt(HEAD_SIZE)
    ncb = CACHE // BLK

    @pl.when(tile == 0)
    def _():
        def fill(s, carry):
            blk = jnp.clip(verts_ref[s], 0, ncb - 1)
            src = pl.multiple_of(blk * BLK, BLK)
            dst = pl.multiple_of(s * BLK, BLK)
            kvert[pl.ds(dst, BLK), :] = k_ref[pl.ds(src, BLK), :]
            vvert[pl.ds(dst, BLK), :] = v_ref[pl.ds(src, BLK), :]
            return carry

        lax.fori_loop(0, NVMAX, fill, 0)

    for b in range(nb):
        qb = tile * nb + b
        for d in range(nd):
            blk = sblk_ref[qb * nd + d]
            src = pl.multiple_of(blk * BLK, BLK)
            kslash[b, pl.ds(d * BLK, BLK), :] = k_ref[pl.ds(src, BLK), :]
            vslash[b, pl.ds(d * BLK, BLK), :] = v_ref[pl.ds(src, BLK), :]

    q = q_ref[...]
    count = count_ref[0]
    s_v = lax.dot_general(q, kvert[...], (((1,), (1,)), ((), ())),
                          preferred_element_type=jnp.float32) * softmax_scale
    vcol = lax.broadcasted_iota(jnp.int32, (1, nvc), 1)
    vlive = vcol < count * BLK
    s_v = jnp.where(vlive, s_v, big_negative)
    q3 = q.reshape(nb, BLK, HEAD_SIZE)
    s_s = lax.dot_general(q3, kslash[...], (((2,), (2,)), ((0,), (0,))),
                          preferred_element_type=jnp.float32) * softmax_scale
    col = lax.broadcasted_iota(jnp.int32, (nb, BLK, width), 2)
    row = lax.broadcasted_iota(jnp.int32, (nb, BLK, width), 1)
    causal = (col >= BLK) | (col <= row)
    smask = (smask_ref[...] > 0) & causal
    s_s = jnp.where(smask, s_s, big_negative)
    top_v = jnp.max(s_v, axis=1, keepdims=True).reshape(nb, BLK, 1)
    top_s = jnp.max(s_s, axis=2, keepdims=True)
    top = jnp.maximum(top_v, top_s)
    p_v = jnp.where(vlive, jnp.exp(s_v - top.reshape(TQ, 1)), 0.0)
    p_s = jnp.where(smask, jnp.exp(s_s - top), 0.0)
    total = jnp.sum(p_v, axis=1, keepdims=True).reshape(nb, BLK, 1) + jnp.sum(
        p_s, axis=2, keepdims=True)
    acc_v = jnp.dot(p_v.astype(jnp.bfloat16), vvert[...], preferred_element_type=jnp.float32)
    acc_s = lax.dot_general(p_s.astype(jnp.bfloat16), vslash[...], (((2,), (1,)), ((0,), (0,))),
                            preferred_element_type=jnp.float32)
    acc = acc_v.reshape(nb, BLK, HEAD_SIZE) + acc_s
    o_ref[...] = (acc / total).reshape(TQ, HEAD_SIZE).astype(o_ref.dtype)


def head_attention(own_query, all_k, all_v, verts, count, slashes):
    prefill_stretch = own_query.shape[0]
    ncb = CACHE // BLK
    nqb = prefill_stretch // BLK
    nd = NS + 1
    offsets = jnp.concatenate([jnp.zeros((1,), jnp.int32), slashes])
    blocks = ncb + jnp.arange(nqb, dtype=jnp.int32)[:, None] - offsets[None, :]
    used = jnp.arange(NVMAX, dtype=jnp.int32)[None, None, :] < count
    listed = jnp.any((blocks[:, :, None] == verts[None, None, :]) & used, axis=2)
    valid = (blocks >= 0) & jnp.logical_not(listed)
    sblk = jnp.clip(blocks, 0, all_k.shape[0] // BLK - 1).reshape(-1)
    smask = jnp.repeat(valid.astype(jnp.int32), BLK, axis=1).reshape(nqb, 1, nd * BLK)
    nb = TQ // BLK
    grid_spec = pltpu.PrefetchScalarGridSpec(
        num_scalar_prefetch=3,
        grid=(prefill_stretch // TQ,),
        in_specs=[
            pl.BlockSpec((TQ, HEAD_SIZE), lambda i, *_: (i, 0)),
            pl.BlockSpec(all_k.shape, lambda i, *_: (0, 0)),
            pl.BlockSpec(all_v.shape, lambda i, *_: (0, 0)),
            pl.BlockSpec((nb, 1, nd * BLK), lambda i, *_: (i, 0, 0)),
        ],
        out_specs=pl.BlockSpec((TQ, HEAD_SIZE), lambda i, *_: (i, 0)),
        scratch_shapes=[
            pltpu.VMEM((NVMAX * BLK, HEAD_SIZE), jnp.bfloat16),
            pltpu.VMEM((NVMAX * BLK, HEAD_SIZE), jnp.bfloat16),
            pltpu.VMEM((nb, nd * BLK, HEAD_SIZE), jnp.bfloat16),
            pltpu.VMEM((nb, nd * BLK, HEAD_SIZE), jnp.bfloat16),
        ],
    )
    return pl.pallas_call(
        attention_kernel,
        grid_spec=grid_spec,
        out_shape=jax.ShapeDtypeStruct((prefill_stretch, HEAD_SIZE), jnp.bfloat16),
        compiler_params=pltpu.CompilerParams(dimension_semantics=("arbitrary",)),
    )(verts, count.reshape(1), sblk, own_query, all_k, all_v, smask)


def per_device(queries, keys, values, cache_keys, cache_values, vertical, vertical_count, slash):
    query_rows, key_rows, value_rows = from_behind((queries, keys, values), "section", 1)
    tok = query_rows.shape[1]
    nx = lax.axis_size("gx")
    nz = lax.axis_size("gz")
    heads = nx * nz
    kv_heads = key_rows.shape[2] // HEAD_SIZE
    prefill_stretch = tok * heads
    q_rows = query_rows[0].reshape(tok, heads, HEAD_SIZE)
    own_query = lax.all_to_all(
        q_rows, ("gx", "gz"), split_axis=1, concat_axis=0, tiled=True
    ).reshape(prefill_stretch, HEAD_SIZE)

    def stretch_part(rows):
        part = lax.all_to_all(
            rows[0].reshape(tok, kv_heads, HEAD_SIZE), "gx", split_axis=1, concat_axis=0,
            tiled=True,
        )
        gathered = lax.all_gather(part.reshape(nx, tok, HEAD_SIZE), "gz", axis=0, tiled=False)
        return gathered.transpose(1, 0, 2, 3).reshape(prefill_stretch, HEAD_SIZE)

    stretch_k = stretch_part(key_rows)
    stretch_v = stretch_part(value_rows)
    cache_k = lax.all_gather(cache_keys[0, 0], "gz", axis=0, tiled=True)
    cache_v = lax.all_gather(cache_values[0, 0], "gz", axis=0, tiled=True)
    all_k = jnp.concatenate([cache_k, stretch_k], axis=0)
    all_v = jnp.concatenate([cache_v, stretch_v], axis=0)
    result = head_attention(own_query, all_k, all_v, vertical[0, 0], vertical_count[0, 0],
                            slash[0, 0])
    back = lax.all_to_all(
        result.reshape(prefill_stretch, 1, HEAD_SIZE),
        ("gx", "gz"),
        split_axis=0,
        concat_axis=1,
        tiled=True,
    )
    return back.reshape(1, tok, heads * HEAD_SIZE)


def solution(mesh):
    nsec, nseq = mesh.devices.shape
    kv_groups = nseq // GROUP
    grid_mesh = Mesh(mesh.devices.reshape(nsec, kv_groups, GROUP), ("section", "gx", "gz"))
    seq = ("gx", "gz")
    return jax.shard_map(
        per_device,
        mesh=grid_mesh,
        in_specs=(
            P("section", seq, None),
            P("section", seq, None),
            P("section", seq, None),
            P("section", seq, None, None),
            P("section", seq, None, None),
            P("section", seq, None),
            P("section", seq),
            P("section", seq, None),
        ),
        out_specs=P("section", seq, None),
        check_vma=False,
    )
```

time: 741 us -> 279 us (0.38)
  the two profiles are of different devices: /device:TPU:88 before, /device:TPU:16 now
where the time goes in v1:
time: 279 us; the launch traced here: 278 us
  waiting for transfers between devices  147 us (53%)
  blocking collectives  49 us (18%)
  Pallas kernels  33.1 us (12%)
  local copies, waits for them, and re-layouts  14.7 us (5%)
  between operations  13.9 us (5%)
  starting transfers between devices  11.5 us (4%)
  other arithmetic  8.4 us (3%)
    all_gather x2, waiting for transfers between devices, stretch_part(): lax.all_gather(part.reshape(nx, tok, HEAD_SIZE), 'gz', axis=0, tiled=False)  43.6 us
    all_gather x1, waiting for transfers between devices, per_device(): cache_k = lax.all_gather(cache_keys[0, 0], 'gz', axis=0, tiled=True)  41.3 us
    all_gather x1, waiting for transfers between devices, per_device(): cache_v = lax.all_gather(cache_values[0, 0], 'gz', axis=0, tiled=True)  39.5 us
    pallas_call x1, Pallas kernels, head_attention(): pl.pallas_call(attention_kernel, grid_spec=grid_spec, out_shape=jax.Shape...  33.1 us
    all_to_all x1, blocking collectives, per_device(): lax.all_to_all(result.reshape(prefill_stretch, 1, HEAD_SIZE), ('gx', 'gz'...  30.6 us
    ppermute x3, waiting for transfers between devices, from_behind(): return lax.ppermute(x, axis, [(i, (i + by) % peers) for i in range(peers)])  21.7 us
    all_to_all x2, blocking collectives, stretch_part(): lax.all_to_all(rows[0].reshape(tok, kv_heads, HEAD_SIZE), 'gx', split_axi...  18.4 us
    all_to_all x1, starting transfers between devices, per_device(): lax.all_to_all(q_rows, ('gx', 'gz'), split_axis=1, concat_axis=0, tiled=T...  11.3 us
  transfers between devices with their start and end apart: 8, of which 7 were waited for; matrix products, arithmetic and copies ran while one was open for 5% of the time, Pallas kernels for 0%

profile of v1, /device:TPU:16, one launch (start us, length us, event | category | flops | bytes accessed | tf_op | source)
XLA Modules:
  0.0 278.0 jit_solution(5418954941477423645)
XLA Ops:
  6.5 1.0 copy.57
  7.6 4.4 %collective-permute-done.1 = bf16[1,128,512]{1,2,0:T(8,128)(2,1)S(1)} collective-permute-done((bf16[1,128,512]{1,2,0:T(8,128)(2,1)S(1)}, bf16[1,128,512]{1,2,0:T(8,128)(2,1)S(1)}, u32[]{:S(2)}, u32[]{:S(2)}) %collective-permute-start.1) | collective-permute-done | bytes 131104 | tf_op jit(solution)/shard_map/ppermute | solution.py:24
  12.0 10.1 %all_to_all.60 = bf16[128,4,128]{0,2,1:T(8,128)(2,1)S(1)} all-to-all(bf16[128,4,128]{0,2,1:T(8,128)(2,1)S(1)} %bitcast.51), channel_id=1, replica_groups=mesh['section'=16,'gx'=4,'gz'=8] {'gx'}, dimensions={1} | all-to-all | bytes 262144 | tf_op jit(solution)/shard_map/all_to_all | solution.py:138
  22.1 0.8 copy.58
  22.9 1.0 copy.60
  23.9 4.4 %collective-permute-done.2 = bf16[1,128,512]{1,2,0:T(8,128)(2,1)S(1)} collective-permute-done((bf16[1,128,512]{1,2,0:T(8,128)(2,1)S(1)}, bf16[1,128,512]{1,2,0:T(8,128)(2,1)S(1)}, u32[]{:S(2)}, u32[]{:S(2)}) %collective-permute-start.2) | collective-permute-done | bytes 131104 | tf_op jit(solution)/shard_map/ppermute | solution.py:24
  28.3 8.3 %all_to_all.61 = bf16[128,4,128]{0,2,1:T(8,128)(2,1)S(1)} all-to-all(bf16[128,4,128]{0,2,1:T(8,128)(2,1)S(1)} %bitcast.52), channel_id=1, replica_groups=mesh['section'=16,'gx'=4,'gz'=8] {'gx'}, dimensions={1} | all-to-all | bytes 262144 | tf_op jit(solution)/shard_map/all_to_all | solution.py:138
  36.7 0.8 copy.61
  37.5 0.7 all-gather.9.cloned.1.call-update
  38.3 0.5 all-gather.13.cloned.1.call-update
  39.7 13.0 %collective-permute-done = bf16[1,128,4096]{2,1,0:T(8,128)(2,1)S(1)} collective-permute-done((bf16[1,128,4096]{2,1,0:T(8,128)(2,1)}, bf16[1,128,4096]{2,1,0:T(8,128)(2,1)S(1)}, u32[]{:S(2)}, u32[]{:S(2)}) %collective-permute-start) | collective-permute-done | bytes 1048608 | tf_op jit(solution)/shard_map/ppermute | solution.py:24
  53.0 1.4 copy.56
  54.3 11.3 %all-to-all-start = ((bf16[128,32,128]{2,0,1:T(8,128)(2,1)}), bf16[128,32,128]{2,0,1:T(8,128)(2,1)S(1)}, u32[]{:S(2)}, u32[]{:S(2)}) async-start(bf16[128,32,128]{2,0,1:T(8,128)(2,1)} %copy.56), calls=%async_computation | async-start | bytes 2097152 | tf_op jit(solution)/shard_map/all_to_all | solution.py:133
  66.0 1.0 reshape_reshape.4.smask_ref
  67.1 0.7 min.12.sblk_ref
  67.8 1.5 all-gather.11.cloned.1.call-done
  69.3 1.3 copy.59
  70.6 42.1 %all-gather.15.cloned.1.call-done = bf16[32,128,1,128]{3,1,2,0:T(8,128)(2,1)} async-done(((bf16[4,128,1,128]{3,1,2,0:T(8,128)(2,1)}), bf16[32,128,1,128]{3,1,2,0:T(8,128)(2,1)}) %all-gather.15.cloned.1.call-update) | async-done | bytes 1048592 | tf_op jit(solution)/shard_map/all_gather | solution.py:142
  112.7 1.3 copy.62
  114.0 41.3 %all-gather.9.cloned.1.call-done = bf16[1,1,4096,128]{3,2,1,0:T(8,128)(2,1)} async-done(((bf16[1,1,512,128]{3,2,1,0:T(8,128)(2,1)}), bf16[1,1,4096,128]{3,2,1,0:T(8,128)(2,1)}) %all-gather.9.cloned.1.call-update) | async-done | bytes 1048592 | tf_op jit(solution)/shard_map/all_gather | solution.py:147
  155.2 2.7 pad_maximum_fusion.k_ref
  157.9 39.5 %all-gather.13.cloned.1.call-done = bf16[1,1,4096,128]{3,2,1,0:T(8,128)(2,1)} async-done(((bf16[1,1,512,128]{3,2,1,0:T(8,128)(2,1)}), bf16[1,1,4096,128]{3,2,1,0:T(8,128)(2,1)}) %all-gather.13.cloned.1.call-update) | async-done | bytes 1048592 | tf_op jit(solution)/shard_map/all_gather | solution.py:148
  197.5 2.7 pad_maximum_fusion.1.v_ref
  200.2 1.0 copy-done
  201.1 33.1 %shard_map.82 = bf16[4096,128]{1,0:T(8,128)(2,1)} custom-call(s32[32]{0:T(128)} %bitcast.53, s32[1]{0:T(128)} %bitcast.35.count_ref, s32[768]{0:T(1024)} %min.12.sblk_ref, bf16[4096,128]{1,0:T(8,128)(2,1)} %bitcast.41, bf16[8192,128]{1,0:T(8,128)(2,1)} %pad_maximum_fusion.k_ref, bf16[8192,128]{1,0:T(8,128)(2,1)} %pad_maximum_fusion.1.v_ref, ...), custom_call_target="tpu_custom_call" | custom-call | tf_op jit(solution)/shard_map/pallas_call | solution.py:116
  234.3 0.5 broadcast.37
  234.8 2.7 reduce
  237.4 0.3 reshape.70
  237.7 30.6 %all_to_all.62 = bf16[32,2,8192]{2,1,0:T(2,128)(2,1)S(1)} all-to-all(bf16[32,2,8192]{2,1,0:T(2,128)(2,1)S(1)} %reshape.70), channel_id=1, replica_groups=mesh['section'=16,'gx'=4,'gz'=8] {'gx','gz'}, dimensions={0} | all-to-all | bytes 2097152 | tf_op jit(solution)/shard_map/all_to_all | solution.py:153
  268.3 1.0 reshape.71
  269.5 0.7 copy.66
  270.2 1.3 copy.67
  (26 shorter events, 1.3 us)
Async XLA Ops:
  6.5 32.9 %copy-start.2 = (s32[1,1,11]{2,1,0:T(1,128)S(1)}, s32[1,1,11]{2,1,0:T(1,128)}, u32[]{:S(2)}) copy-start(s32[1,1,11]{2,1,0:T(1,128)} %param.15) | copy-start | bytes 136
  6.5 33.1 %copy-start.1 = (s32[1,1,32]{2,1,0:T(1,128)S(1)}, s32[1,1,32]{2,1,0:T(1,128)}, u32[]{:S(2)}) copy-start(s32[1,1,32]{2,1,0:T(1,128)} %param.13) | copy-start | bytes 388
  6.5 62.7 %all-gather.11.cloned.1.call-start = ((), (), s32[]{:S(2)}) async-start(), calls=%async_computation.5 | async-start | bytes 1179648 | tf_op jit(solution)/shard_map/all_gather | solution.py:142
  7.6 4.4 %collective-permute-start.1 = (bf16[1,128,512]{1,2,0:T(8,128)(2,1)S(1)}, bf16[1,128,512]{1,2,0:T(8,128)(2,1)S(1)}, u32[]{:S(2)}, u32[]{:S(2)}) collective-permute-start(bf16[1,128,512]{1,2,0:T(8,128)(2,1)S(1)} %copy.57), channel_id=1, source_target_pairs={{0,32},{32,64},{64,96},{96,128},{128,160},{160,192},{192,224},{224... | collective-permute-start | bytes 393224 | tf_op jit(solution)/shard_map/ppermute | solution.py:24
  22.8 89.8 %all-gather.15.cloned.1.call-start = ((), (), s32[]{:S(2)}) async-start(), calls=%async_computation.7 | async-start | bytes 1179648 | tf_op jit(solution)/shard_map/all_gather | solution.py:142
  23.9 4.4 %collective-permute-start.2 = (bf16[1,128,512]{1,2,0:T(8,128)(2,1)S(1)}, bf16[1,128,512]{1,2,0:T(8,128)(2,1)S(1)}, u32[]{:S(2)}, u32[]{:S(2)}) collective-permute-start(bf16[1,128,512]{1,2,0:T(8,128)(2,1)S(1)} %copy.60), channel_id=1, source_target_pairs={{0,32},{32,64},{64,96},{96,128},{128,160},{160,192},{192,224},{224... | collective-permute-start | bytes 393224 | tf_op jit(solution)/shard_map/ppermute | solution.py:24
  37.5 117.8 %all-gather.9.cloned.1.call-start = ((), (), s32[]{:S(2)}) async-start(), calls=%async_computation.4 | async-start | bytes 1179648 | tf_op jit(solution)/shard_map/all_gather | solution.py:147
  38.2 159.3 %all-gather.13.cloned.1.call-start = ((), (), s32[]{:S(2)}) async-start(), calls=%async_computation.6 | async-start | bytes 1179648 | tf_op jit(solution)/shard_map/all_gather | solution.py:148
  38.3 14.4 %collective-permute-start = (bf16[1,128,4096]{2,1,0:T(8,128)(2,1)}, bf16[1,128,4096]{2,1,0:T(8,128)(2,1)S(1)}, u32[]{:S(2)}, u32[]{:S(2)}) collective-permute-start(bf16[1,128,4096]{2,1,0:T(8,128)(2,1)} %param.8), channel_id=1, source_target_pairs={{0,32},{32,64},{64,96},{96,128},{128,160},{160,192},{192,224},{224... | collective-permute-start | bytes 3145736 | tf_op jit(solution)/shard_map/ppermute | solution.py:24
  54.3 145.8 %all-to-all-start = ((bf16[128,32,128]{2,0,1:T(8,128)(2,1)}), bf16[128,32,128]{2,0,1:T(8,128)(2,1)S(1)}, u32[]{:S(2)}, u32[]{:S(2)}) async-start(bf16[128,32,128]{2,0,1:T(8,128)(2,1)} %copy.56), calls=%async_computation | async-start | bytes 2097152 | tf_op jit(solution)/shard_map/all_to_all | solution.py:133
  200.2 1.0 copy-start
Sparse Core Ops, SparseCore 0:
  23.0 46.2 all-gather.10
  71.4 41.2 all-gather.14
  114.7 40.4 all-gather.8
  157.2 40.2 all-gather.12

commit v2 on v1

v2 whole, which is shorter than its diff:
```python
import functools
import math

import jax
import jax.numpy as jnp
from jax import lax
from jax.experimental import pallas as pl
from jax.experimental.pallas import tpu as pltpu
from jax.sharding import Mesh
from jax.sharding import PartitionSpec as P

HEAD_SIZE = 128
GROUP = 8
BLK = 64
NVMAX = 32
NS = 11
CACHE = 4096
TQ = 256

big_negative = -1e30


def from_behind(x, axis, by):
    peers = lax.axis_size(axis)
    return lax.ppermute(x, axis, [(i, (i + by) % peers) for i in range(peers)])


def attention_kernel(verts_ref, count_ref, sblk_ref, q_ref, ckv_ref, skv_ref, smask_ref, o_ref,
                     kvert, kslash, *, tok, nz):
    nb = TQ // BLK
    nd = NS + 1
    width = nd * BLK
    nvc = NVMAX * BLK
    tile = pl.program_id(0)
    softmax_scale = 1.0 / math.sqrt(HEAD_SIZE)
    ncb = CACHE // BLK
    per_dev = tok // BLK

    @pl.when(tile == 0)
    def _():
        def fill(s, carry):
            blk = jnp.clip(verts_ref[s], 0, ncb - 1)
            src = pl.multiple_of(blk * BLK, BLK)
            dst = pl.multiple_of(s * BLK, BLK)
            kvert[pl.ds(dst, BLK), :] = ckv_ref[pl.ds(src, BLK), :]
            return carry

        lax.fori_loop(0, NVMAX, fill, 0)

    for b in range(nb):
        qb = tile * nb + b
        for d in range(nd):
            blk = sblk_ref[qb * nd + d]

            @pl.when(blk < ncb)
            def _():
                src = pl.multiple_of(blk * BLK, BLK)
                kslash[b, pl.ds(d * BLK, BLK), :] = ckv_ref[pl.ds(src, BLK), :]

            @pl.when(blk >= ncb)
            def _():
                s = blk - ncb
                dev = s // per_dev
                row = pl.multiple_of((dev // nz) * tok + (s % per_dev) * BLK, BLK)
                kslash[b, pl.ds(d * BLK, BLK), :] = skv_ref[dev % nz, pl.ds(row, BLK), :]

    q = q_ref[...]
    count = count_ref[0]
    s_v = lax.dot_general(q, kvert[:, :HEAD_SIZE], (((1,), (1,)), ((), ())),
                          preferred_element_type=jnp.float32) * softmax_scale
    vcol = lax.broadcasted_iota(jnp.int32, (1, nvc), 1)
    vlive = vcol < count * BLK
    s_v = jnp.where(vlive, s_v, big_negative)
    q3 = q.reshape(nb, BLK, HEAD_SIZE)
    s_s = lax.dot_general(q3, kslash[:, :, :HEAD_SIZE], (((2,), (2,)), ((0,), (0,))),
                          preferred_element_type=jnp.float32) * softmax_scale
    col = lax.broadcasted_iota(jnp.int32, (nb, BLK, width), 2)
    row = lax.broadcasted_iota(jnp.int32, (nb, BLK, width), 1)
    causal = (col >= BLK) | (col <= row)
    smask = (smask_ref[...] > 0) & causal
    s_s = jnp.where(smask, s_s, big_negative)
    top_v = jnp.max(s_v, axis=1, keepdims=True).reshape(nb, BLK, 1)
    top_s = jnp.max(s_s, axis=2, keepdims=True)
    top = jnp.maximum(top_v, top_s)
    p_v = jnp.where(vlive, jnp.exp(s_v - top.reshape(TQ, 1)), 0.0)
    p_s = jnp.where(smask, jnp.exp(s_s - top), 0.0)
    total = jnp.sum(p_v, axis=1, keepdims=True).reshape(nb, BLK, 1) + jnp.sum(
        p_s, axis=2, keepdims=True)
    acc_v = jnp.dot(p_v.astype(jnp.bfloat16), kvert[:, HEAD_SIZE:],
                    preferred_element_type=jnp.float32)
    acc_s = lax.dot_general(p_s.astype(jnp.bfloat16), kslash[:, :, HEAD_SIZE:],
                            (((2,), (1,)), ((0,), (0,))), preferred_element_type=jnp.float32)
    acc = acc_v.reshape(nb, BLK, HEAD_SIZE) + acc_s
    o_ref[...] = (acc / total).reshape(TQ, HEAD_SIZE).astype(o_ref.dtype)


def head_attention(own_query, ckv, skv, verts, count, slashes, tok):
    prefill_stretch = own_query.shape[0]
    nz = skv.shape[0]
    ncb = CACHE // BLK
    nqb = prefill_stretch // BLK
    nd = NS + 1
    offsets = jnp.concatenate([jnp.zeros((1,), jnp.int32), slashes])
    blocks = ncb + jnp.arange(nqb, dtype=jnp.int32)[:, None] - offsets[None, :]
    used = jnp.arange(NVMAX, dtype=jnp.int32)[None, None, :] < count
    listed = jnp.any((blocks[:, :, None] == verts[None, None, :]) & used, axis=2)
    valid = (blocks >= 0) & jnp.logical_not(listed)
    sblk = jnp.clip(blocks, 0, ncb + nqb - 1).reshape(-1)
    smask = jnp.repeat(valid.astype(jnp.int32), BLK, axis=1).reshape(nqb, 1, nd * BLK)
    nb = TQ // BLK
    grid_spec = pltpu.PrefetchScalarGridSpec(
        num_scalar_prefetch=3,
        grid=(prefill_stretch // TQ,),
        in_specs=[
            pl.BlockSpec((TQ, HEAD_SIZE), lambda i, *_: (i, 0)),
            pl.BlockSpec(ckv.shape, lambda i, *_: (0, 0)),
            pl.BlockSpec(skv.shape, lambda i, *_: (0, 0, 0)),
            pl.BlockSpec((nb, 1, nd * BLK), lambda i, *_: (i, 0, 0)),
        ],
        out_specs=pl.BlockSpec((TQ, HEAD_SIZE), lambda i, *_: (i, 0)),
        scratch_shapes=[
            pltpu.VMEM((NVMAX * BLK, 2 * HEAD_SIZE), jnp.bfloat16),
            pltpu.VMEM((nb, nd * BLK, 2 * HEAD_SIZE), jnp.bfloat16),
        ],
    )
    return pl.pallas_call(
        functools.partial(attention_kernel, tok=tok, nz=nz),
        grid_spec=grid_spec,
        out_shape=jax.ShapeDtypeStruct((prefill_stretch, HEAD_SIZE), jnp.bfloat16),
        compiler_params=pltpu.CompilerParams(dimension_semantics=("arbitrary",)),
    )(verts, count.reshape(1), sblk, own_query, ckv, skv, smask)


def per_device(queries, keys, values, cache_keys, cache_values, vertical, vertical_count, slash):
    query_rows, key_rows, value_rows = from_behind((queries, keys, values), "section", 1)
    tok = query_rows.shape[1]
    nx = lax.axis_size("gx")
    nz = lax.axis_size("gz")
    heads = nx * nz
    kv_heads = key_rows.shape[2] // HEAD_SIZE
    prefill_stretch = tok * heads
    q_rows = query_rows[0].reshape(tok, heads, HEAD_SIZE)
    own_query = lax.all_to_all(
        q_rows, ("gx", "gz"), split_axis=1, concat_axis=0, tiled=True
    ).reshape(prefill_stretch, HEAD_SIZE)

    kv_rows = jnp.concatenate(
        [
            key_rows[0].reshape(tok, kv_heads, HEAD_SIZE),
            value_rows[0].reshape(tok, kv_heads, HEAD_SIZE),
        ],
        axis=2,
    )
    part = lax.all_to_all(kv_rows, "gx", split_axis=1, concat_axis=0, tiled=True)
    skv = lax.all_gather(part.reshape(nx * tok, 2 * HEAD_SIZE), "gz", axis=0, tiled=False)
    cache_part = jnp.concatenate([cache_keys[0, 0], cache_values[0, 0]], axis=1)
    ckv = lax.all_gather(cache_part, "gz", axis=0, tiled=True)
    result = head_attention(own_query, ckv, skv, vertical[0, 0], vertical_count[0, 0],
                            slash[0, 0], tok)
    back = lax.all_to_all(
        result.reshape(prefill_stretch, 1, HEAD_SIZE),
        ("gx", "gz"),
        split_axis=0,
        concat_axis=1,
        tiled=True,
    )
    return back.reshape(1, tok, heads * HEAD_SIZE)


def solution(mesh):
    nsec, nseq = mesh.devices.shape
    kv_groups = nseq // GROUP
    grid_mesh = Mesh(mesh.devices.reshape(nsec, kv_groups, GROUP), ("section", "gx", "gz"))
    seq = ("gx", "gz")
    return jax.shard_map(
        per_device,
        mesh=grid_mesh,
        in_specs=(
            P("section", seq, None),
            P("section", seq, None),
            P("section", seq, None),
            P("section", seq, None, None),
            P("section", seq, None, None),
            P("section", seq, None),
            P("section", seq),
            P("section", seq, None),
        ),
        out_specs=P("section", seq, None),
        check_vma=False,
    )
```

time: 279 us -> 202 us (0.72)
  waiting for transfers between devices: 147 us -> 69.9 us
  Pallas kernels: 33.1 us -> 46 us
  local copies, waits for them, and re-layouts: 14.7 us -> 7.72 us
  other arithmetic: 8.4 us -> 4.85 us
    all_gather x4 -> x2, waiting for transfers between devices: 124 us -> 24.1 us  [the longest x1 24.1 us: per_device(): lax.all_gather(part.reshape(nx * tok, 2 * HEAD_SIZE), 'gz', axis=0, tiled...]
    all_to_all x1, waiting for transfers between devices: 0.01 us -> 27.3 us  [per_device(): lax.all_to_all(q_rows, ('gx', 'gz'), split_axis=1, concat_axis=0, tiled=T...]
    pallas_call x1, Pallas kernels: 33.1 us -> 46 us  [head_attention(): pl.pallas_call(functools.partial(attention_kernel, tok=tok, nz=nz), grid_...]
    all_to_all x2 -> x1, blocking collectives: 18.4 us -> 10.9 us  [per_device(): lax.all_to_all(kv_rows, 'gx', split_axis=1, concat_axis=0, tiled=True)]
    all_to_all x1, blocking collectives: 30.6 us -> 35.5 us  [per_device(): lax.all_to_all(result.reshape(prefill_stretch, 1, HEAD_SIZE), ('gx', 'gz'...]
    concatenate x2, other arithmetic: 5.37 us -> 1.82 us  [the longest x1 1.78 us: per_device(): cache_part = jnp.concatenate([cache_keys[0, 0], cache_values[0, 0]], axis=1)]
    ppermute x3, waiting for transfers between devices: 21.7 us -> 18.5 us  [from_behind(): return lax.ppermute(x, axis, [(i, (i + by) % peers) for i in range(peers)])]
    unnamed x12, local copies, waits for them, and re-layouts: 4.74 us -> 1.71 us
  transfers between devices with their start and end apart: 8 -> 6, of which waited for: 7 -> 5; matrix products, arithmetic and copies ran while one was open for 5% -> 2% of each run, Pallas kernels for 0% -> 0%
where the time goes in v2:
time: 202 us
  waiting for transfers between devices  69.9 us (35%)
  blocking collectives  46.4 us (23%)
  Pallas kernels  46 us (23%)
  between operations  14.2 us (7%)
  starting transfers between devices  13.1 us (6%)
  local copies, waits for them, and re-layouts  7.72 us (4%)
  other arithmetic  4.85 us (2%)
    pallas_call x1, Pallas kernels, head_attention(): pl.pallas_call(functools.partial(attention_kernel, tok=tok, nz=nz), grid_...  46 us
    all_to_all x1, blocking collectives, per_device(): lax.all_to_all(result.reshape(prefill_stretch, 1, HEAD_SIZE), ('gx', 'gz'...  35.5 us
    all_to_all x1, waiting for transfers between devices, per_device(): lax.all_to_all(q_rows, ('gx', 'gz'), split_axis=1, concat_axis=0, tiled=T...  27.3 us
    all_gather x1, waiting for transfers between devices, per_device(): lax.all_gather(part.reshape(nx * tok, 2 * HEAD_SIZE), 'gz', axis=0, tiled...  24.1 us
    ppermute x3, waiting for transfers between devices, from_behind(): return lax.ppermute(x, axis, [(i, (i + by) % peers) for i in range(peers)])  18.5 us
    all_to_all x1, starting transfers between devices, per_device(): lax.all_to_all(q_rows, ('gx', 'gz'), split_axis=1, concat_axis=0, tiled=T...  11.3 us
    all_to_all x1, blocking collectives, per_device(): lax.all_to_all(kv_rows, 'gx', split_axis=1, concat_axis=0, tiled=True)  10.9 us
  transfers between devices with their start and end apart: 6, of which 5 were waited for; matrix products, arithmetic and copies ran while one was open for 2% of the time, Pallas kernels for 0%

profile of v2, /device:TPU:16, one launch (start us, length us, event | category | flops | bytes accessed | tf_op | source)
XLA Modules:
  0.0 202.0 jit_solution(13277981278213961613)
XLA Ops:
  6.5 1.8 pad_maximum_fusion
  8.3 0.0 all-gather.5.cloned.1.call-start
  8.4 0.0 collective-permute-start.1
  8.4 1.7 collective-permute-start.2
  10.1 2.9 %collective-permute-done.1 = bf16[1,128,512]{2,1,0:T(8,128)(2,1)S(1)} collective-permute-done((bf16[1,128,512]{2,1,0:T(8,128)(2,1)}, bf16[1,128,512]{2,1,0:T(8,128)(2,1)S(1)}, u32[]{:S(2)}, u32[]{:S(2)}) %collective-permute-start.1) | collective-permute-done | bytes 131104 | tf_op jit(solution)/shard_map/ppermute | solution.py:25
  13.1 1.3 collective-permute-done.2
  14.5 10.9 %all_to_all.45 = bf16[128,4,256]{2,0,1:T(8,128)(2,1)} all-to-all(bf16[128,4,256]{2,0,1:T(8,128)(2,1)S(1)} %pad_maximum_fusion.1), channel_id=1, replica_groups=mesh['section'=16,'gx'=4,'gz'=8] {'gx'}, dimensions={1} | all-to-all | bytes 524288 | tf_op jit(solution)/shard_map/all_to_all | solution.py:154
  25.4 0.0 collective-permute-start
  25.5 14.2 %collective-permute-done = bf16[1,128,4096]{2,1,0:T(8,128)(2,1)S(1)} collective-permute-done((bf16[1,128,4096]{2,1,0:T(8,128)(2,1)S(1)}, bf16[1,128,4096]{2,1,0:T(8,128)(2,1)S(1)}, u32[]{:S(2)}, u32[]{:S(2)}) %collective-permute-start) | collective-permute-done | bytes 1048608 | tf_op jit(solution)/shard_map/ppermute | solution.py:25
  39.7 0.2 copy.46
  39.9 1.4 copy.37
  41.3 11.3 %all-to-all-start = ((bf16[128,32,128]{2,0,1:T(8,128)(2,1)}), bf16[128,32,128]{2,0,1:T(8,128)(2,1)S(1)}, u32[]{:S(2)}, u32[]{:S(2)}) async-start(bf16[128,32,128]{2,0,1:T(8,128)(2,1)} %copy.37), calls=%async_computation | async-start | bytes 2097152 | tf_op jit(solution)/shard_map/all_to_all | solution.py:143
  53.3 0.1 pad_add_fusion
  53.4 0.1 broadcast_subtract_fusion
  53.5 0.1 and_reduce_fusion
  53.6 0.1 and_convert_fusion
  53.7 0.1 copy.40
  53.8 0.2 broadcast_in_dim.2
  54.0 1.0 reshape_reshape.4.smask_ref
  54.9 0.1 copy.36
  55.0 0.7 min.12.sblk_ref
  55.7 27.3 %all-to-all-done = bf16[128,32,128]{2,0,1:T(8,128)(2,1)S(1)} async-done(((bf16[128,32,128]{2,0,1:T(8,128)(2,1)}), bf16[128,32,128]{2,0,1:T(8,128)(2,1)S(1)}, u32[]{:S(2)}, u32[]{:S(2)}) %all-to-all-start) | async-done | bytes 1048608 | tf_op jit(solution)/shard_map/all_to_all | solution.py:143
  83.0 24.1 %all-gather.5.cloned.1.call-done.skv_ref = bf16[8,512,256]{2,1,0:T(8,128)(2,1)} async-done(((bf16[1,512,256]{2,1,0:T(8,128)(2,1)}), bf16[8,512,256]{2,1,0:T(8,128)(2,1)}) %all-gather.5.cloned.1.call-update) | async-done | bytes 2097168 | tf_op jit(solution)/shard_map/all_gather | solution.py:155
  107.1 46.0 %shard_map.82 = bf16[4096,128]{1,0:T(8,128)(2,1)} custom-call(s32[32]{0:T(128)} %bitcast.35, s32[1]{0:T(128)} %bitcast.24.count_ref, s32[768]{0:T(1024)} %min.12.sblk_ref, bf16[4096,128]{1,0:T(8,128)(2,1)} %bitcast.30, bf16[4096,256]{1,0:T(8,128)(2,1)} %all-gather.3.cloned.1.call-done.ckv_ref, bf16[8,512,256]{2,1,0:T(8,128)(2,1)} %all-gather.5.cloned.1.call-done.skv_ref, ...), custom_call_target="tpu_custom_call" | custom-call | tf_op jit(solution)/shard_map/pallas_call | solution.py:126
  153.1 0.5 broadcast.37
  153.6 2.7 %reduce = bf16[4096,128]{1,0:T(8,128)(2,1)S(1)} reduce(bf16[4096,1,128]{2,0,1:T(8,128)(2,1)} %bitcast.29, bf16[]{:T(256)} %broadcast.37), dimensions={1}, to_apply=%copy.42.reduce_sub_computation | reduce | bytes 2097154 | tf_op jit(solution)/shard_map/reshape | solution.py:161
  156.3 0.3 reshape.57
  156.5 35.5 %all_to_all.46 = bf16[32,2,8192]{2,1,0:T(2,128)(2,1)S(1)} all-to-all(bf16[32,2,8192]{2,1,0:T(2,128)(2,1)S(1)} %reshape.57), channel_id=1, replica_groups=mesh['section'=16,'gx'=4,'gz'=8] {'gx','gz'}, dimensions={0} | all-to-all | bytes 2097152 | tf_op jit(solution)/shard_map/all_to_all | solution.py:160
  192.0 1.0 reshape.58
  193.1 0.1 copy.45
  193.2 0.7 copy.43
  193.9 1.3 copy.44
  (19 shorter events, 0.2 us)
Async XLA Ops:
  6.5 18.9 %copy-start.2 = (bf16[1,128,4096]{2,1,0:T(8,128)(2,1)S(1)}, bf16[1,128,4096]{2,1,0:T(8,128)(2,1)}, u32[]{:S(2)}) copy-start(bf16[1,128,4096]{2,1,0:T(8,128)(2,1)} %param.8) | copy-start | bytes 3145732
  6.5 76.5 %all-gather.3.cloned.1.call-start = ((), (), s32[]{:S(2)}) async-start(), calls=%async_computation.3 | async-start | bytes 2359296 | tf_op jit(solution)/shard_map/all_gather | solution.py:157
  8.3 98.7 %all-gather.5.cloned.1.call-start = ((), (), s32[]{:S(2)}) async-start(), calls=%async_computation.4 | async-start | bytes 2359296 | tf_op jit(solution)/shard_map/all_gather | solution.py:155
  8.4 4.6 %collective-permute-start.1 = (bf16[1,128,512]{2,1,0:T(8,128)(2,1)}, bf16[1,128,512]{2,1,0:T(8,128)(2,1)S(1)}, u32[]{:S(2)}, u32[]{:S(2)}) collective-permute-start(bf16[1,128,512]{2,1,0:T(8,128)(2,1)} %param.9), channel_id=1, source_target_pairs={{0,32},{32,64},{64,96},{96,128},{128,160},{160,192},{192,224},{224... | collective-permute-start | bytes 393224 | tf_op jit(solution)/shard_map/ppermute | solution.py:25
  8.4 6.0 %collective-permute-start.2 = (bf16[1,128,512]{2,1,0:T(8,128)(2,1)}, bf16[1,128,512]{2,1,0:T(8,128)(2,1)S(1)}, u32[]{:S(2)}, u32[]{:S(2)}) collective-permute-start(bf16[1,128,512]{2,1,0:T(8,128)(2,1)} %param.10), channel_id=1, source_target_pairs={{0,32},{32,64},{64,96},{96,128},{128,160},{160,192},{192,224},{224... | collective-permute-start | bytes 393224 | tf_op jit(solution)/shard_map/ppermute | solution.py:25
  25.4 14.2 %collective-permute-start = (bf16[1,128,4096]{2,1,0:T(8,128)(2,1)S(1)}, bf16[1,128,4096]{2,1,0:T(8,128)(2,1)S(1)}, u32[]{:S(2)}, u32[]{:S(2)}) collective-permute-start(bf16[1,128,4096]{2,1,0:T(8,128)(2,1)S(1)} %copy-done.2), channel_id=1, source_target_pairs={{0,32},{32,64},{64,96},{96,128},{128,160},{160,192},{192,224},{224... | collective-permute-start | bytes 3145736 | tf_op jit(solution)/shard_map/ppermute | solution.py:25
  39.9 13.4 %copy-start.3 = (s32[1,1,11]{2,1,0:T(1,128)S(1)}, s32[1,1,11]{2,1,0:T(1,128)}, u32[]{:S(2)}) copy-start(s32[1,1,11]{2,1,0:T(1,128)} %param.15) | copy-start | bytes 136
  39.9 13.5 %copy-start.1 = (s32[1,1,32]{2,1,0:T(1,128)S(1)}, s32[1,1,32]{2,1,0:T(1,128)}, u32[]{:S(2)}) copy-start(s32[1,1,32]{2,1,0:T(1,128)} %param.13) | copy-start | bytes 388
  41.3 41.7 %all-to-all-start = ((bf16[128,32,128]{2,0,1:T(8,128)(2,1)}), bf16[128,32,128]{2,0,1:T(8,128)(2,1)S(1)}, u32[]{:S(2)}, u32[]{:S(2)}) async-start(bf16[128,32,128]{2,0,1:T(8,128)(2,1)} %copy.37), calls=%async_computation | async-start | bytes 2097152 | tf_op jit(solution)/shard_map/all_to_all | solution.py:143
  83.0 24.1 %copy-start = (bf16[128,32,128]{2,0,1:T(8,128)(2,1)}, bf16[128,32,128]{2,0,1:T(8,128)(2,1)S(1)}, u32[]{:S(2)}) copy-start(bf16[128,32,128]{2,0,1:T(8,128)(2,1)S(1)} %all-to-all-done) | copy-start | bytes 3145732
Sparse Core Ops, SparseCore 0:
  9.4 52.8 all-gather.2
  64.4 42.6 all-gather.4

commit v3 on v2

--- a/solution.py
+++ b/solution.py
@@ -25,7 +25,24 @@
     return lax.ppermute(x, axis, [(i, (i + by) % peers) for i in range(peers)])
 
 
-def attention_kernel(verts_ref, count_ref, sblk_ref, q_ref, ckv_ref, skv_ref, smask_ref, o_ref,
+def ring_gather(piece, axis):
+    peers = lax.axis_size(axis)
+    ahead = [(i, (i + 1) % peers) for i in range(peers)]
+    behind = [(i, (i - 1) % peers) for i in range(peers)]
+    planes = [None] * peers
+    planes[0] = piece
+    up = piece
+    down = piece
+    for step in range(1, peers // 2 + 1):
+        up = lax.ppermute(up, axis, ahead)
+        planes[peers - step] = up
+        if step < peers - step:
+            down = lax.ppermute(down, axis, behind)
+            planes[step] = down
+    return jnp.stack(planes)
+
+
+def attention_kernel(verts_ref, count_ref, sblk_ref, rank_ref, q_ref, ckv_ref, skv_ref, smask_ref, o_ref,
                      kvert, kslash, *, tok, nz):
     nb = TQ // BLK
     nd = NS + 1
@@ -35,14 +52,18 @@
     softmax_scale = 1.0 / math.sqrt(HEAD_SIZE)
     ncb = CACHE // BLK
     per_dev = tok // BLK
+    rank = rank_ref[0]
+    cache_rows = ckv_ref.shape[1]
+    cache_per = cache_rows // BLK
 
     @pl.when(tile == 0)
     def _():
         def fill(s, carry):
             blk = jnp.clip(verts_ref[s], 0, ncb - 1)
-            src = pl.multiple_of(blk * BLK, BLK)
+            src = pl.multiple_of((blk % cache_per) * BLK, BLK)
+            plane = (blk // cache_per - rank + nz) % nz
             dst = pl.multiple_of(s * BLK, BLK)
-            kvert[pl.ds(dst, BLK), :] = ckv_ref[pl.ds(src, BLK), :]
+            kvert[pl.ds(dst, BLK), :] = ckv_ref[plane, pl.ds(src, BLK), :]
             return carry
 
         lax.fori_loop(0, NVMAX, fill, 0)
@@ -54,15 +75,17 @@
 
             @pl.when(blk < ncb)
             def _():
-                src = pl.multiple_of(blk * BLK, BLK)
-                kslash[b, pl.ds(d * BLK, BLK), :] = ckv_ref[pl.ds(src, BLK), :]
+                src = pl.multiple_of((blk % cache_per) * BLK, BLK)
+                plane = (blk // cache_per - rank + nz) % nz
+                kslash[b, pl.ds(d * BLK, BLK), :] = ckv_ref[plane, pl.ds(src, BLK), :]
 
             @pl.when(blk >= ncb)
             def _():
                 s = blk - ncb
                 dev = s // per_dev
                 row = pl.multiple_of((dev // nz) * tok + (s % per_dev) * BLK, BLK)
-                kslash[b, pl.ds(d * BLK, BLK), :] = skv_ref[dev % nz, pl.ds(row, BLK), :]
+                plane = (dev % nz - rank + nz) % nz
+                kslash[b, pl.ds(d * BLK, BLK), :] = skv_ref[plane, pl.ds(row, BLK), :]
 
     q = q_ref[...]
     count = count_ref[0]
@@ -94,7 +117,7 @@
     o_ref[...] = (acc / total).reshape(TQ, HEAD_SIZE).astype(o_ref.dtype)
 
 
-def head_attention(own_query, ckv, skv, verts, count, slashes, tok):
+def head_attention(own_query, ckv, skv, verts, count, slashes, tok, rank):
     prefill_stretch = own_query.shape[0]
     nz = skv.shape[0]
     ncb = CACHE // BLK
@@ -109,11 +132,11 @@
     smask = jnp.repeat(valid.astype(jnp.int32), BLK, axis=1).reshape(nqb, 1, nd * BLK)
     nb = TQ // BLK
     grid_spec = pltpu.PrefetchScalarGridSpec(
-        num_scalar_prefetch=3,
+        num_scalar_prefetch=4,
         grid=(prefill_stretch // TQ,),
         in_specs=[
             pl.BlockSpec((TQ, HEAD_SIZE), lambda i, *_: (i, 0)),
-            pl.BlockSpec(ckv.shape, lambda i, *_: (0, 0)),
+            pl.BlockSpec(ckv.shape, lambda i, *_: (0, 0, 0)),
             pl.BlockSpec(skv.shape, lambda i, *_: (0, 0, 0)),
             pl.BlockSpec((nb, 1, nd * BLK), lambda i, *_: (i, 0, 0)),
         ],
@@ -128,7 +151,7 @@
         grid_spec=grid_spec,
         out_shape=jax.ShapeDtypeStruct((prefill_stretch, HEAD_SIZE), jnp.bfloat16),
         compiler_params=pltpu.CompilerParams(dimension_semantics=("arbitrary",)),
-    )(verts, count.reshape(1), sblk, own_query, ckv, skv, smask)
+    )(verts, count.reshape(1), sblk, rank.reshape(1), own_query, ckv, skv, smask)
 
 
 def per_device(queries, keys, values, cache_keys, cache_values, vertical, vertical_count, slash):
@@ -152,11 +175,12 @@
         axis=2,
     )
     part = lax.all_to_all(kv_rows, "gx", split_axis=1, concat_axis=0, tiled=True)
-    skv = lax.all_gather(part.reshape(nx * tok, 2 * HEAD_SIZE), "gz", axis=0, tiled=False)
     cache_part = jnp.concatenate([cache_keys[0, 0], cache_values[0, 0]], axis=1)
-    ckv = lax.all_gather(cache_part, "gz", axis=0, tiled=True)
+    ckv = ring_gather(cache_part, "gz")
+    skv = ring_gather(part.reshape(nx * tok, 2 * HEAD_SIZE), "gz")
+    rank = lax.axis_index("gz").astype(jnp.int32)
     result = head_attention(own_query, ckv, skv, vertical[0, 0], vertical_count[0, 0],
-                            slash[0, 0], tok)
+                            slash[0, 0], tok, rank)
     back = lax.all_to_all(
         result.reshape(prefill_stretch, 1, HEAD_SIZE),
         ("gx", "gz"),

time: 202 us -> 215 us (1.064)
  starting transfers between devices: 13.1 us -> 68.1 us
  waiting for transfers between devices: 69.9 us -> 23.7 us
  local copies, waits for them, and re-layouts: 7.72 us -> 22.5 us
  between operations: 14.2 us -> 1.07 us
  blocking collectives: 46.4 us -> 35.6 us
  Pallas kernels: 46 us -> 55.4 us
  other arithmetic: 4.85 us -> 7.76 us
    ppermute x0 -> x14, starting transfers between devices: none -> 54.3 us  [the longest x6 37.2 us: ring_gather(): down = lax.ppermute(down, axis, behind)]
    all_to_all x1, waiting for transfers between devices: 27.3 us -> 0.01 us  [per_device(): lax.all_to_all(q_rows, ('gx', 'gz'), split_axis=1, concat_axis=0, tiled=T...]
    all_gather x2 -> x0, waiting for transfers between devices: 24.1 us -> none  [the longest x1 24.1 us: per_device(): lax.all_gather(part.reshape(nx * tok, 2 * HEAD_SIZE), 'gz', axis=0, tiled...]
    ppermute x0 -> x14, waiting for transfers between devices: none -> 23.7 us  [the longest x8 23.4 us: ring_gather(): up = lax.ppermute(up, axis, ahead)]
    ppermute x3, waiting for transfers between devices: 18.5 us -> 0.01 us  [from_behind(): return lax.ppermute(x, axis, [(i, (i + by) % peers) for i in range(peers)])]
    unnamed x12 -> x27, local copies, waits for them, and re-layouts: 1.71 us -> 14.8 us
    all_to_all x1 -> x0, blocking collectives: 10.9 us -> none  [per_device(): lax.all_to_all(kv_rows, 'gx', split_axis=1, concat_axis=0, tiled=True)]
    pallas_call x1, Pallas kernels: 46 us -> 55.4 us  [head_attention(): pl.pallas_call(functools.partial(attention_kernel, tok=tok, nz=nz), grid_...]
  transfers between devices with their start and end apart: 6 -> 19, of which waited for: 5 -> 3; matrix products, arithmetic and copies ran while one was open for 2% -> 9% of each run, Pallas kernels for 0% -> 0%
where the time goes in v3:
time: 215 us; the launch traced here: 214 us
  starting transfers between devices  68.1 us (32%)
  Pallas kernels  55.4 us (26%)
  blocking collectives  35.6 us (17%)
  waiting for transfers between devices  23.7 us (11%)
  local copies, waits for them, and re-layouts  22.5 us (10%)
  other arithmetic  7.76 us (4%)
    pallas_call x1, Pallas kernels, head_attention(): pl.pallas_call(functools.partial(attention_kernel, tok=tok, nz=nz), grid_...  55.4 us
    ppermute x6, starting transfers between devices, ring_gather(): down = lax.ppermute(down, axis, behind)  37.2 us
    all_to_all x1, blocking collectives, per_device(): lax.all_to_all(result.reshape(prefill_stretch, 1, HEAD_SIZE), ('gx', 'gz'...  35.6 us
    ppermute x8, waiting for transfers between devices, ring_gather(): up = lax.ppermute(up, axis, ahead)  23.4 us
    ppermute x8, starting transfers between devices, ring_gather(): up = lax.ppermute(up, axis, ahead)  17.1 us
    unnamed x27, local copies, waits for them, and re-layouts  14.8 us
    all_to_all x1, starting transfers between devices, per_device(): lax.all_to_all(q_rows, ('gx', 'gz'), split_axis=1, concat_axis=0, tiled=T...  7.77 us
  transfers between devices with their start and end apart: 19, of which 3 were waited for; matrix products, arithmetic and copies ran while one was open for 9% of the time, Pallas kernels for 0%

profile of v3, /device:TPU:16, one launch (start us, length us, event | category | flops | bytes accessed | tf_op | source)
XLA Modules:
  0.0 214.2 jit_solution(15591125644342024150)
XLA Ops:
  0.0 1.7 pad_maximum_fusion
  1.7 10.9 %collective-permute-start.1 = (bf16[512,256]{1,0:T(8,128)(2,1)}, bf16[512,256]{1,0:T(8,128)(2,1)}, u32[]{:S(2)}, u32[]{:S(2)}) collective-permute-start(bf16[512,256]{1,0:T(8,128)(2,1)} %pad_maximum_fusion), channel_id=1, source_target_pairs={{0,7},{1,0},{2,1},{3,2},{4,3},{5,4},{6,5},{7,6},{8,15},{9,8},{10,9... | collective-permute-start | bytes 786440 | tf_op jit(solution)/shard_map/ppermute | solution.py:40
  12.6 1.9 collective-permute-start.4
  14.6 1.7 collective-permute-start.9
  20.7 1.0 bitcast_dynamic-update-slice_fusion.14
  22.6 4.3 %all-to-all-start.1 = ((bf16[128,4,256]{2,0,1:T(8,128)(2,1)}), bf16[128,4,256]{2,0,1:T(8,128)(2,1)S(1)}, u32[]{:S(2)}, u32[]{:S(2)}) async-start(bf16[128,4,256]{2,0,1:T(8,128)(2,1)} %pad_maximum_fusion.1), calls=%async_computation.1 | async-start | bytes 524288 | tf_op jit(solution)/shard_map/all_to_all | solution.py:177
  26.9 5.1 %collective-permute-start.2 = (bf16[512,256]{1,0:T(8,128)(2,1)}, bf16[512,256]{1,0:T(8,128)(2,1)}, u32[]{:S(2)}, u32[]{:S(2)}) collective-permute-start(bf16[512,256]{1,0:T(8,128)(2,1)} %collective-permute-done.1), channel_id=1, source_target_pairs={{0,7},{1,0},{2,1},{3,2},{4,3},{5,4},{6,5},{7,6},{8,15},{9,8},{10,9... | collective-permute-start | bytes 786440 | tf_op jit(solution)/shard_map/ppermute | solution.py:40
  32.0 1.9 collective-permute-start.5
  33.9 1.0 bitcast_dynamic-update-slice_fusion.13
  34.9 5.1 %collective-permute-start.10 = (bf16[512,256]{1,0:T(8,128)(2,1)S(1)}, bf16[512,256]{1,0:T(8,128)(2,1)S(1)}, u32[]{:S(2)}, u32[]{:S(2)}) collective-permute-start(bf16[512,256]{1,0:T(8,128)(2,1)S(1)} %bitcast.65), channel_id=1, source_target_pairs={{0,7},{1,0},{2,1},{3,2},{4,3},{5,4},{6,5},{7,6},{8,15},{9,8},{10,9... | collective-permute-start | bytes 786440 | tf_op jit(solution)/shard_map/ppermute | solution.py:40
  40.1 1.9 collective-permute-start.13
  42.0 5.1 %collective-permute-start.3 = (bf16[512,256]{1,0:T(8,128)(2,1)}, bf16[512,256]{1,0:T(8,128)(2,1)S(1)}, u32[]{:S(2)}, u32[]{:S(2)}) collective-permute-start(bf16[512,256]{1,0:T(8,128)(2,1)} %collective-permute-done.2), channel_id=1, source_target_pairs={{0,7},{1,0},{2,1},{3,2},{4,3},{5,4},{6,5},{7,6},{8,15},{9,8},{10,9... | collective-permute-start | bytes 786440 | tf_op jit(solution)/shard_map/ppermute | solution.py:40
  47.2 1.9 collective-permute-start.6
  50.1 5.1 %collective-permute-start.11 = (bf16[512,256]{1,0:T(8,128)(2,1)S(1)}, bf16[512,256]{1,0:T(8,128)(2,1)}, u32[]{:S(2)}, u32[]{:S(2)}) collective-permute-start(bf16[512,256]{1,0:T(8,128)(2,1)S(1)} %collective-permute-done.10), channel_id=1, source_target_pairs={{0,7},{1,0},{2,1},{3,2},{4,3},{5,4},{6,5},{7,6},{8,15},{9,8},{10,9... | collective-permute-start | bytes 786440 | tf_op jit(solution)/shard_map/ppermute | solution.py:40
  55.3 1.9 collective-permute-start.14
  57.2 2.4 %collective-permute-done.6 = bf16[512,256]{1,0:T(8,128)(2,1)} collective-permute-done((bf16[512,256]{1,0:T(8,128)(2,1)}, bf16[512,256]{1,0:T(8,128)(2,1)}, u32[]{:S(2)}, u32[]{:S(2)}) %collective-permute-start.6) | collective-permute-done | bytes 262176 | tf_op jit(solution)/shard_map/ppermute | solution.py:37
  59.6 1.9 collective-permute-start.7
  61.8 5.7 %collective-permute-start.12 = (bf16[512,256]{1,0:T(8,128)(2,1)}, bf16[512,256]{1,0:T(8,128)(2,1)}, u32[]{:S(2)}, u32[]{:S(2)}) collective-permute-start(bf16[512,256]{1,0:T(8,128)(2,1)} %collective-permute-done.11), channel_id=1, source_target_pairs={{0,7},{1,0},{2,1},{3,2},{4,3},{5,4},{6,5},{7,6},{8,15},{9,8},{10,9... | collective-permute-start | bytes 786440 | tf_op jit(solution)/shard_map/ppermute | solution.py:40
  67.6 1.9 collective-permute-start.15
  70.5 1.3 copy-done.2
  72.0 1.4 copy.37
  73.4 7.8 %all-to-all-start = ((bf16[128,32,128]{2,0,1:T(8,128)(2,1)}), bf16[128,32,128]{2,0,1:T(8,128)(2,1)S(1)}, u32[]{:S(2)}, u32[]{:S(2)}) async-start(bf16[128,32,128]{2,0,1:T(8,128)(2,1)} %copy.37), calls=%async_computation | async-start | bytes 2097152 | tf_op jit(solution)/shard_map/all_to_all | solution.py:166
  81.2 1.0 bitcast_dynamic-update-slice_fusion.10
  84.2 3.7 %collective-permute-start.16 = (bf16[512,256]{1,0:T(8,128)(2,1)}, bf16[512,256]{1,0:T(8,128)(2,1)S(1)}, u32[]{:S(2)}, u32[]{:S(2)}) collective-permute-start(bf16[512,256]{1,0:T(8,128)(2,1)} %collective-permute-done.15), channel_id=1, source_target_pairs={{0,1},{1,2},{2,3},{3,4},{4,5},{5,6},{6,7},{7,0},{8,9},{9,10},{10,1... | collective-permute-start | bytes 786440 | tf_op jit(solution)/shard_map/ppermute | solution.py:37
  88.9 1.9 bitcast_dynamic-update-slice_fusion.4
  90.7 21.0 %collective-permute-done.16 = bf16[512,256]{1,0:T(8,128)(2,1)S(1)} collective-permute-done((bf16[512,256]{1,0:T(8,128)(2,1)}, bf16[512,256]{1,0:T(8,128)(2,1)S(1)}, u32[]{:S(2)}, u32[]{:S(2)}) %collective-permute-start.16) | collective-permute-done | bytes 262176 | tf_op jit(solution)/shard_map/ppermute | solution.py:37
  112.5 1.7 bitcast_dynamic-update-slice_fusion.2
  116.5 55.4 %shard_map.82 = bf16[4096,128]{1,0:T(8,128)(2,1)} custom-call(s32[32]{0:T(128)} %bitcast.73, s32[1]{0:T(128)} %bitcast.57.count_ref, s32[768]{0:T(1024)} %min.12.sblk_ref, s32[1]{0:T(128)} %bitcast.3.rank_ref, bf16[4096,128]{1,0:T(8,128)(2,1)} %bitcast.60, bf16[8,512,256]{2,1,0:T(8,128)(2,1)} %copy-done.1, ...), custom_call_target="tpu_custom_call" | custom-call | tf_op jit(solution)/shard_map/pallas_call | solution.py:149
  172.4 2.7 %reduce = bf16[4096,128]{1,0:T(8,128)(2,1)S(1)} reduce(bf16[4096,1,128]{2,0,1:T(8,128)(2,1)} %bitcast.59, bf16[]{:T(256)} %broadcast.37), dimensions={1}, to_apply=%copy.42.reduce_sub_computation | reduce | bytes 2097154 | tf_op jit(solution)/shard_map/reshape | solution.py:185
  175.3 35.6 %all_to_all.45 = bf16[32,2,8192]{2,1,0:T(2,128)(2,1)S(1)} all-to-all(bf16[32,2,8192]{2,1,0:T(2,128)(2,1)S(1)} %reshape.66), channel_id=1, replica_groups=mesh['section'=16,'gx'=4,'gz'=8] {'gx','gz'}, dimensions={0} | all-to-all | bytes 2097152 | tf_op jit(solution)/shard_map/all_to_all | solution.py:184
  211.0 1.0 reshape.67
  212.8 1.3 copy.44
  (60 shorter events, 14.8 us)
Async XLA Ops:
  1.7 25.2 %collective-permute-start.1 = (bf16[512,256]{1,0:T(8,128)(2,1)}, bf16[512,256]{1,0:T(8,128)(2,1)}, u32[]{:S(2)}, u32[]{:S(2)}) collective-permute-start(bf16[512,256]{1,0:T(8,128)(2,1)} %pad_maximum_fusion), channel_id=1, source_target_pairs={{0,7},{1,0},{2,1},{3,2},{4,3},{5,4},{6,5},{7,6},{8,15},{9,8},{10,9... | collective-permute-start | bytes 786440 | tf_op jit(solution)/shard_map/ppermute | solution.py:40
  12.6 19.4 %collective-permute-start.4 = (bf16[512,256]{1,0:T(8,128)(2,1)}, bf16[512,256]{1,0:T(8,128)(2,1)}, u32[]{:S(2)}, u32[]{:S(2)}) collective-permute-start(bf16[512,256]{1,0:T(8,128)(2,1)} %pad_maximum_fusion), channel_id=1, source_target_pairs={{0,1},{1,2},{2,3},{3,4},{4,5},{5,6},{6,7},{7,0},{8,9},{9,10},{10,1... | collective-permute-start | bytes 786440 | tf_op jit(solution)/shard_map/ppermute | solution.py:37
  14.6 7.1 %collective-permute-start.8 = (bf16[1,128,512]{2,1,0:T(8,128)(2,1)}, bf16[1,128,512]{2,1,0:T(8,128)(2,1)S(1)}, u32[]{:S(2)}, u32[]{:S(2)}) collective-permute-start(bf16[1,128,512]{2,1,0:T(8,128)(2,1)} %param.9), channel_id=1, source_target_pairs={{0,32},{32,64},{64,96},{96,128},{128,160},{160,192},{192,224},{224... | collective-permute-start | bytes 393224 | tf_op jit(solution)/shard_map/ppermute | solution.py:25
  14.6 7.2 %collective-permute-start.9 = (bf16[1,128,512]{2,1,0:T(8,128)(2,1)}, bf16[1,128,512]{2,1,0:T(8,128)(2,1)S(1)}, u32[]{:S(2)}, u32[]{:S(2)}) collective-permute-start(bf16[1,128,512]{2,1,0:T(8,128)(2,1)} %param.10), channel_id=1, source_target_pairs={{0,32},{32,64},{64,96},{96,128},{128,160},{160,192},{192,224},{224... | collective-permute-start | bytes 393224 | tf_op jit(solution)/shard_map/ppermute | solution.py:25
  16.3 54.2 %collective-permute-start = (bf16[1,128,4096]{2,1,0:T(8,128)(2,1)}, bf16[1,128,4096]{2,1,0:T(8,128)(2,1)S(1)}, u32[]{:S(2)}, u32[]{:S(2)}) collective-permute-start(bf16[1,128,4096]{2,1,0:T(8,128)(2,1)} %param.8), channel_id=1, source_target_pairs={{0,32},{32,64},{64,96},{96,128},{128,160},{160,192},{192,224},{224... | collective-permute-start | bytes 3145736 | tf_op jit(solution)/shard_map/ppermute | solution.py:25
  22.6 12.3 %all-to-all-start.1 = ((bf16[128,4,256]{2,0,1:T(8,128)(2,1)}), bf16[128,4,256]{2,0,1:T(8,128)(2,1)S(1)}, u32[]{:S(2)}, u32[]{:S(2)}) async-start(bf16[128,4,256]{2,0,1:T(8,128)(2,1)} %pad_maximum_fusion.1), calls=%async_computation.1 | async-start | bytes 524288 | tf_op jit(solution)/shard_map/all_to_all | solution.py:177
  26.9 15.2 %collective-permute-start.2 = (bf16[512,256]{1,0:T(8,128)(2,1)}, bf16[512,256]{1,0:T(8,128)(2,1)}, u32[]{:S(2)}, u32[]{:S(2)}) collective-permute-start(bf16[512,256]{1,0:T(8,128)(2,1)} %collective-permute-done.1), channel_id=1, source_target_pairs={{0,7},{1,0},{2,1},{3,2},{4,3},{5,4},{6,5},{7,6},{8,15},{9,8},{10,9... | collective-permute-start | bytes 786440 | tf_op jit(solution)/shard_map/ppermute | solution.py:40
  32.0 15.2 %collective-permute-start.5 = (bf16[512,256]{1,0:T(8,128)(2,1)}, bf16[512,256]{1,0:T(8,128)(2,1)}, u32[]{:S(2)}, u32[]{:S(2)}) collective-permute-start(bf16[512,256]{1,0:T(8,128)(2,1)} %collective-permute-done.4), channel_id=1, source_target_pairs={{0,1},{1,2},{2,3},{3,4},{4,5},{5,6},{6,7},{7,0},{8,9},{9,10},{10,1... | collective-permute-start | bytes 786440 | tf_op jit(solution)/shard_map/ppermute | solution.py:37
  34.9 15.2 %collective-permute-start.10 = (bf16[512,256]{1,0:T(8,128)(2,1)S(1)}, bf16[512,256]{1,0:T(8,128)(2,1)S(1)}, u32[]{:S(2)}, u32[]{:S(2)}) collective-permute-start(bf16[512,256]{1,0:T(8,128)(2,1)S(1)} %bitcast.65), channel_id=1, source_target_pairs={{0,7},{1,0},{2,1},{3,2},{4,3},{5,4},{6,5},{7,6},{8,15},{9,8},{10,9... | collective-permute-start | bytes 786440 | tf_op jit(solution)/shard_map/ppermute | solution.py:40
  40.1 15.2 %collective-permute-start.13 = (bf16[512,256]{1,0:T(8,128)(2,1)S(1)}, bf16[512,256]{1,0:T(8,128)(2,1)S(1)}, u32[]{:S(2)}, u32[]{:S(2)}) collective-permute-start(bf16[512,256]{1,0:T(8,128)(2,1)S(1)} %bitcast.66), channel_id=1, source_target_pairs={{0,1},{1,2},{2,3},{3,4},{4,5},{5,6},{6,7},{7,0},{8,9},{9,10},{10,1... | collective-permute-start | bytes 786440 | tf_op jit(solution)/shard_map/ppermute | solution.py:37
  42.0 19.5 %collective-permute-start.3 = (bf16[512,256]{1,0:T(8,128)(2,1)}, bf16[512,256]{1,0:T(8,128)(2,1)S(1)}, u32[]{:S(2)}, u32[]{:S(2)}) collective-permute-start(bf16[512,256]{1,0:T(8,128)(2,1)} %collective-permute-done.2), channel_id=1, source_target_pairs={{0,7},{1,0},{2,1},{3,2},{4,3},{5,4},{6,5},{7,6},{8,15},{9,8},{10,9... | collective-permute-start | bytes 786440 | tf_op jit(solution)/shard_map/ppermute | solution.py:40
  47.2 12.4 %collective-permute-start.6 = (bf16[512,256]{1,0:T(8,128)(2,1)}, bf16[512,256]{1,0:T(8,128)(2,1)}, u32[]{:S(2)}, u32[]{:S(2)}) collective-permute-start(bf16[512,256]{1,0:T(8,128)(2,1)} %collective-permute-done.5), channel_id=1, source_target_pairs={{0,1},{1,2},{2,3},{3,4},{4,5},{5,6},{6,7},{7,0},{8,9},{9,10},{10,1... | collective-permute-start | bytes 786440 | tf_op jit(solution)/shard_map/ppermute | solution.py:37
  50.1 11.7 %collective-permute-start.11 = (bf16[512,256]{1,0:T(8,128)(2,1)S(1)}, bf16[512,256]{1,0:T(8,128)(2,1)}, u32[]{:S(2)}, u32[]{:S(2)}) collective-permute-start(bf16[512,256]{1,0:T(8,128)(2,1)S(1)} %collective-permute-done.10), channel_id=1, source_target_pairs={{0,7},{1,0},{2,1},{3,2},{4,3},{5,4},{6,5},{7,6},{8,15},{9,8},{10,9... | collective-permute-start | bytes 786440 | tf_op jit(solution)/shard_map/ppermute | solution.py:40
  55.2 15.2 %copy-start.3 = (bf16[512,256]{1,0:T(8,128)(2,1)}, bf16[512,256]{1,0:T(8,128)(2,1)S(1)}, u32[]{:S(2)}) copy-start(bf16[512,256]{1,0:T(8,128)(2,1)S(1)} %collective-permute-done.13) | copy-start | bytes 786436
  55.3 12.3 %collective-permute-start.14 = (bf16[512,256]{1,0:T(8,128)(2,1)S(1)}, bf16[512,256]{1,0:T(8,128)(2,1)S(1)}, u32[]{:S(2)}, u32[]{:S(2)}) collective-permute-start(bf16[512,256]{1,0:T(8,128)(2,1)S(1)} %collective-permute-done.13), channel_id=1, source_target_pairs={{0,1},{1,2},{2,3},{3,4},{4,5},{5,6},{6,7},{7,0},{8,9},{9,10},{10,1... | collective-permute-start | bytes 786440 | tf_op jit(solution)/shard_map/ppermute | solution.py:37
  59.6 21.6 %collective-permute-start.7 = (bf16[512,256]{1,0:T(8,128)(2,1)}, bf16[512,256]{1,0:T(8,128)(2,1)}, u32[]{:S(2)}, u32[]{:S(2)}) collective-permute-start(bf16[512,256]{1,0:T(8,128)(2,1)} %collective-permute-done.6), channel_id=1, source_target_pairs={{0,1},{1,2},{2,3},{3,4},{4,5},{5,6},{6,7},{7,0},{8,9},{9,10},{10,1... | collective-permute-start | bytes 786440 | tf_op jit(solution)/shard_map/ppermute | solution.py:37
  61.8 27.0 %collective-permute-start.12 = (bf16[512,256]{1,0:T(8,128)(2,1)}, bf16[512,256]{1,0:T(8,128)(2,1)}, u32[]{:S(2)}, u32[]{:S(2)}) collective-permute-start(bf16[512,256]{1,0:T(8,128)(2,1)} %collective-permute-done.11), channel_id=1, source_target_pairs={{0,7},{1,0},{2,1},{3,2},{4,3},{5,4},{6,5},{7,6},{8,15},{9,8},{10,9... | collective-permute-start | bytes 786440 | tf_op jit(solution)/shard_map/ppermute | solution.py:40
  67.6 16.6 %collective-permute-start.15 = (bf16[512,256]{1,0:T(8,128)(2,1)S(1)}, bf16[512,256]{1,0:T(8,128)(2,1)}, u32[]{:S(2)}, u32[]{:S(2)}) collective-permute-start(bf16[512,256]{1,0:T(8,128)(2,1)S(1)} %collective-permute-done.14), channel_id=1, source_target_pairs={{0,1},{1,2},{2,3},{3,4},{4,5},{5,6},{6,7},{7,0},{8,9},{9,10},{10,1... | collective-permute-start | bytes 786440 | tf_op jit(solution)/shard_map/ppermute | solution.py:37
  70.5 1.3 copy-start.2
  73.4 42.1 %all-to-all-start = ((bf16[128,32,128]{2,0,1:T(8,128)(2,1)}), bf16[128,32,128]{2,0,1:T(8,128)(2,1)S(1)}, u32[]{:S(2)}, u32[]{:S(2)}) async-start(bf16[128,32,128]{2,0,1:T(8,128)(2,1)} %copy.37), calls=%async_computation | async-start | bytes 2097152 | tf_op jit(solution)/shard_map/all_to_all | solution.py:166
  81.2 33.7 %copy-start.4 = (bf16[512,256]{1,0:T(8,128)(2,1)S(1)}, bf16[512,256]{1,0:T(8,128)(2,1)}, u32[]{:S(2)}) copy-start(bf16[512,256]{1,0:T(8,128)(2,1)} %copy-done.3) | copy-start | bytes 786436
  84.2 27.6 %collective-permute-start.16 = (bf16[512,256]{1,0:T(8,128)(2,1)}, bf16[512,256]{1,0:T(8,128)(2,1)S(1)}, u32[]{:S(2)}, u32[]{:S(2)}) collective-permute-start(bf16[512,256]{1,0:T(8,128)(2,1)} %collective-permute-done.15), channel_id=1, source_target_pairs={{0,1},{1,2},{2,3},{3,4},{4,5},{5,6},{6,7},{7,0},{8,9},{9,10},{10,1... | collective-permute-start | bytes 786440 | tf_op jit(solution)/shard_map/ppermute | solution.py:37
  88.8 26.7 %copy-start.1 = (bf16[8,512,256]{2,1,0:T(8,128)(2,1)}, bf16[8,512,256]{2,1,0:T(8,128)(2,1)S(1)}, u32[]{:S(2)}) copy-start(bf16[8,512,256]{2,1,0:T(8,128)(2,1)S(1)} %bitcast_dynamic-update-slice_fusion.7.ckv_ref) | copy-start | bytes 6291460
  115.5 1.0 copy-start

commit v4 on v2

--- a/solution.py
+++ b/solution.py
@@ -25,16 +25,10 @@
     return lax.ppermute(x, axis, [(i, (i + by) % peers) for i in range(peers)])
 
 
-def attention_kernel(verts_ref, count_ref, sblk_ref, q_ref, ckv_ref, skv_ref, smask_ref, o_ref,
-                     kvert, kslash, *, tok, nz):
-    nb = TQ // BLK
-    nd = NS + 1
-    width = nd * BLK
-    nvc = NVMAX * BLK
+def vertical_kernel(verts_ref, q_ref, ckv_ref, vbias_ref, acc_ref, top_ref, total_ref, kvert):
     tile = pl.program_id(0)
     softmax_scale = 1.0 / math.sqrt(HEAD_SIZE)
     ncb = CACHE // BLK
-    per_dev = tok // BLK
 
     @pl.when(tile == 0)
     def _():
@@ -47,6 +41,26 @@
 
         lax.fori_loop(0, NVMAX, fill, 0)
 
+    scores = lax.dot_general(q_ref[...], kvert[:, :HEAD_SIZE], (((1,), (1,)), ((), ())),
+                             preferred_element_type=jnp.float32) * softmax_scale + vbias_ref[...]
+    top = jnp.max(scores, axis=1, keepdims=True)
+    weights = jnp.exp(scores - top)
+    total_ref[...] = jnp.sum(weights, axis=1, keepdims=True)
+    top_ref[...] = top
+    acc_ref[...] = jnp.dot(weights.astype(jnp.bfloat16), kvert[:, HEAD_SIZE:],
+                           preferred_element_type=jnp.float32)
+
+
+def slash_kernel(sblk_ref, q_ref, ckv_ref, skv_ref, smask_ref, acc_ref, top_ref, total_ref,
+                 o_ref, kslash, *, tok, nz):
+    nb = TQ // BLK
+    nd = NS + 1
+    width = nd * BLK
+    tile = pl.program_id(0)
+    softmax_scale = 1.0 / math.sqrt(HEAD_SIZE)
+    ncb = CACHE // BLK
+    per_dev = tok // BLK
+
     for b in range(nb):
         qb = tile * nb + b
         for d in range(nd):
@@ -64,14 +78,7 @@
                 row = pl.multiple_of((dev // nz) * tok + (s % per_dev) * BLK, BLK)
                 kslash[b, pl.ds(d * BLK, BLK), :] = skv_ref[dev % nz, pl.ds(row, BLK), :]
 
-    q = q_ref[...]
-    count = count_ref[0]
-    s_v = lax.dot_general(q, kvert[:, :HEAD_SIZE], (((1,), (1,)), ((), ())),
-                          preferred_element_type=jnp.float32) * softmax_scale
-    vcol = lax.broadcasted_iota(jnp.int32, (1, nvc), 1)
-    vlive = vcol < count * BLK
-    s_v = jnp.where(vlive, s_v, big_negative)
-    q3 = q.reshape(nb, BLK, HEAD_SIZE)
+    q3 = q_ref[...].reshape(nb, BLK, HEAD_SIZE)
     s_s = lax.dot_general(q3, kslash[:, :, :HEAD_SIZE], (((2,), (2,)), ((0,), (0,))),
                           preferred_element_type=jnp.float32) * softmax_scale
     col = lax.broadcasted_iota(jnp.int32, (nb, BLK, width), 2)
@@ -79,19 +86,47 @@
     causal = (col >= BLK) | (col <= row)
     smask = (smask_ref[...] > 0) & causal
     s_s = jnp.where(smask, s_s, big_negative)
-    top_v = jnp.max(s_v, axis=1, keepdims=True).reshape(nb, BLK, 1)
-    top_s = jnp.max(s_s, axis=2, keepdims=True)
-    top = jnp.maximum(top_v, top_s)
-    p_v = jnp.where(vlive, jnp.exp(s_v - top.reshape(TQ, 1)), 0.0)
-    p_s = jnp.where(smask, jnp.exp(s_s - top), 0.0)
-    total = jnp.sum(p_v, axis=1, keepdims=True).reshape(nb, BLK, 1) + jnp.sum(
-        p_s, axis=2, keepdims=True)
-    acc_v = jnp.dot(p_v.astype(jnp.bfloat16), kvert[:, HEAD_SIZE:],
-                    preferred_element_type=jnp.float32)
+    top_v = top_ref[...].reshape(nb, BLK, 1)
+    top = jnp.maximum(top_v, jnp.max(s_s, axis=2, keepdims=True))
+    factor = jnp.exp(top_v - top)
+    p_s = jnp.exp(s_s - top)
+    total = total_ref[...].reshape(nb, BLK, 1) * factor + jnp.sum(p_s, axis=2, keepdims=True)
     acc_s = lax.dot_general(p_s.astype(jnp.bfloat16), kslash[:, :, HEAD_SIZE:],
                             (((2,), (1,)), ((0,), (0,))), preferred_element_type=jnp.float32)
-    acc = acc_v.reshape(nb, BLK, HEAD_SIZE) + acc_s
+    acc = acc_ref[...].reshape(nb, BLK, HEAD_SIZE) * factor + acc_s
     o_ref[...] = (acc / total).reshape(TQ, HEAD_SIZE).astype(o_ref.dtype)
+
+
+def vertical_part(own_query, ckv, verts, count):
+    prefill_stretch = own_query.shape[0]
+    nvc = NVMAX * BLK
+    slot = jnp.arange(nvc, dtype=jnp.int32) // BLK
+    vbias = jnp.where(slot < count, 0.0, big_negative).astype(jnp.float32).reshape(1, nvc)
+    grid_spec = pltpu.PrefetchScalarGridSpec(
+        num_scalar_prefetch=1,
+        grid=(prefill_stretch // TQ,),
+        in_specs=[
+            pl.BlockSpec((TQ, HEAD_SIZE), lambda i, *_: (i, 0)),
+            pl.BlockSpec(ckv.shape, lambda i, *_: (0, 0)),
+            pl.BlockSpec((1, nvc), lambda i, *_: (0, 0)),
+        ],
+        out_specs=[
+            pl.BlockSpec((TQ, HEAD_SIZE), lambda i, *_: (i, 0)),
+            pl.BlockSpec((TQ, 1), lambda i, *_: (i, 0)),
+            pl.BlockSpec((TQ, 1), lambda i, *_: (i, 0)),
+        ],
+        scratch_shapes=[pltpu.VMEM((nvc, 2 * HEAD_SIZE), jnp.bfloat16)],
+    )
+    return pl.pallas_call(
+        vertical_kernel,
+        grid_spec=grid_spec,
+        out_shape=[
+            jax.ShapeDtypeStruct((prefill_stretch, HEAD_SIZE), jnp.float32),
+            jax.ShapeDtypeStruct((prefill_stretch, 1), jnp.float32),
+            jax.ShapeDtypeStruct((prefill_stretch, 1), jnp.float32),
+        ],
+        compiler_params=pltpu.CompilerParams(dimension_semantics=("arbitrary",)),
+    )(verts, own_query, ckv, vbias)
 
 
 def head_attention(own_query, ckv, skv, verts, count, slashes, tok):
@@ -100,6 +135,7 @@
     ncb = CACHE // BLK
     nqb = prefill_stretch // BLK
     nd = NS + 1
+    acc_v, top_v, total_v = vertical_part(own_query, ckv, verts, count)
     offsets = jnp.concatenate([jnp.zeros((1,), jnp.int32), slashes])
     blocks = ncb + jnp.arange(nqb, dtype=jnp.int32)[:, None] - offsets[None, :]
     used = jnp.arange(NVMAX, dtype=jnp.int32)[None, None, :] < count
@@ -109,26 +145,26 @@
     smask = jnp.repeat(valid.astype(jnp.int32), BLK, axis=1).reshape(nqb, 1, nd * BLK)
     nb = TQ // BLK
     grid_spec = pltpu.PrefetchScalarGridSpec(
-        num_scalar_prefetch=3,
+        num_scalar_prefetch=1,
         grid=(prefill_stretch // TQ,),
         in_specs=[
             pl.BlockSpec((TQ, HEAD_SIZE), lambda i, *_: (i, 0)),
             pl.BlockSpec(ckv.shape, lambda i, *_: (0, 0)),
             pl.BlockSpec(skv.shape, lambda i, *_: (0, 0, 0)),
             pl.BlockSpec((nb, 1, nd * BLK), lambda i, *_: (i, 0, 0)),
+            pl.BlockSpec((TQ, HEAD_SIZE), lambda i, *_: (i, 0)),
+            pl.BlockSpec((TQ, 1), lambda i, *_: (i, 0)),
+            pl.BlockSpec((TQ, 1), lambda i, *_: (i, 0)),
         ],
         out_specs=pl.BlockSpec((TQ, HEAD_SIZE), lambda i, *_: (i, 0)),
-        scratch_shapes=[
-            pltpu.VMEM((NVMAX * BLK, 2 * HEAD_SIZE), jnp.bfloat16),
-            pltpu.VMEM((nb, nd * BLK, 2 * HEAD_SIZE), jnp.bfloat16),
-        ],
+        scratch_shapes=[pltpu.VMEM((nb, nd * BLK, 2 * HEAD_SIZE), jnp.bfloat16)],
     )
     return pl.pallas_call(
-        functools.partial(attention_kernel, tok=tok, nz=nz),
+        functools.partial(slash_kernel, tok=tok, nz=nz),
         grid_spec=grid_spec,
         out_shape=jax.ShapeDtypeStruct((prefill_stretch, HEAD_SIZE), jnp.bfloat16),
         compiler_params=pltpu.CompilerParams(dimension_semantics=("arbitrary",)),
-    )(verts, count.reshape(1), sblk, own_query, ckv, skv, smask)
+    )(sblk, own_query, ckv, skv, smask, acc_v, top_v, total_v)
 
 
 def per_device(queries, keys, values, cache_keys, cache_values, vertical, vertical_count, slash):

time: 202 us -> 188 us (0.931)
  waiting for transfers between devices: 69.9 us -> 47.1 us
  Pallas kernels: 46 us -> 52.5 us
    all_gather x1, waiting for transfers between devices: 24.1 us -> 2 us  [per_device(): lax.all_gather(part.reshape(nx * tok, 2 * HEAD_SIZE), 'gz', axis=0, tiled...]
    pallas_call x1 -> x2, Pallas kernels: 46 us -> 52.5 us  [the longest x1 31.3 us: head_attention(): pl.pallas_call(functools.partial(slash_kernel, tok=tok, nz=nz), grid_spec...]
  transfers between devices with their start and end apart: 6 -> 6, of which waited for: 5 -> 5; matrix products, arithmetic and copies ran while one was open for 2% -> 3% of each run, Pallas kernels for 0% -> 11%
where the time goes in v4:
time: 188 us; the launch traced here: 187 us
  Pallas kernels  52.5 us (28%)
  waiting for transfers between devices  47.1 us (25%)
  blocking collectives  46.4 us (25%)
  between operations  14.2 us (8%)
  starting transfers between devices  13.1 us (7%)
  local copies, waits for them, and re-layouts  8.67 us (5%)
  other arithmetic  5.46 us (3%)
    all_to_all x1, blocking collectives, per_device(): lax.all_to_all(result.reshape(prefill_stretch, 1, HEAD_SIZE), ('gx', 'gz'...  35.5 us
    pallas_call x1, Pallas kernels, head_attention(): pl.pallas_call(functools.partial(slash_kernel, tok=tok, nz=nz), grid_spec...  31.3 us
    all_to_all x1, waiting for transfers between devices, per_device(): lax.all_to_all(q_rows, ('gx', 'gz'), split_axis=1, concat_axis=0, tiled=T...  26.6 us
    pallas_call x1, Pallas kernels, vertical_part(): pl.pallas_call(vertical_kernel, grid_spec=grid_spec, out_shape=[jax.Shape...  21.3 us
    ppermute x3, waiting for transfers between devices, from_behind(): return lax.ppermute(x, axis, [(i, (i + by) % peers) for i in range(peers)])  18.5 us
    all_to_all x1, starting transfers between devices, per_device(): lax.all_to_all(q_rows, ('gx', 'gz'), split_axis=1, concat_axis=0, tiled=T...  11.3 us
    all_to_all x1, blocking collectives, per_device(): lax.all_to_all(kv_rows, 'gx', split_axis=1, concat_axis=0, tiled=True)  10.9 us
  transfers between devices with their start and end apart: 6, of which 5 were waited for; matrix products, arithmetic and copies ran while one was open for 3% of the time, Pallas kernels for 11%

profile of v4, /device:TPU:16, one launch (start us, length us, event | category | flops | bytes accessed | tf_op | source)
XLA Modules:
  0.0 187.4 jit_solution(11721486978646433130)
XLA Ops:
  6.5 1.8 pad_maximum_fusion
  8.4 1.7 collective-permute-start.2
  10.1 2.9 %collective-permute-done.1 = bf16[1,128,512]{2,1,0:T(8,128)(2,1)S(1)} collective-permute-done((bf16[1,128,512]{2,1,0:T(8,128)(2,1)}, bf16[1,128,512]{2,1,0:T(8,128)(2,1)S(1)}, u32[]{:S(2)}, u32[]{:S(2)}) %collective-permute-start.1) | collective-permute-done | bytes 131104 | tf_op jit(solution)/shard_map/ppermute | solution.py:25
  13.1 1.3 collective-permute-done.2
  14.5 10.9 %all_to_all.45 = bf16[128,4,256]{2,0,1:T(8,128)(2,1)} all-to-all(bf16[128,4,256]{2,0,1:T(8,128)(2,1)S(1)} %pad_maximum_fusion.1), channel_id=1, replica_groups=mesh['section'=16,'gx'=4,'gz'=8] {'gx'}, dimensions={1} | all-to-all | bytes 524288 | tf_op jit(solution)/shard_map/all_to_all | solution.py:190
  25.5 14.2 %collective-permute-done = bf16[1,128,4096]{2,1,0:T(8,128)(2,1)S(1)} collective-permute-done((bf16[1,128,4096]{2,1,0:T(8,128)(2,1)S(1)}, bf16[1,128,4096]{2,1,0:T(8,128)(2,1)S(1)}, u32[]{:S(2)}, u32[]{:S(2)}) %collective-permute-start) | collective-permute-done | bytes 1048608 | tf_op jit(solution)/shard_map/ppermute | solution.py:25
  39.7 0.2 copy.46
  40.0 1.4 copy.37
  41.3 11.3 %all-to-all-start = ((bf16[128,32,128]{2,0,1:T(8,128)(2,1)}), bf16[128,32,128]{2,0,1:T(8,128)(2,1)S(1)}, u32[]{:S(2)}, u32[]{:S(2)}) async-start(bf16[128,32,128]{2,0,1:T(8,128)(2,1)} %copy.37), calls=%async_computation | async-start | bytes 2097152 | tf_op jit(solution)/shard_map/all_to_all | solution.py:179
  53.3 0.1 pad_add_fusion
  53.4 0.1 broadcast_subtract_fusion
  53.5 0.1 and_reduce_fusion
  53.6 0.1 and_convert_fusion
  53.7 0.1 copy.40
  53.8 0.2 broadcast_in_dim.15
  54.0 0.9 reshape_reshape.4.smask_ref
  54.9 0.1 copy.36
  55.0 0.7 min.12.sblk_ref
  55.7 0.6 compare_select_fusion.vbias_ref
  56.3 26.6 %all-to-all-done = bf16[128,32,128]{2,0,1:T(8,128)(2,1)S(1)} async-done(((bf16[128,32,128]{2,0,1:T(8,128)(2,1)}), bf16[128,32,128]{2,0,1:T(8,128)(2,1)S(1)}, u32[]{:S(2)}, u32[]{:S(2)}) %all-to-all-start) | async-done | bytes 1048608 | tf_op jit(solution)/shard_map/all_to_all | solution.py:179
  82.9 1.0 copy-done
  83.9 21.3 %shard_map.82 = (f32[4096,128]{1,0:T(8,128)}, f32[4096,1]{1,0:T(8,128)}, f32[4096,1]{1,0:T(8,128)}) custom-call(s32[32]{0:T(128)} %bitcast.35, bf16[4096,128]{1,0:T(8,128)(2,1)} %bitcast.25, bf16[4096,256]{1,0:T(8,128)(2,1)} %all-gather.3.cloned.1.call-done.ckv_ref, f32[1,2048]{1,0:T(1,128)} %compare_select_fusion.vbias_ref), custom_call_target="tpu_custom_call" | custom-call | tf_op jit(solution)/shard_map/pallas_call | solution.py:120
  105.1 2.0 %all-gather.5.cloned.1.call-done.skv_ref = bf16[8,512,256]{2,1,0:T(8,128)(2,1)} async-done(((bf16[1,512,256]{2,1,0:T(8,128)(2,1)}), bf16[8,512,256]{2,1,0:T(8,128)(2,1)}) %all-gather.5.cloned.1.call-update) | async-done | bytes 2097168 | tf_op jit(solution)/shard_map/all_gather | solution.py:191
  107.1 31.3 %shard_map.83 = bf16[4096,128]{1,0:T(8,128)(2,1)} custom-call(s32[768]{0:T(1024)} %min.12.sblk_ref, bf16[4096,128]{1,0:T(8,128)(2,1)} %bitcast.26, bf16[4096,256]{1,0:T(8,128)(2,1)} %all-gather.3.cloned.1.call-done.ckv_ref, bf16[8,512,256]{2,1,0:T(8,128)(2,1)} %all-gather.5.cloned.1.call-done.skv_ref, s32[64,1,768]{2,1,0:T(1,128)} %reshape_reshape.4.smask_ref, ...), custom_call_target="tpu_custom_call" | custom-call | tf_op jit(solution)/shard_map/pallas_call | solution.py:162
  138.4 0.5 broadcast.102
  138.9 2.7 %reduce = bf16[4096,128]{1,0:T(8,128)(2,1)S(1)} reduce(bf16[4096,1,128]{2,0,1:T(8,128)(2,1)} %bitcast.27, bf16[]{:T(256)} %broadcast.102), dimensions={1}, to_apply=%copy.42.reduce_sub_computation | reduce | bytes 2097154 | tf_op jit(solution)/shard_map/reshape | solution.py:197
  141.6 0.3 reshape.98
  141.9 35.5 %all_to_all.46 = bf16[32,2,8192]{2,1,0:T(2,128)(2,1)S(1)} all-to-all(bf16[32,2,8192]{2,1,0:T(2,128)(2,1)S(1)} %reshape.98), channel_id=1, replica_groups=mesh['section'=16,'gx'=4,'gz'=8] {'gx','gz'}, dimensions={0} | all-to-all | bytes 2097152 | tf_op jit(solution)/shard_map/all_to_all | solution.py:196
  177.4 1.0 reshape.99
  178.4 0.1 copy.45
  178.6 0.7 copy.43
  179.2 1.3 copy.44
  (21 shorter events, 0.3 us)
Async XLA Ops:
  6.5 18.9 %copy-start.2 = (bf16[1,128,4096]{2,1,0:T(8,128)(2,1)S(1)}, bf16[1,128,4096]{2,1,0:T(8,128)(2,1)}, u32[]{:S(2)}) copy-start(bf16[1,128,4096]{2,1,0:T(8,128)(2,1)} %param.8) | copy-start | bytes 3145732
  6.5 76.4 %all-gather.3.cloned.1.call-start = ((), (), s32[]{:S(2)}) async-start(), calls=%async_computation.3 | async-start | bytes 2359296 | tf_op jit(solution)/shard_map/all_gather | solution.py:193
  8.4 98.8 %all-gather.5.cloned.1.call-start = ((), (), s32[]{:S(2)}) async-start(), calls=%async_computation.4 | async-start | bytes 2359296 | tf_op jit(solution)/shard_map/all_gather | solution.py:191
  8.4 4.6 %collective-permute-start.1 = (bf16[1,128,512]{2,1,0:T(8,128)(2,1)}, bf16[1,128,512]{2,1,0:T(8,128)(2,1)S(1)}, u32[]{:S(2)}, u32[]{:S(2)}) collective-permute-start(bf16[1,128,512]{2,1,0:T(8,128)(2,1)} %param.9), channel_id=1, source_target_pairs={{0,32},{32,64},{64,96},{96,128},{128,160},{160,192},{192,224},{224... | collective-permute-start | bytes 393224 | tf_op jit(solution)/shard_map/ppermute | solution.py:25
  8.4 6.0 %collective-permute-start.2 = (bf16[1,128,512]{2,1,0:T(8,128)(2,1)}, bf16[1,128,512]{2,1,0:T(8,128)(2,1)S(1)}, u32[]{:S(2)}, u32[]{:S(2)}) collective-permute-start(bf16[1,128,512]{2,1,0:T(8,128)(2,1)} %param.10), channel_id=1, source_target_pairs={{0,32},{32,64},{64,96},{96,128},{128,160},{160,192},{192,224},{224... | collective-permute-start | bytes 393224 | tf_op jit(solution)/shard_map/ppermute | solution.py:25
  25.4 14.2 %collective-permute-start = (bf16[1,128,4096]{2,1,0:T(8,128)(2,1)S(1)}, bf16[1,128,4096]{2,1,0:T(8,128)(2,1)S(1)}, u32[]{:S(2)}, u32[]{:S(2)}) collective-permute-start(bf16[1,128,4096]{2,1,0:T(8,128)(2,1)S(1)} %copy-done.2), channel_id=1, source_target_pairs={{0,32},{32,64},{64,96},{96,128},{128,160},{160,192},{192,224},{224... | collective-permute-start | bytes 3145736 | tf_op jit(solution)/shard_map/ppermute | solution.py:25
  39.9 13.4 %copy-start.3 = (s32[1,1,11]{2,1,0:T(1,128)S(1)}, s32[1,1,11]{2,1,0:T(1,128)}, u32[]{:S(2)}) copy-start(s32[1,1,11]{2,1,0:T(1,128)} %param.15) | copy-start | bytes 136
  39.9 13.5 %copy-start.1 = (s32[1,1,32]{2,1,0:T(1,128)S(1)}, s32[1,1,32]{2,1,0:T(1,128)}, u32[]{:S(2)}) copy-start(s32[1,1,32]{2,1,0:T(1,128)} %param.13) | copy-start | bytes 388
  41.3 41.6 %all-to-all-start = ((bf16[128,32,128]{2,0,1:T(8,128)(2,1)}), bf16[128,32,128]{2,0,1:T(8,128)(2,1)S(1)}, u32[]{:S(2)}, u32[]{:S(2)}) async-start(bf16[128,32,128]{2,0,1:T(8,128)(2,1)} %copy.37), calls=%async_computation | async-start | bytes 2097152 | tf_op jit(solution)/shard_map/all_to_all | solution.py:179
  82.9 1.0 copy-start
Sparse Core Ops, SparseCore 0:
  9.4 52.8 all-gather.2
  64.4 42.6 all-gather.4

commit v5 on v4

--- a/solution.py
+++ b/solution.py
@@ -51,41 +51,34 @@
                            preferred_element_type=jnp.float32)
 
 
-def slash_kernel(sblk_ref, q_ref, ckv_ref, skv_ref, smask_ref, acc_ref, top_ref, total_ref,
-                 o_ref, kslash, *, tok, nz):
+def slash_kernel(crow_ref, splane_ref, srow_ref, pick_ref, q_ref, ckv_ref, skv_ref, sbias_ref,
+                 acc_ref, top_ref, total_ref, o_ref, kslash, causal_bias):
     nb = TQ // BLK
     nd = NS + 1
     width = nd * BLK
     tile = pl.program_id(0)
     softmax_scale = 1.0 / math.sqrt(HEAD_SIZE)
-    ncb = CACHE // BLK
-    per_dev = tok // BLK
+
+    @pl.when(tile == 0)
+    def _():
+        col = lax.broadcasted_iota(jnp.int32, (BLK, width), 1)
+        row = lax.broadcasted_iota(jnp.int32, (BLK, width), 0)
+        causal = (col >= BLK) | (col <= row)
+        causal_bias[...] = jnp.where(causal, 0.0, big_negative).astype(jnp.float32)
 
     for b in range(nb):
         qb = tile * nb + b
         for d in range(nd):
-            blk = sblk_ref[qb * nd + d]
-
-            @pl.when(blk < ncb)
-            def _():
-                src = pl.multiple_of(blk * BLK, BLK)
-                kslash[b, pl.ds(d * BLK, BLK), :] = ckv_ref[pl.ds(src, BLK), :]
-
-            @pl.when(blk >= ncb)
-            def _():
-                s = blk - ncb
-                dev = s // per_dev
-                row = pl.multiple_of((dev // nz) * tok + (s % per_dev) * BLK, BLK)
-                kslash[b, pl.ds(d * BLK, BLK), :] = skv_ref[dev % nz, pl.ds(row, BLK), :]
+            at = qb * nd + d
+            from_cache = ckv_ref[pl.ds(pl.multiple_of(crow_ref[at], BLK), BLK), :]
+            from_stretch = skv_ref[splane_ref[at], pl.ds(pl.multiple_of(srow_ref[at], BLK), BLK), :]
+            kslash[b, pl.ds(d * BLK, BLK), :] = jnp.where(pick_ref[at] > 0, from_stretch,
+                                                          from_cache)
 
     q3 = q_ref[...].reshape(nb, BLK, HEAD_SIZE)
     s_s = lax.dot_general(q3, kslash[:, :, :HEAD_SIZE], (((2,), (2,)), ((0,), (0,))),
                           preferred_element_type=jnp.float32) * softmax_scale
-    col = lax.broadcasted_iota(jnp.int32, (nb, BLK, width), 2)
-    row = lax.broadcasted_iota(jnp.int32, (nb, BLK, width), 1)
-    causal = (col >= BLK) | (col <= row)
-    smask = (smask_ref[...] > 0) & causal
-    s_s = jnp.where(smask, s_s, big_negative)
+    s_s = s_s + sbias_ref[...] + causal_bias[...][None, :, :]
     top_v = top_ref[...].reshape(nb, BLK, 1)
     top = jnp.maximum(top_v, jnp.max(s_s, axis=2, keepdims=True))
     factor = jnp.exp(top_v - top)
@@ -141,11 +134,18 @@
     used = jnp.arange(NVMAX, dtype=jnp.int32)[None, None, :] < count
     listed = jnp.any((blocks[:, :, None] == verts[None, None, :]) & used, axis=2)
     valid = (blocks >= 0) & jnp.logical_not(listed)
-    sblk = jnp.clip(blocks, 0, ncb + nqb - 1).reshape(-1)
-    smask = jnp.repeat(valid.astype(jnp.int32), BLK, axis=1).reshape(nqb, 1, nd * BLK)
+    per_dev = tok // BLK
+    stretch_blk = jnp.clip(blocks - ncb, 0, nqb - 1)
+    dev = stretch_blk // per_dev
+    pick = (blocks >= ncb).astype(jnp.int32).reshape(-1)
+    crow = (jnp.clip(blocks, 0, ncb - 1) * BLK).reshape(-1)
+    splane = (dev % nz).reshape(-1)
+    srow = ((dev // nz) * tok + (stretch_blk % per_dev) * BLK).reshape(-1)
+    sbias = jnp.repeat(jnp.where(valid, 0.0, big_negative).astype(jnp.float32), BLK,
+                       axis=1).reshape(nqb, 1, nd * BLK)
     nb = TQ // BLK
     grid_spec = pltpu.PrefetchScalarGridSpec(
-        num_scalar_prefetch=1,
+        num_scalar_prefetch=4,
         grid=(prefill_stretch // TQ,),
         in_specs=[
             pl.BlockSpec((TQ, HEAD_SIZE), lambda i, *_: (i, 0)),
@@ -157,14 +157,17 @@
             pl.BlockSpec((TQ, 1), lambda i, *_: (i, 0)),
         ],
         out_specs=pl.BlockSpec((TQ, HEAD_SIZE), lambda i, *_: (i, 0)),
-        scratch_shapes=[pltpu.VMEM((nb, nd * BLK, 2 * HEAD_SIZE), jnp.bfloat16)],
+        scratch_shapes=[
+            pltpu.VMEM((nb, nd * BLK, 2 * HEAD_SIZE), jnp.bfloat16),
+            pltpu.VMEM((BLK, nd * BLK), jnp.float32),
+        ],
     )
     return pl.pallas_call(
-        functools.partial(slash_kernel, tok=tok, nz=nz),
+        slash_kernel,
         grid_spec=grid_spec,
         out_shape=jax.ShapeDtypeStruct((prefill_stretch, HEAD_SIZE), jnp.bfloat16),
         compiler_params=pltpu.CompilerParams(dimension_semantics=("arbitrary",)),
-    )(sblk, own_query, ckv, skv, smask, acc_v, top_v, total_v)
+    )(crow, splane, srow, pick, own_query, ckv, skv, sbias, acc_v, top_v, total_v)
 
 
 def per_device(queries, keys, values, cache_keys, cache_values, vertical, vertical_count, slash):

time: 188 us -> 174 us (0.926)
  the two profiles are of different devices: /device:TPU:16 before, /device:TPU:24 now
where the time goes in v5:
time: 174 us; the launch traced here: 173 us
  waiting for transfers between devices  44 us (25%)
  blocking collectives  43.2 us (25%)
  Pallas kernels  41.9 us (24%)
  starting transfers between devices  14.3 us (8%)
  between operations  14.2 us (8%)
  local copies, waits for them, and re-layouts  9.67 us (6%)
  other arithmetic  6.14 us (4%)
    all_to_all x1, blocking collectives, per_device(): lax.all_to_all(result.reshape(prefill_stretch, 1, HEAD_SIZE), ('gx', 'gz'...  31.6 us
    all_to_all x1, waiting for transfers between devices, per_device(): lax.all_to_all(q_rows, ('gx', 'gz'), split_axis=1, concat_axis=0, tiled=T...  22.3 us
    pallas_call x1, Pallas kernels, vertical_part(): pl.pallas_call(vertical_kernel, grid_spec=grid_spec, out_shape=[jax.Shape...  21.3 us
    pallas_call x1, Pallas kernels, head_attention(): pl.pallas_call(slash_kernel, grid_spec=grid_spec, out_shape=jax.ShapeDtyp...  20.6 us
    ppermute x3, waiting for transfers between devices, from_behind(): return lax.ppermute(x, axis, [(i, (i + by) % peers) for i in range(peers)])  17.2 us
    all_to_all x1, blocking collectives, per_device(): lax.all_to_all(kv_rows, 'gx', split_axis=1, concat_axis=0, tiled=True)  11.6 us
    all_to_all x1, starting transfers between devices, per_device(): lax.all_to_all(q_rows, ('gx', 'gz'), split_axis=1, concat_axis=0, tiled=T...  11.3 us
    all_gather x1, waiting for transfers between devices, per_device(): lax.all_gather(part.reshape(nx * tok, 2 * HEAD_SIZE), 'gz', axis=0, tiled...  4.49 us
  transfers between devices with their start and end apart: 6, of which 5 were waited for; matrix products, arithmetic and copies ran while one was open for 4% of the time, Pallas kernels for 12%

profile of v5, /device:TPU:24, one launch (start us, length us, event | category | flops | bytes accessed | tf_op | source)
XLA Modules:
  0.0 173.4 jit_solution(15231245860325400958)
XLA Ops:
  6.5 1.8 %pad_maximum_fusion = bf16[512,256]{1,0:T(8,128)(2,1)} fusion(bf16[512,128]{1,0:T(8,128)(2,1)} %bitcast.33, bf16[512,128]{1,0:T(8,128)(2,1)} %bitcast.34), kind=kLoop, calls=%fused_computation | loop fusion | flops 524288 | bytes 524288 | tf_op jit(solution)/shard_map/concatenate | solution.py:195
  8.4 2.9 %collective-permute-start.2 = (bf16[1,128,512]{2,1,0:T(8,128)(2,1)}, bf16[1,128,512]{2,1,0:T(8,128)(2,1)S(1)}, u32[]{:S(2)}, u32[]{:S(2)}) collective-permute-start(bf16[1,128,512]{2,1,0:T(8,128)(2,1)} %param.10), channel_id=1, source_target_pairs={{0,32},{32,64},{64,96},{96,128},{128,160},{160,192},{192,224},{224... | collective-permute-start | bytes 393224 | tf_op jit(solution)/shard_map/ppermute | solution.py:25
  11.3 1.7 collective-permute-done.1
  13.1 1.3 collective-permute-done.2
  14.5 11.6 %all_to_all.45 = bf16[128,4,256]{2,0,1:T(8,128)(2,1)} all-to-all(bf16[128,4,256]{2,0,1:T(8,128)(2,1)S(1)} %pad_maximum_fusion.1), channel_id=1, replica_groups=mesh['section'=16,'gx'=4,'gz'=8] {'gx'}, dimensions={1} | all-to-all | bytes 524288 | tf_op jit(solution)/shard_map/all_to_all | solution.py:193
  26.1 14.2 %collective-permute-done = bf16[1,128,4096]{2,1,0:T(8,128)(2,1)S(1)} collective-permute-done((bf16[1,128,4096]{2,1,0:T(8,128)(2,1)S(1)}, bf16[1,128,4096]{2,1,0:T(8,128)(2,1)S(1)}, u32[]{:S(2)}, u32[]{:S(2)}) %collective-permute-start) | collective-permute-done | bytes 1048608 | tf_op jit(solution)/shard_map/ppermute | solution.py:25
  40.4 0.2 copy.48
  40.6 1.4 copy.39
  42.0 11.3 %all-to-all-start = ((bf16[128,32,128]{2,0,1:T(8,128)(2,1)}), bf16[128,32,128]{2,0,1:T(8,128)(2,1)S(1)}, u32[]{:S(2)}, u32[]{:S(2)}) async-start(bf16[128,32,128]{2,0,1:T(8,128)(2,1)} %copy.39), calls=%async_computation | async-start | bytes 2097152 | tf_op jit(solution)/shard_map/all_to_all | solution.py:182
  54.2 0.1 and_reduce_fusion
  54.4 0.1 copy.42
  54.5 0.2 broadcast_in_dim.25
  54.7 0.9 reshape_reshape.4.sbias_ref
  55.7 0.1 min.17
  55.9 0.7 mul.19.crow_ref
  56.7 0.1 copy.38
  56.8 0.7 reshape.118.pick_ref
  57.5 0.6 compare_select_fusion.vbias_ref
  58.1 0.6 fusion.6
  58.7 22.3 %all-to-all-done = bf16[128,32,128]{2,0,1:T(8,128)(2,1)S(1)} async-done(((bf16[128,32,128]{2,0,1:T(8,128)(2,1)}), bf16[128,32,128]{2,0,1:T(8,128)(2,1)S(1)}, u32[]{:S(2)}, u32[]{:S(2)}) %all-to-all-start) | async-done | bytes 1048608 | tf_op jit(solution)/shard_map/all_to_all | solution.py:182
  81.0 1.0 copy-done
  81.9 21.3 %shard_map.82 = (f32[4096,128]{1,0:T(8,128)}, f32[4096,1]{1,0:T(8,128)}, f32[4096,1]{1,0:T(8,128)}) custom-call(s32[32]{0:T(128)} %bitcast.35, bf16[4096,128]{1,0:T(8,128)(2,1)} %bitcast.25, bf16[4096,256]{1,0:T(8,128)(2,1)} %all-gather.3.cloned.1.call-done.ckv_ref, f32[1,2048]{1,0:T(1,128)} %compare_select_fusion.vbias_ref), custom_call_target="tpu_custom_call" | custom-call | tf_op jit(solution)/shard_map/pallas_call | solution.py:113
  103.2 4.5 %all-gather.5.cloned.1.call-done.skv_ref = bf16[8,512,256]{2,1,0:T(8,128)(2,1)} async-done(((bf16[1,512,256]{2,1,0:T(8,128)(2,1)}), bf16[8,512,256]{2,1,0:T(8,128)(2,1)}) %all-gather.5.cloned.1.call-update) | async-done | bytes 2097168 | tf_op jit(solution)/shard_map/all_gather | solution.py:194
  107.7 20.6 %shard_map.83 = bf16[4096,128]{1,0:T(8,128)(2,1)} custom-call(s32[768]{0:T(1024)} %mul.19.crow_ref, s32[768]{0:T(1024)} %get-tuple-element.12.splane_ref, s32[768]{0:T(1024)} %get-tuple-element.11.srow_ref, s32[768]{0:T(1024)} %reshape.118.pick_ref, bf16[4096,128]{1,0:T(8,128)(2,1)} %bitcast.26, bf16[4096,256]{1,0:T(8,128)(2,1)} %all-gather.3.cloned.1.call-done.ckv_ref, ...), custom_call_target="tpu_custom_call" | custom-call | tf_op jit(solution)/shard_map/pallas_call | solution.py:165
  128.3 0.5 broadcast.189
  128.8 2.7 %reduce = bf16[4096,128]{1,0:T(8,128)(2,1)S(1)} reduce(bf16[4096,1,128]{2,0,1:T(8,128)(2,1)} %bitcast.27, bf16[]{:T(256)} %broadcast.189), dimensions={1}, to_apply=%copy.44.reduce_sub_computation | reduce | bytes 2097154 | tf_op jit(solution)/shard_map/reshape | solution.py:200
  131.5 0.3 reshape.119
  131.7 31.6 %all_to_all.46 = bf16[32,2,8192]{2,1,0:T(2,128)(2,1)S(1)} all-to-all(bf16[32,2,8192]{2,1,0:T(2,128)(2,1)S(1)} %reshape.119), channel_id=1, replica_groups=mesh['section'=16,'gx'=4,'gz'=8] {'gx','gz'}, dimensions={0} | all-to-all | bytes 2097152 | tf_op jit(solution)/shard_map/all_to_all | solution.py:199
  163.3 1.0 reshape.120
  164.4 0.1 copy.47
  164.5 0.7 copy.45
  165.2 1.3 copy.46
  (27 shorter events, 0.8 us)
Async XLA Ops:
  6.5 19.6 %copy-start.2 = (bf16[1,128,4096]{2,1,0:T(8,128)(2,1)S(1)}, bf16[1,128,4096]{2,1,0:T(8,128)(2,1)}, u32[]{:S(2)}) copy-start(bf16[1,128,4096]{2,1,0:T(8,128)(2,1)} %param.8) | copy-start | bytes 3145732
  6.5 74.4 %all-gather.3.cloned.1.call-start = ((), (), s32[]{:S(2)}) async-start(), calls=%async_computation.3 | async-start | bytes 2359296 | tf_op jit(solution)/shard_map/all_gather | solution.py:196
  8.3 99.3 %all-gather.5.cloned.1.call-start = ((), (), s32[]{:S(2)}) async-start(), calls=%async_computation.4 | async-start | bytes 2359296 | tf_op jit(solution)/shard_map/all_gather | solution.py:194
  8.4 4.6 %collective-permute-start.1 = (bf16[1,128,512]{2,1,0:T(8,128)(2,1)}, bf16[1,128,512]{2,1,0:T(8,128)(2,1)S(1)}, u32[]{:S(2)}, u32[]{:S(2)}) collective-permute-start(bf16[1,128,512]{2,1,0:T(8,128)(2,1)} %param.9), channel_id=1, source_target_pairs={{0,32},{32,64},{64,96},{96,128},{128,160},{160,192},{192,224},{224... | collective-permute-start | bytes 393224 | tf_op jit(solution)/shard_map/ppermute | solution.py:25
  8.4 6.0 %collective-permute-start.2 = (bf16[1,128,512]{2,1,0:T(8,128)(2,1)}, bf16[1,128,512]{2,1,0:T(8,128)(2,1)S(1)}, u32[]{:S(2)}, u32[]{:S(2)}) collective-permute-start(bf16[1,128,512]{2,1,0:T(8,128)(2,1)} %param.10), channel_id=1, source_target_pairs={{0,32},{32,64},{64,96},{96,128},{128,160},{160,192},{192,224},{224... | collective-permute-start | bytes 393224 | tf_op jit(solution)/shard_map/ppermute | solution.py:25
  26.1 14.2 %collective-permute-start = (bf16[1,128,4096]{2,1,0:T(8,128)(2,1)S(1)}, bf16[1,128,4096]{2,1,0:T(8,128)(2,1)S(1)}, u32[]{:S(2)}, u32[]{:S(2)}) collective-permute-start(bf16[1,128,4096]{2,1,0:T(8,128)(2,1)S(1)} %copy-done.2), channel_id=1, source_target_pairs={{0,32},{32,64},{64,96},{96,128},{128,160},{160,192},{192,224},{224... | collective-permute-start | bytes 3145736 | tf_op jit(solution)/shard_map/ppermute | solution.py:25
  40.6 13.4 %copy-start.3 = (s32[1,1,11]{2,1,0:T(1,128)S(1)}, s32[1,1,11]{2,1,0:T(1,128)}, u32[]{:S(2)}) copy-start(s32[1,1,11]{2,1,0:T(1,128)} %param.15) | copy-start | bytes 136
  40.6 13.5 %copy-start.1 = (s32[1,1,32]{2,1,0:T(1,128)S(1)}, s32[1,1,32]{2,1,0:T(1,128)}, u32[]{:S(2)}) copy-start(s32[1,1,32]{2,1,0:T(1,128)} %param.13) | copy-start | bytes 388
  42.0 38.9 %all-to-all-start = ((bf16[128,32,128]{2,0,1:T(8,128)(2,1)}), bf16[128,32,128]{2,0,1:T(8,128)(2,1)S(1)}, u32[]{:S(2)}, u32[]{:S(2)}) async-start(bf16[128,32,128]{2,0,1:T(8,128)(2,1)} %copy.39), calls=%async_computation | async-start | bytes 2097152 | tf_op jit(solution)/shard_map/all_to_all | solution.py:182
  80.9 1.0 copy-start
Sparse Core Ops, SparseCore 0:
  9.4 50.8 all-gather.2
  62.4 45.2 all-gather.4

commit v6 on v5

--- a/solution.py
+++ b/solution.py
@@ -52,7 +52,7 @@
 
 
 def slash_kernel(crow_ref, splane_ref, srow_ref, pick_ref, q_ref, ckv_ref, skv_ref, sbias_ref,
-                 acc_ref, top_ref, total_ref, o_ref, kslash, causal_bias):
+                 acc_ref, top_ref, total_ref, o_ref, kslash, causal_bias, *, parity):
     nb = TQ // BLK
     nd = NS + 1
     width = nd * BLK
@@ -67,7 +67,7 @@
         causal_bias[...] = jnp.where(causal, 0.0, big_negative).astype(jnp.float32)
 
     for b in range(nb):
-        qb = tile * nb + b
+        qb = 2 * (tile * nb + b) + parity
         for d in range(nd):
             at = qb * nd + d
             from_cache = ckv_ref[pl.ds(pl.multiple_of(crow_ref[at], BLK), BLK), :]
@@ -78,7 +78,7 @@
     q3 = q_ref[...].reshape(nb, BLK, HEAD_SIZE)
     s_s = lax.dot_general(q3, kslash[:, :, :HEAD_SIZE], (((2,), (2,)), ((0,), (0,))),
                           preferred_element_type=jnp.float32) * softmax_scale
-    s_s = s_s + sbias_ref[...] + causal_bias[...][None, :, :]
+    s_s = s_s + sbias_ref[...].reshape(nb, 1, width) + causal_bias[...][None, :, :]
     top_v = top_ref[...].reshape(nb, BLK, 1)
     top = jnp.maximum(top_v, jnp.max(s_s, axis=2, keepdims=True))
     factor = jnp.exp(top_v - top)
@@ -87,7 +87,7 @@
     acc_s = lax.dot_general(p_s.astype(jnp.bfloat16), kslash[:, :, HEAD_SIZE:],
                             (((2,), (1,)), ((0,), (0,))), preferred_element_type=jnp.float32)
     acc = acc_ref[...].reshape(nb, BLK, HEAD_SIZE) * factor + acc_s
-    o_ref[...] = (acc / total).reshape(TQ, HEAD_SIZE).astype(o_ref.dtype)
+    o_ref[...] = (acc / total).astype(o_ref.dtype)
 
 
 def vertical_part(own_query, ckv, verts, count):
@@ -144,30 +144,40 @@
     sbias = jnp.repeat(jnp.where(valid, 0.0, big_negative).astype(jnp.float32), BLK,
                        axis=1).reshape(nqb, 1, nd * BLK)
     nb = TQ // BLK
-    grid_spec = pltpu.PrefetchScalarGridSpec(
-        num_scalar_prefetch=4,
-        grid=(prefill_stretch // TQ,),
-        in_specs=[
-            pl.BlockSpec((TQ, HEAD_SIZE), lambda i, *_: (i, 0)),
-            pl.BlockSpec(ckv.shape, lambda i, *_: (0, 0)),
-            pl.BlockSpec(skv.shape, lambda i, *_: (0, 0, 0)),
-            pl.BlockSpec((nb, 1, nd * BLK), lambda i, *_: (i, 0, 0)),
-            pl.BlockSpec((TQ, HEAD_SIZE), lambda i, *_: (i, 0)),
-            pl.BlockSpec((TQ, 1), lambda i, *_: (i, 0)),
-            pl.BlockSpec((TQ, 1), lambda i, *_: (i, 0)),
-        ],
-        out_specs=pl.BlockSpec((TQ, HEAD_SIZE), lambda i, *_: (i, 0)),
-        scratch_shapes=[
-            pltpu.VMEM((nb, nd * BLK, 2 * HEAD_SIZE), jnp.bfloat16),
-            pltpu.VMEM((BLK, nd * BLK), jnp.float32),
-        ],
-    )
-    return pl.pallas_call(
-        slash_kernel,
-        grid_spec=grid_spec,
-        out_shape=jax.ShapeDtypeStruct((prefill_stretch, HEAD_SIZE), jnp.bfloat16),
-        compiler_params=pltpu.CompilerParams(dimension_semantics=("arbitrary",)),
-    )(crow, splane, srow, pick, own_query, ckv, skv, sbias, acc_v, top_v, total_v)
+    width = nd * BLK
+    halves = nqb // 2
+    q4 = own_query.reshape(halves, 2, BLK, HEAD_SIZE)
+    acc4 = acc_v.reshape(halves, 2, BLK, HEAD_SIZE)
+    top4 = top_v.reshape(halves, 2, BLK, 1)
+    total4 = total_v.reshape(halves, 2, BLK, 1)
+    sbias4 = sbias.reshape(halves, 2, 1, width)
+    outs = []
+    for parity in range(2):
+        grid_spec = pltpu.PrefetchScalarGridSpec(
+            num_scalar_prefetch=4,
+            grid=(halves // nb,),
+            in_specs=[
+                pl.BlockSpec((nb, 1, BLK, HEAD_SIZE), lambda i, *_, p=parity: (i, p, 0, 0)),
+                pl.BlockSpec(ckv.shape, lambda i, *_: (0, 0)),
+                pl.BlockSpec(skv.shape, lambda i, *_: (0, 0, 0)),
+                pl.BlockSpec((nb, 1, 1, width), lambda i, *_, p=parity: (i, p, 0, 0)),
+                pl.BlockSpec((nb, 1, BLK, HEAD_SIZE), lambda i, *_, p=parity: (i, p, 0, 0)),
+                pl.BlockSpec((nb, 1, BLK, 1), lambda i, *_, p=parity: (i, p, 0, 0)),
+                pl.BlockSpec((nb, 1, BLK, 1), lambda i, *_, p=parity: (i, p, 0, 0)),
+            ],
+            out_specs=pl.BlockSpec((nb, BLK, HEAD_SIZE), lambda i, *_: (i, 0, 0)),
+            scratch_shapes=[
+                pltpu.VMEM((nb, width, 2 * HEAD_SIZE), jnp.bfloat16),
+                pltpu.VMEM((BLK, width), jnp.float32),
+            ],
+        )
+        outs.append(pl.pallas_call(
+            functools.partial(slash_kernel, parity=parity),
+            grid_spec=grid_spec,
+            out_shape=jax.ShapeDtypeStruct((halves, BLK, HEAD_SIZE), jnp.bfloat16),
+            compiler_params=pltpu.CompilerParams(dimension_semantics=("arbitrary",)),
+        )(crow, splane, srow, pick, q4, ckv, skv, sbias4, acc4, top4, total4))
+    return outs
 
 
 def per_device(queries, keys, values, cache_keys, cache_values, vertical, vertical_count, slash):
@@ -194,16 +204,14 @@
     skv = lax.all_gather(part.reshape(nx * tok, 2 * HEAD_SIZE), "gz", axis=0, tiled=False)
     cache_part = jnp.concatenate([cache_keys[0, 0], cache_values[0, 0]], axis=1)
     ckv = lax.all_gather(cache_part, "gz", axis=0, tiled=True)
-    result = head_attention(own_query, ckv, skv, vertical[0, 0], vertical_count[0, 0],
+    halves = head_attention(own_query, ckv, skv, vertical[0, 0], vertical_count[0, 0],
                             slash[0, 0], tok)
-    back = lax.all_to_all(
-        result.reshape(prefill_stretch, 1, HEAD_SIZE),
-        ("gx", "gz"),
-        split_axis=0,
-        concat_axis=1,
-        tiled=True,
-    )
-    return back.reshape(1, tok, heads * HEAD_SIZE)
+    pieces = []
+    for half in halves:
+        moved = lax.all_to_all(half[:, :, None, :], ("gx", "gz"), split_axis=0, concat_axis=2,
+                               tiled=True)
+        pieces.append(moved.reshape(tok // 2, heads * HEAD_SIZE))
+    return jnp.concatenate(pieces, axis=0).reshape(1, tok, heads * HEAD_SIZE)
 
 
 def solution(mesh):

time: 174 us -> 172 us (0.989)
  blocking collectives: 43.2 us -> 11.6 us
  waiting for transfers between devices: 44 us -> 59.4 us
  starting transfers between devices: 14.3 us -> 28.9 us
  Pallas kernels: 41.9 us -> 45.7 us
  local copies, waits for them, and re-layouts: 9.67 us -> 6.81 us
    all_to_all x1 -> x0, blocking collectives: 31.6 us -> none  [per_device(): lax.all_to_all(result.reshape(prefill_stretch, 1, HEAD_SIZE), ('gx', 'gz'...]
    all_to_all x0 -> x2, waiting for transfers between devices: none -> 15.5 us  [per_device(): lax.all_to_all(half[:, :, None, :], ('gx', 'gz'), split_axis=0, concat_ax...]
    all_to_all x0 -> x2, starting transfers between devices: none -> 14.7 us  [per_device(): lax.all_to_all(half[:, :, None, :], ('gx', 'gz'), split_axis=0, concat_ax...]
    pallas_call x1 -> x2, Pallas kernels: 20.6 us -> 24.5 us  [head_attention(): pl.pallas_call(functools.partial(slash_kernel, parity=parity), grid_spec=...]
  transfers between devices with their start and end apart: 6 -> 8, of which waited for: 5 -> 7; matrix products, arithmetic and copies ran while one was open for 4% -> 4% of each run, Pallas kernels for 12% -> 20%
where the time goes in v6:
time: 172 us; the launch traced here: 171 us
  waiting for transfers between devices  59.4 us (35%)
  Pallas kernels  45.7 us (27%)
  starting transfers between devices  28.9 us (17%)
  between operations  14.2 us (8%)
  blocking collectives  11.6 us (7%)
  local copies, waits for them, and re-layouts  6.81 us (4%)
  other arithmetic  4.57 us (3%)
    pallas_call x2, Pallas kernels, head_attention(): pl.pallas_call(functools.partial(slash_kernel, parity=parity), grid_spec=...  24.5 us
    all_to_all x1, waiting for transfers between devices, per_device(): lax.all_to_all(q_rows, ('gx', 'gz'), split_axis=1, concat_axis=0, tiled=T...  22.3 us
    pallas_call x1, Pallas kernels, vertical_part(): pl.pallas_call(vertical_kernel, grid_spec=grid_spec, out_shape=[jax.Shape...  21.3 us
    ppermute x3, waiting for transfers between devices, from_behind(): return lax.ppermute(x, axis, [(i, (i + by) % peers) for i in range(peers)])  17.2 us
    all_to_all x2, waiting for transfers between devices, per_device(): lax.all_to_all(half[:, :, None, :], ('gx', 'gz'), split_axis=0, concat_ax...  15.5 us
    all_to_all x2, starting transfers between devices, per_device(): lax.all_to_all(half[:, :, None, :], ('gx', 'gz'), split_axis=0, concat_ax...  14.7 us
    all_to_all x1, blocking collectives, per_device(): lax.all_to_all(kv_rows, 'gx', split_axis=1, concat_axis=0, tiled=True)  11.6 us
    all_to_all x1, starting transfers between devices, per_device(): lax.all_to_all(q_rows, ('gx', 'gz'), split_axis=1, concat_axis=0, tiled=T...  11.3 us
  transfers between devices with their start and end apart: 8, of which 7 were waited for; matrix products, arithmetic and copies ran while one was open for 4% of the time, Pallas kernels for 20%

profile of v6, /device:TPU:24, one launch (start us, length us, event | category | flops | bytes accessed | tf_op | source)
XLA Modules:
  0.0 171.2 jit_solution(7880921102479485673)
XLA Ops:
  6.5 1.8 %pad_maximum_fusion = bf16[512,256]{1,0:T(8,128)(2,1)} fusion(bf16[512,128]{1,0:T(8,128)(2,1)} %bitcast.67, bf16[512,128]{1,0:T(8,128)(2,1)} %bitcast.68), kind=kLoop, calls=%fused_computation.3 | loop fusion | flops 524288 | bytes 524288 | tf_op jit(solution)/shard_map/concatenate | solution.py:205
  8.5 2.9 %collective-permute-start.2 = (bf16[1,128,512]{2,1,0:T(8,128)(2,1)}, bf16[1,128,512]{2,1,0:T(8,128)(2,1)S(1)}, u32[]{:S(2)}, u32[]{:S(2)}) collective-permute-start(bf16[1,128,512]{2,1,0:T(8,128)(2,1)} %param.10), channel_id=1, source_target_pairs={{0,32},{32,64},{64,96},{96,128},{128,160},{160,192},{192,224},{224... | collective-permute-start | bytes 393224 | tf_op jit(solution)/shard_map/ppermute | solution.py:25
  11.3 1.7 collective-permute-done.1
  13.1 1.3 collective-permute-done.2
  14.6 11.6 %all_to_all.60 = bf16[128,4,256]{2,0,1:T(8,128)(2,1)} all-to-all(bf16[128,4,256]{2,0,1:T(8,128)(2,1)S(1)} %pad_maximum_fusion.1), channel_id=1, replica_groups=mesh['section'=16,'gx'=4,'gz'=8] {'gx'}, dimensions={1} | all-to-all | bytes 524288 | tf_op jit(solution)/shard_map/all_to_all | solution.py:203
  26.2 14.2 %collective-permute-done = bf16[1,128,4096]{2,1,0:T(8,128)(2,1)S(1)} collective-permute-done((bf16[1,128,4096]{2,1,0:T(8,128)(2,1)S(1)}, bf16[1,128,4096]{2,1,0:T(8,128)(2,1)S(1)}, u32[]{:S(2)}, u32[]{:S(2)}) %collective-permute-start) | collective-permute-done | bytes 1048608 | tf_op jit(solution)/shard_map/ppermute | solution.py:25
  40.4 0.2 copy.41
  40.7 1.4 copy.31
  42.0 11.3 %all-to-all-start = ((bf16[128,32,128]{2,0,1:T(8,128)(2,1)}), bf16[128,32,128]{2,0,1:T(8,128)(2,1)S(1)}, u32[]{:S(2)}, u32[]{:S(2)}) async-start(bf16[128,32,128]{2,0,1:T(8,128)(2,1)} %copy.31), calls=%async_computation | async-start | bytes 2097152 | tf_op jit(solution)/shard_map/all_to_all | solution.py:192
  54.2 0.1 copy.30
  54.3 0.7 reshape.136.pick_ref
  55.1 0.1 and_reduce_fusion
  55.4 0.1 min.17
  55.7 0.7 mul.19.crow_ref
  56.3 0.2 broadcast_in_dim.31
  56.5 0.9 reshape_reshape_reshape.4.sbias_ref
  57.5 0.6 compare_select_fusion.vbias_ref
  58.1 0.6 fusion.6
  58.7 22.3 %all-to-all-done = bf16[128,32,128]{2,0,1:T(8,128)(2,1)S(1)} async-done(((bf16[128,32,128]{2,0,1:T(8,128)(2,1)}), bf16[128,32,128]{2,0,1:T(8,128)(2,1)S(1)}, u32[]{:S(2)}, u32[]{:S(2)}) %all-to-all-start) | async-done | bytes 1048608 | tf_op jit(solution)/shard_map/all_to_all | solution.py:192
  81.0 1.0 copy-done
  82.0 21.3 %shard_map.82 = (f32[4096,128]{1,0:T(8,128)}, f32[4096,1]{1,0:T(8,128)}, f32[4096,1]{1,0:T(8,128)}) custom-call(s32[32]{0:T(128)} %bitcast.69, bf16[4096,128]{1,0:T(8,128)(2,1)} %bitcast.49, bf16[4096,256]{1,0:T(8,128)(2,1)} %all-gather.3.cloned.1.call-done.ckv_ref, f32[1,2048]{1,0:T(1,128)} %compare_select_fusion.vbias_ref), custom_call_target="tpu_custom_call" | custom-call | tf_op jit(solution)/shard_map/pallas_call | solution.py:113
  103.2 4.3 %all-gather.5.cloned.1.call-done.skv_ref = bf16[8,512,256]{2,1,0:T(8,128)(2,1)} async-done(((bf16[1,512,256]{2,1,0:T(8,128)(2,1)}), bf16[8,512,256]{2,1,0:T(8,128)(2,1)}) %all-gather.5.cloned.1.call-update) | async-done | bytes 2097168 | tf_op jit(solution)/shard_map/all_gather | solution.py:204
  107.5 12.2 %shard_map.84 = bf16[32,64,128]{2,1,0:T(8,128)(2,1)} custom-call(s32[768]{0:T(1024)} %mul.19.crow_ref, s32[768]{0:T(1024)} %get-tuple-element.12.splane_ref, s32[768]{0:T(1024)} %get-tuple-element.11.srow_ref, s32[768]{0:T(1024)} %reshape.136.pick_ref, bf16[32,2,64,128]{3,2,1,0:T(8,128)(2,1)} %bitcast.50, ...), custom_call_target="tpu_custom_call" | custom-call | tf_op jit(solution)/shard_map/pallas_call | solution.py:174
  119.7 6.5 %all-to-all-start.3 = ((bf16[32,64,1,128]{3,1,2,0:T(8,128)(2,1)}), bf16[32,64,1,128]{3,1,2,0:T(8,128)(2,1)S(1)}, u32[]{:S(2)}, u32[]{:S(2)}) async-start(bf16[32,64,1,128]{3,1,2,0:T(8,128)(2,1)} %bitcast.60), calls=%async_computation.3 | async-start | bytes 1048576 | tf_op jit(solution)/shard_map/all_to_all | solution.py:211
  126.3 12.2 %shard_map.83 = bf16[32,64,128]{2,1,0:T(8,128)(2,1)} custom-call(s32[768]{0:T(1024)} %mul.19.crow_ref, s32[768]{0:T(1024)} %get-tuple-element.12.splane_ref, s32[768]{0:T(1024)} %get-tuple-element.11.srow_ref, s32[768]{0:T(1024)} %reshape.136.pick_ref, bf16[32,2,64,128]{3,2,1,0:T(8,128)(2,1)} %bitcast.51, ...), custom_call_target="tpu_custom_call" | custom-call | tf_op jit(solution)/shard_map/pallas_call | solution.py:174
  138.5 1.7 all-to-all-done.3
  140.2 8.1 %all-to-all-start.2 = ((bf16[32,64,1,128]{3,1,2,0:T(8,128)(2,1)}), bf16[32,64,1,128]{3,1,2,0:T(8,128)(2,1)S(1)}, u32[]{:S(2)}, u32[]{:S(2)}) async-start(bf16[32,64,1,128]{3,1,2,0:T(8,128)(2,1)} %bitcast.59), calls=%async_computation.2 | async-start | bytes 1048576 | tf_op jit(solution)/shard_map/all_to_all | solution.py:211
  148.3 0.3 copy.40
  148.7 13.9 %all-to-all-done.2 = bf16[32,64,1,128]{3,1,2,0:T(8,128)(2,1)S(1)} async-done(((bf16[32,64,1,128]{3,1,2,0:T(8,128)(2,1)}), bf16[32,64,1,128]{3,1,2,0:T(8,128)(2,1)S(1)}, u32[]{:S(2)}, u32[]{:S(2)}) %all-to-all-start.2) | async-done | bytes 524320 | tf_op jit(solution)/shard_map/all_to_all | solution.py:211
  162.5 0.3 copy.37
  162.9 0.4 copy_bitcast_fusion
  163.3 1.1 maximum_bitcast_fusion
  (28 shorter events, 0.9 us)
Async XLA Ops:
  6.5 19.6 %copy-start.2 = (bf16[1,128,4096]{2,1,0:T(8,128)(2,1)S(1)}, bf16[1,128,4096]{2,1,0:T(8,128)(2,1)}, u32[]{:S(2)}) copy-start(bf16[1,128,4096]{2,1,0:T(8,128)(2,1)} %param.8) | copy-start | bytes 3145732
  6.5 74.4 %all-gather.3.cloned.1.call-start = ((), (), s32[]{:S(2)}) async-start(), calls=%async_computation.4 | async-start | bytes 2359296 | tf_op jit(solution)/shard_map/all_gather | solution.py:206
  8.4 99.1 %all-gather.5.cloned.1.call-start = ((), (), s32[]{:S(2)}) async-start(), calls=%async_computation.5 | async-start | bytes 2359296 | tf_op jit(solution)/shard_map/all_gather | solution.py:204
  8.4 4.6 %collective-permute-start.1 = (bf16[1,128,512]{2,1,0:T(8,128)(2,1)}, bf16[1,128,512]{2,1,0:T(8,128)(2,1)S(1)}, u32[]{:S(2)}, u32[]{:S(2)}) collective-permute-start(bf16[1,128,512]{2,1,0:T(8,128)(2,1)} %param.9), channel_id=1, source_target_pairs={{0,32},{32,64},{64,96},{96,128},{128,160},{160,192},{192,224},{224... | collective-permute-start | bytes 393224 | tf_op jit(solution)/shard_map/ppermute | solution.py:25
  8.5 6.0 %collective-permute-start.2 = (bf16[1,128,512]{2,1,0:T(8,128)(2,1)}, bf16[1,128,512]{2,1,0:T(8,128)(2,1)S(1)}, u32[]{:S(2)}, u32[]{:S(2)}) collective-permute-start(bf16[1,128,512]{2,1,0:T(8,128)(2,1)} %param.10), channel_id=1, source_target_pairs={{0,32},{32,64},{64,96},{96,128},{128,160},{160,192},{192,224},{224... | collective-permute-start | bytes 393224 | tf_op jit(solution)/shard_map/ppermute | solution.py:25
  26.1 14.2 %collective-permute-start = (bf16[1,128,4096]{2,1,0:T(8,128)(2,1)S(1)}, bf16[1,128,4096]{2,1,0:T(8,128)(2,1)S(1)}, u32[]{:S(2)}, u32[]{:S(2)}) collective-permute-start(bf16[1,128,4096]{2,1,0:T(8,128)(2,1)S(1)} %copy-done.2), channel_id=1, source_target_pairs={{0,32},{32,64},{64,96},{96,128},{128,160},{160,192},{192,224},{224... | collective-permute-start | bytes 3145736 | tf_op jit(solution)/shard_map/ppermute | solution.py:25
  40.6 13.4 %copy-start.3 = (s32[1,1,11]{2,1,0:T(1,128)S(1)}, s32[1,1,11]{2,1,0:T(1,128)}, u32[]{:S(2)}) copy-start(s32[1,1,11]{2,1,0:T(1,128)} %param.15) | copy-start | bytes 136
  40.6 14.4 %copy-start.1 = (s32[1,1,32]{2,1,0:T(1,128)S(1)}, s32[1,1,32]{2,1,0:T(1,128)}, u32[]{:S(2)}) copy-start(s32[1,1,32]{2,1,0:T(1,128)} %param.13) | copy-start | bytes 388
  42.0 38.9 %all-to-all-start = ((bf16[128,32,128]{2,0,1:T(8,128)(2,1)}), bf16[128,32,128]{2,0,1:T(8,128)(2,1)S(1)}, u32[]{:S(2)}, u32[]{:S(2)}) async-start(bf16[128,32,128]{2,0,1:T(8,128)(2,1)} %copy.31), calls=%async_computation | async-start | bytes 2097152 | tf_op jit(solution)/shard_map/all_to_all | solution.py:192
  81.0 1.0 copy-start
  119.7 20.5 %all-to-all-start.3 = ((bf16[32,64,1,128]{3,1,2,0:T(8,128)(2,1)}), bf16[32,64,1,128]{3,1,2,0:T(8,128)(2,1)S(1)}, u32[]{:S(2)}, u32[]{:S(2)}) async-start(bf16[32,64,1,128]{3,1,2,0:T(8,128)(2,1)} %bitcast.60), calls=%async_computation.3 | async-start | bytes 1048576 | tf_op jit(solution)/shard_map/all_to_all | solution.py:211
  140.2 22.3 %all-to-all-start.2 = ((bf16[32,64,1,128]{3,1,2,0:T(8,128)(2,1)}), bf16[32,64,1,128]{3,1,2,0:T(8,128)(2,1)S(1)}, u32[]{:S(2)}, u32[]{:S(2)}) async-start(bf16[32,64,1,128]{3,1,2,0:T(8,128)(2,1)} %bitcast.59), calls=%async_computation.2 | async-start | bytes 1048576 | tf_op jit(solution)/shard_map/all_to_all | solution.py:211
Sparse Core Ops, SparseCore 0:
  9.4 50.8 all-gather.2
  62.4 45.0 all-gather.4

commit v7 on v6

--- a/solution.py
+++ b/solution.py
@@ -181,17 +181,16 @@
 
 
 def per_device(queries, keys, values, cache_keys, cache_values, vertical, vertical_count, slash):
-    query_rows, key_rows, value_rows = from_behind((queries, keys, values), "section", 1)
-    tok = query_rows.shape[1]
+    key_rows, value_rows = from_behind((keys, values), "section", 1)
+    tok = queries.shape[1]
     nx = lax.axis_size("gx")
     nz = lax.axis_size("gz")
     heads = nx * nz
     kv_heads = key_rows.shape[2] // HEAD_SIZE
     prefill_stretch = tok * heads
-    q_rows = query_rows[0].reshape(tok, heads, HEAD_SIZE)
-    own_query = lax.all_to_all(
-        q_rows, ("gx", "gz"), split_axis=1, concat_axis=0, tiled=True
-    ).reshape(prefill_stretch, HEAD_SIZE)
+    q_rows = queries[0].reshape(tok, heads, HEAD_SIZE)
+    head_rows = lax.all_to_all(q_rows, ("gx", "gz"), split_axis=1, concat_axis=0, tiled=True)
+    own_query = from_behind(head_rows.reshape(prefill_stretch, HEAD_SIZE), "section", 1)
 
     kv_rows = jnp.concatenate(
         [

time: 172 us -> 186 us (1.081)
  the two profiles are of different devices: /device:TPU:24 before, /device:TPU:8 now
where the time goes in v7:
time: 186 us; the launch traced here: 185 us
  waiting for transfers between devices  76 us (41%)
  Pallas kernels  45.7 us (25%)
  starting transfers between devices  27.3 us (15%)
  between operations  14.2 us (8%)
  blocking collectives  10.9 us (6%)
  local copies, waits for them, and re-layouts  6.81 us (4%)
  other arithmetic  4.57 us (2%)
    all_to_all x1, waiting for transfers between devices, per_device(): lax.all_to_all(q_rows, ('gx', 'gz'), split_axis=1, concat_axis=0, tiled=T...  36.8 us
    pallas_call x2, Pallas kernels, head_attention(): pl.pallas_call(functools.partial(slash_kernel, parity=parity), grid_spec=...  24.5 us
    pallas_call x1, Pallas kernels, vertical_part(): pl.pallas_call(vertical_kernel, grid_spec=grid_spec, out_shape=[jax.Shape...  21.3 us
    all_to_all x2, waiting for transfers between devices, per_device(): lax.all_to_all(half[:, :, None, :], ('gx', 'gz'), split_axis=0, concat_ax...  16.3 us
    all_to_all x2, starting transfers between devices, per_device(): lax.all_to_all(half[:, :, None, :], ('gx', 'gz'), split_axis=0, concat_ax...  14.3 us
    ppermute x3, waiting for transfers between devices, from_behind(): return lax.ppermute(x, axis, [(i, (i + by) % peers) for i in range(peers)])  13.9 us
    all_to_all x1, starting transfers between devices, per_device(): lax.all_to_all(q_rows, ('gx', 'gz'), split_axis=1, concat_axis=0, tiled=T...  11.3 us
    all_to_all x1, blocking collectives, per_device(): lax.all_to_all(kv_rows, 'gx', split_axis=1, concat_axis=0, tiled=True)  10.9 us
  transfers between devices with their start and end apart: 8, of which 7 were waited for; matrix products, arithmetic and copies ran while one was open for 4% of the time, Pallas kernels for 18%

profile of v7, /device:TPU:8, one launch (start us, length us, event | category | flops | bytes accessed | tf_op | source)
XLA Modules:
  0.0 185.5 jit_solution(7356050734465770875)
XLA Ops:
  6.5 1.8 pad_maximum_fusion
  8.5 1.7 collective-permute-start.2
  10.1 2.9 %collective-permute-done.1 = bf16[1,128,512]{2,1,0:T(8,128)(2,1)S(1)} collective-permute-done((bf16[1,128,512]{2,1,0:T(8,128)(2,1)}, bf16[1,128,512]{2,1,0:T(8,128)(2,1)S(1)}, u32[]{:S(2)}, u32[]{:S(2)}) %collective-permute-start.1) | collective-permute-done | bytes 131104 | tf_op jit(solution)/shard_map/ppermute | solution.py:25
  13.1 1.3 collective-permute-done.2
  14.6 10.9 %all_to_all.60 = bf16[128,4,256]{2,0,1:T(8,128)(2,1)} all-to-all(bf16[128,4,256]{2,0,1:T(8,128)(2,1)S(1)} %pad_maximum_fusion.1), channel_id=1, replica_groups=mesh['section'=16,'gx'=4,'gz'=8] {'gx'}, dimensions={1} | all-to-all | bytes 524288 | tf_op jit(solution)/shard_map/all_to_all | solution.py:202
  25.5 0.2 copy.41
  25.7 1.4 copy.31
  27.1 11.3 %all-to-all-start = ((bf16[128,32,128]{2,0,1:T(8,128)(2,1)}), bf16[128,32,128]{2,0,1:T(8,128)(2,1)S(1)}, u32[]{:S(2)}, u32[]{:S(2)}) async-start(bf16[128,32,128]{2,0,1:T(8,128)(2,1)} %copy.31), calls=%async_computation | async-start | bytes 2097152 | tf_op jit(solution)/shard_map/all_to_all | solution.py:192
  39.3 36.8 %all-to-all-done = bf16[128,32,128]{2,0,1:T(8,128)(2,1)S(1)} async-done(((bf16[128,32,128]{2,0,1:T(8,128)(2,1)}), bf16[128,32,128]{2,0,1:T(8,128)(2,1)S(1)}, u32[]{:S(2)}, u32[]{:S(2)}) %all-to-all-start) | async-done | bytes 1048608 | tf_op jit(solution)/shard_map/all_to_all | solution.py:192
  76.1 0.7 reshape.139.pick_ref
  76.9 0.1 and_reduce_fusion
  77.1 0.1 copy.34
  77.3 0.1 min.17
  77.5 0.7 mul.19.crow_ref
  78.2 0.2 broadcast_in_dim.31
  78.4 0.9 reshape_reshape_reshape.4.sbias_ref
  79.4 0.6 compare_select_fusion.vbias_ref
  80.0 0.6 fusion.6
  80.6 9.7 %collective-permute-done.q_ref = bf16[4096,128]{1,0:T(8,128)(2,1)S(1)} collective-permute-done((bf16[4096,128]{1,0:T(8,128)(2,1)S(1)}, bf16[4096,128]{1,0:T(8,128)(2,1)S(1)}, u32[]{:S(2)}, u32[]{:S(2)}) %collective-permute-start) | collective-permute-done | bytes 1048608 | tf_op jit(solution)/shard_map/ppermute | solution.py:25
  90.3 1.0 copy-done
  91.2 21.3 %shard_map.82 = (f32[4096,128]{1,0:T(8,128)}, f32[4096,1]{1,0:T(8,128)}, f32[4096,1]{1,0:T(8,128)}) custom-call(s32[32]{0:T(128)} %bitcast.68, bf16[4096,128]{1,0:T(8,128)(2,1)} %copy-done, bf16[4096,256]{1,0:T(8,128)(2,1)} %all-gather.3.cloned.1.call-done.ckv_ref, f32[1,2048]{1,0:T(1,128)} %compare_select_fusion.vbias_ref), custom_call_target="tpu_custom_call" | custom-call | tf_op jit(solution)/shard_map/pallas_call | solution.py:113
  112.5 8.9 %all-gather.5.cloned.1.call-done.skv_ref = bf16[8,512,256]{2,1,0:T(8,128)(2,1)} async-done(((bf16[1,512,256]{2,1,0:T(8,128)(2,1)}), bf16[8,512,256]{2,1,0:T(8,128)(2,1)}) %all-gather.5.cloned.1.call-update) | async-done | bytes 2097168 | tf_op jit(solution)/shard_map/all_gather | solution.py:203
  121.4 12.2 %shard_map.84 = bf16[32,64,128]{2,1,0:T(8,128)(2,1)} custom-call(s32[768]{0:T(1024)} %mul.19.crow_ref, s32[768]{0:T(1024)} %get-tuple-element.12.splane_ref, s32[768]{0:T(1024)} %get-tuple-element.11.srow_ref, s32[768]{0:T(1024)} %reshape.139.pick_ref, bf16[32,2,64,128]{3,2,1,0:T(8,128)(2,1)} %bitcast.48, ...), custom_call_target="tpu_custom_call" | custom-call | tf_op jit(solution)/shard_map/pallas_call | solution.py:174
  133.6 6.9 %all-to-all-start.3 = ((bf16[32,64,1,128]{3,1,2,0:T(8,128)(2,1)}), bf16[32,64,1,128]{3,1,2,0:T(8,128)(2,1)S(1)}, u32[]{:S(2)}, u32[]{:S(2)}) async-start(bf16[32,64,1,128]{3,1,2,0:T(8,128)(2,1)} %bitcast.58), calls=%async_computation.3 | async-start | bytes 1048576 | tf_op jit(solution)/shard_map/all_to_all | solution.py:210
  140.5 12.3 %shard_map.83 = bf16[32,64,128]{2,1,0:T(8,128)(2,1)} custom-call(s32[768]{0:T(1024)} %mul.19.crow_ref, s32[768]{0:T(1024)} %get-tuple-element.12.splane_ref, s32[768]{0:T(1024)} %get-tuple-element.11.srow_ref, s32[768]{0:T(1024)} %reshape.139.pick_ref, bf16[32,2,64,128]{3,2,1,0:T(8,128)(2,1)} %bitcast.49, ...), custom_call_target="tpu_custom_call" | custom-call | tf_op jit(solution)/shard_map/pallas_call | solution.py:174
  152.8 2.4 %all-to-all-done.3 = bf16[32,64,1,128]{3,1,2,0:T(8,128)(2,1)S(1)} async-done(((bf16[32,64,1,128]{3,1,2,0:T(8,128)(2,1)}), bf16[32,64,1,128]{3,1,2,0:T(8,128)(2,1)S(1)}, u32[]{:S(2)}, u32[]{:S(2)}) %all-to-all-start.3) | async-done | bytes 524320 | tf_op jit(solution)/shard_map/all_to_all | solution.py:210
  155.2 7.4 %all-to-all-start.2 = ((bf16[32,64,1,128]{3,1,2,0:T(8,128)(2,1)}), bf16[32,64,1,128]{3,1,2,0:T(8,128)(2,1)S(1)}, u32[]{:S(2)}, u32[]{:S(2)}) async-start(bf16[32,64,1,128]{3,1,2,0:T(8,128)(2,1)} %bitcast.57), calls=%async_computation.2 | async-start | bytes 1048576 | tf_op jit(solution)/shard_map/all_to_all | solution.py:210
  162.6 0.3 copy.40
  162.9 13.9 %all-to-all-done.2 = bf16[32,64,1,128]{3,1,2,0:T(8,128)(2,1)S(1)} async-done(((bf16[32,64,1,128]{3,1,2,0:T(8,128)(2,1)}), bf16[32,64,1,128]{3,1,2,0:T(8,128)(2,1)S(1)}, u32[]{:S(2)}, u32[]{:S(2)}) %all-to-all-start.2) | async-done | bytes 524320 | tf_op jit(solution)/shard_map/all_to_all | solution.py:210
  176.8 0.3 copy.37
  177.2 0.4 copy_bitcast_fusion
  177.6 1.1 maximum_bitcast_fusion
  (28 shorter events, 0.9 us)
Async XLA Ops:
  6.5 18.9 %copy-start.1 = (bf16[1,128,4096]{2,1,0:T(8,128)(2,1)S(1)}, bf16[1,128,4096]{2,1,0:T(8,128)(2,1)}, u32[]{:S(2)}) copy-start(bf16[1,128,4096]{2,1,0:T(8,128)(2,1)} %param.8) | copy-start | bytes 3145732
  6.5 83.7 %all-gather.3.cloned.1.call-start = ((), (), s32[]{:S(2)}) async-start(), calls=%async_computation.4 | async-start | bytes 2359296 | tf_op jit(solution)/shard_map/all_gather | solution.py:205
  8.4 113.0 %all-gather.5.cloned.1.call-start = ((), (), s32[]{:S(2)}) async-start(), calls=%async_computation.5 | async-start | bytes 2359296 | tf_op jit(solution)/shard_map/all_gather | solution.py:203
  8.4 4.6 %collective-permute-start.1 = (bf16[1,128,512]{2,1,0:T(8,128)(2,1)}, bf16[1,128,512]{2,1,0:T(8,128)(2,1)S(1)}, u32[]{:S(2)}, u32[]{:S(2)}) collective-permute-start(bf16[1,128,512]{2,1,0:T(8,128)(2,1)} %param.9), channel_id=1, source_target_pairs={{0,32},{32,64},{64,96},{96,128},{128,160},{160,192},{192,224},{224... | collective-permute-start | bytes 393224 | tf_op jit(solution)/shard_map/ppermute | solution.py:25
  8.5 6.0 %collective-permute-start.2 = (bf16[1,128,512]{2,1,0:T(8,128)(2,1)}, bf16[1,128,512]{2,1,0:T(8,128)(2,1)S(1)}, u32[]{:S(2)}, u32[]{:S(2)}) collective-permute-start(bf16[1,128,512]{2,1,0:T(8,128)(2,1)} %param.10), channel_id=1, source_target_pairs={{0,32},{32,64},{64,96},{96,128},{128,160},{160,192},{192,224},{224... | collective-permute-start | bytes 393224 | tf_op jit(solution)/shard_map/ppermute | solution.py:25
  25.7 13.4 %copy-start.3 = (s32[1,1,11]{2,1,0:T(1,128)S(1)}, s32[1,1,11]{2,1,0:T(1,128)}, u32[]{:S(2)}) copy-start(s32[1,1,11]{2,1,0:T(1,128)} %param.15) | copy-start | bytes 136
  25.7 51.2 %copy-start.2 = (s32[1,1,32]{2,1,0:T(1,128)S(1)}, s32[1,1,32]{2,1,0:T(1,128)}, u32[]{:S(2)}) copy-start(s32[1,1,32]{2,1,0:T(1,128)} %param.13) | copy-start | bytes 388
  27.1 48.9 %all-to-all-start = ((bf16[128,32,128]{2,0,1:T(8,128)(2,1)}), bf16[128,32,128]{2,0,1:T(8,128)(2,1)S(1)}, u32[]{:S(2)}, u32[]{:S(2)}) async-start(bf16[128,32,128]{2,0,1:T(8,128)(2,1)} %copy.31), calls=%async_computation | async-start | bytes 2097152 | tf_op jit(solution)/shard_map/all_to_all | solution.py:192
  76.0 14.2 %collective-permute-start = (bf16[4096,128]{1,0:T(8,128)(2,1)S(1)}, bf16[4096,128]{1,0:T(8,128)(2,1)S(1)}, u32[]{:S(2)}, u32[]{:S(2)}) collective-permute-start(bf16[4096,128]{1,0:T(8,128)(2,1)S(1)} %bitcast.64), channel_id=1, source_target_pairs={{0,32},{32,64},{64,96},{96,128},{128,160},{160,192},{192,224},{224... | collective-permute-start | bytes 3145736 | tf_op jit(solution)/shard_map/ppermute | solution.py:25
  90.3 1.0 copy-start
  133.6 21.6 %all-to-all-start.3 = ((bf16[32,64,1,128]{3,1,2,0:T(8,128)(2,1)}), bf16[32,64,1,128]{3,1,2,0:T(8,128)(2,1)S(1)}, u32[]{:S(2)}, u32[]{:S(2)}) async-start(bf16[32,64,1,128]{3,1,2,0:T(8,128)(2,1)} %bitcast.58), calls=%async_computation.3 | async-start | bytes 1048576 | tf_op jit(solution)/shard_map/all_to_all | solution.py:210
  155.2 21.6 %all-to-all-start.2 = ((bf16[32,64,1,128]{3,1,2,0:T(8,128)(2,1)}), bf16[32,64,1,128]{3,1,2,0:T(8,128)(2,1)S(1)}, u32[]{:S(2)}, u32[]{:S(2)}) async-start(bf16[32,64,1,128]{3,1,2,0:T(8,128)(2,1)} %bitcast.57), calls=%async_computation.2 | async-start | bytes 1048576 | tf_op jit(solution)/shard_map/all_to_all | solution.py:210
Sparse Core Ops, SparseCore 0:
  9.4 66.9 all-gather.2
  78.5 42.8 all-gather.4

commit v8 on v7

--- a/solution.py
+++ b/solution.py
@@ -202,7 +202,9 @@
     part = lax.all_to_all(kv_rows, "gx", split_axis=1, concat_axis=0, tiled=True)
     skv = lax.all_gather(part.reshape(nx * tok, 2 * HEAD_SIZE), "gz", axis=0, tiled=False)
     cache_part = jnp.concatenate([cache_keys[0, 0], cache_values[0, 0]], axis=1)
-    ckv = lax.all_gather(cache_part, "gz", axis=0, tiled=True)
+    copies = jnp.broadcast_to(cache_part[None], (nz,) + cache_part.shape)
+    ckv = lax.all_to_all(copies, "gz", split_axis=0, concat_axis=0, tiled=True).reshape(
+        nz * cache_part.shape[0], 2 * HEAD_SIZE)
     halves = head_attention(own_query, ckv, skv, vertical[0, 0], vertical_count[0, 0],
                             slash[0, 0], tok)
     pieces = []

time: 186 us -> 222 us (1.19)
  the two profiles are of different devices: /device:TPU:8 before, /device:TPU:88 now
where the time goes in v8:
time: 222 us; the launch traced here: 221 us
  waiting for transfers between devices  112 us (50%)
  Pallas kernels  45.7 us (21%)
  starting transfers between devices  35 us (16%)
  between operations  14.2 us (6%)
  local copies, waits for them, and re-layouts  10.6 us (5%)
  other arithmetic  3.5 us (2%)
    all_to_all x1, waiting for transfers between devices, per_device(): lax.all_to_all(copies, 'gz', split_axis=0, concat_axis=0, tiled=True)  46.1 us
    all_to_all x1, waiting for transfers between devices, per_device(): lax.all_to_all(q_rows, ('gx', 'gz'), split_axis=1, concat_axis=0, tiled=T...  28.1 us
    pallas_call x2, Pallas kernels, head_attention(): pl.pallas_call(functools.partial(slash_kernel, parity=parity), grid_spec=...  24.5 us
    pallas_call x1, Pallas kernels, vertical_part(): pl.pallas_call(vertical_kernel, grid_spec=grid_spec, out_shape=[jax.Shape...  21.3 us
    all_to_all x2, waiting for transfers between devices, per_device(): lax.all_to_all(half[:, :, None, :], ('gx', 'gz'), split_axis=0, concat_ax...  19.9 us
    all_to_all x2, starting transfers between devices, per_device(): lax.all_to_all(half[:, :, None, :], ('gx', 'gz'), split_axis=0, concat_ax...  13.1 us
    ppermute x3, waiting for transfers between devices, from_behind(): return lax.ppermute(x, axis, [(i, (i + by) % peers) for i in range(peers)])  11.1 us
    all_to_all x1, starting transfers between devices, per_device(): lax.all_to_all(q_rows, ('gx', 'gz'), split_axis=1, concat_axis=0, tiled=T...  10.7 us
  transfers between devices with their start and end apart: 9, of which 8 were waited for; matrix products, arithmetic and copies ran while one was open for 4% of the time, Pallas kernels for 15%

profile of v8, /device:TPU:88, one launch (start us, length us, event | category | flops | bytes accessed | tf_op | source)
XLA Modules:
  0.0 220.7 jit_solution(4094466467196469493)
XLA Ops:
  6.5 2.9 %collective-permute-start.2 = (bf16[1,128,512]{2,1,0:T(8,128)(2,1)}, bf16[1,128,512]{2,1,0:T(8,128)(2,1)S(1)}, u32[]{:S(2)}, u32[]{:S(2)}) collective-permute-start(bf16[1,128,512]{2,1,0:T(8,128)(2,1)} %param.10), channel_id=1, source_target_pairs={{0,32},{32,64},{64,96},{96,128},{128,160},{160,192},{192,224},{224... | collective-permute-start | bytes 393224 | tf_op jit(solution)/shard_map/ppermute | solution.py:25
  9.4 1.7 collective-permute-done.1
  11.2 1.3 collective-permute-done.2
  12.6 0.7 pad_maximum_fusion.1
  13.4 4.3 %all-to-all-start.2 = ((bf16[128,4,256]{2,0,1:T(8,128)(2,1)}), bf16[128,4,256]{2,0,1:T(8,128)(2,1)S(1)}, u32[]{:S(2)}, u32[]{:S(2)}) async-start(bf16[128,4,256]{2,0,1:T(8,128)(2,1)} %pad_maximum_fusion.1), calls=%async_computation.2 | async-start | bytes 524288 | tf_op jit(solution)/shard_map/all_to_all | solution.py:202
  17.9 1.4 copy.31
  19.3 5.7 %all-to-all-done.2 = bf16[128,4,256]{2,0,1:T(8,128)(2,1)S(1)} async-done(((bf16[128,4,256]{2,0,1:T(8,128)(2,1)}), bf16[128,4,256]{2,0,1:T(8,128)(2,1)S(1)}, u32[]{:S(2)}, u32[]{:S(2)}) %all-to-all-start.2) | async-done | bytes 262176 | tf_op jit(solution)/shard_map/all_to_all | solution.py:202
  25.0 10.7 %all-to-all-start = ((bf16[128,32,128]{2,0,1:T(8,128)(2,1)}), bf16[128,32,128]{2,0,1:T(8,128)(2,1)S(1)}, u32[]{:S(2)}, u32[]{:S(2)}) async-start(bf16[128,32,128]{2,0,1:T(8,128)(2,1)} %copy.31), calls=%async_computation | async-start | bytes 2097152 | tf_op jit(solution)/shard_map/all_to_all | solution.py:192
  35.8 28.1 %all-to-all-done = bf16[128,32,128]{2,0,1:T(8,128)(2,1)S(1)} async-done(((bf16[128,32,128]{2,0,1:T(8,128)(2,1)}), bf16[128,32,128]{2,0,1:T(8,128)(2,1)S(1)}, u32[]{:S(2)}, u32[]{:S(2)}) %all-to-all-start) | async-done | bytes 1048608 | tf_op jit(solution)/shard_map/all_to_all | solution.py:192
  63.9 1.6 broadcast_in_dim.35
  65.5 4.0 %all-to-all-start.1 = ((bf16[8,512,256]{2,1,0:T(8,128)(2,1)}), bf16[8,512,256]{2,1,0:T(8,128)(2,1)S(1)}, u32[]{:S(2)}, u32[]{:S(2)}) async-start(bf16[8,512,256]{2,1,0:T(8,128)(2,1)} %broadcast_in_dim.35), calls=%async_computation.1 | async-start | bytes 4194304 | tf_op jit(solution)/shard_map/all_to_all | solution.py:206
  69.6 0.7 all-gather.2.cloned.1.call-update
  71.2 0.7 reshape.144.pick_ref
  72.6 0.7 mul.19.crow_ref
  73.3 1.0 broadcast_in_dim.38
  74.3 2.0 reshape_reshape_reshape.4.sbias_ref
  76.2 0.6 compare_select_fusion.vbias_ref
  76.9 0.6 fusion.6
  77.5 8.1 %collective-permute-done.q_ref = bf16[4096,128]{1,0:T(8,128)(2,1)S(1)} collective-permute-done((bf16[4096,128]{1,0:T(8,128)(2,1)}, bf16[4096,128]{1,0:T(8,128)(2,1)S(1)}, u32[]{:S(2)}, u32[]{:S(2)}) %collective-permute-start) | collective-permute-done | bytes 1048608 | tf_op jit(solution)/shard_map/ppermute | solution.py:25
  85.5 46.1 %all-to-all-done.1 = bf16[8,512,256]{2,1,0:T(8,128)(2,1)S(1)} async-done(((bf16[8,512,256]{2,1,0:T(8,128)(2,1)}), bf16[8,512,256]{2,1,0:T(8,128)(2,1)S(1)}, u32[]{:S(2)}, u32[]{:S(2)}) %all-to-all-start.1) | async-done | bytes 2097184 | tf_op jit(solution)/shard_map/all_to_all | solution.py:206
  131.7 1.3 copy-done
  133.0 21.3 %shard_map.82 = (f32[4096,128]{1,0:T(8,128)}, f32[4096,1]{1,0:T(8,128)}, f32[4096,1]{1,0:T(8,128)}) custom-call(s32[32]{0:T(128)} %bitcast.72, bf16[4096,128]{1,0:T(8,128)(2,1)} %copy-done.1, bf16[4096,256]{1,0:T(8,128)(2,1)} %bitcast.49, f32[1,2048]{1,0:T(1,128)} %compare_select_fusion.vbias_ref), custom_call_target="tpu_custom_call" | custom-call | tf_op jit(solution)/shard_map/pallas_call | solution.py:113
  154.2 12.2 %shard_map.84 = bf16[32,64,128]{2,1,0:T(8,128)(2,1)} custom-call(s32[768]{0:T(1024)} %mul.19.crow_ref, s32[768]{0:T(1024)} %get-tuple-element.12.splane_ref, s32[768]{0:T(1024)} %get-tuple-element.11.srow_ref, s32[768]{0:T(1024)} %reshape.144.pick_ref, bf16[32,2,64,128]{3,2,1,0:T(8,128)(2,1)} %bitcast.52, bf16[4096,256]{1,0:T(8,128)(2,1)} %bitcast.50, ...), custom_call_target="tpu_custom_call" | custom-call | tf_op jit(solution)/shard_map/pallas_call | solution.py:174
  166.4 7.6 %all-to-all-start.4 = ((bf16[32,64,1,128]{3,1,2,0:T(8,128)(2,1)}), bf16[32,64,1,128]{3,1,2,0:T(8,128)(2,1)S(1)}, u32[]{:S(2)}, u32[]{:S(2)}) async-start(bf16[32,64,1,128]{3,1,2,0:T(8,128)(2,1)} %bitcast.62), calls=%async_computation.4 | async-start | bytes 1048576 | tf_op jit(solution)/shard_map/all_to_all | solution.py:212
  174.0 12.3 %shard_map.83 = bf16[32,64,128]{2,1,0:T(8,128)(2,1)} custom-call(s32[768]{0:T(1024)} %mul.19.crow_ref, s32[768]{0:T(1024)} %get-tuple-element.12.splane_ref, s32[768]{0:T(1024)} %get-tuple-element.11.srow_ref, s32[768]{0:T(1024)} %reshape.144.pick_ref, bf16[32,2,64,128]{3,2,1,0:T(8,128)(2,1)} %bitcast.53, bf16[4096,256]{1,0:T(8,128)(2,1)} %bitcast.51, ...), custom_call_target="tpu_custom_call" | custom-call | tf_op jit(solution)/shard_map/pallas_call | solution.py:174
  186.3 4.3 %all-to-all-done.4 = bf16[32,64,1,128]{3,1,2,0:T(8,128)(2,1)S(1)} async-done(((bf16[32,64,1,128]{3,1,2,0:T(8,128)(2,1)}), bf16[32,64,1,128]{3,1,2,0:T(8,128)(2,1)S(1)}, u32[]{:S(2)}, u32[]{:S(2)}) %all-to-all-start.4) | async-done | bytes 524320 | tf_op jit(solution)/shard_map/all_to_all | solution.py:212
  190.6 5.5 %all-to-all-start.3 = ((bf16[32,64,1,128]{3,1,2,0:T(8,128)(2,1)}), bf16[32,64,1,128]{3,1,2,0:T(8,128)(2,1)S(1)}, u32[]{:S(2)}, u32[]{:S(2)}) async-start(bf16[32,64,1,128]{3,1,2,0:T(8,128)(2,1)} %bitcast.61), calls=%async_computation.3 | async-start | bytes 1048576 | tf_op jit(solution)/shard_map/all_to_all | solution.py:212
  196.1 0.3 copy.40
  196.4 15.6 %all-to-all-done.3 = bf16[32,64,1,128]{3,1,2,0:T(8,128)(2,1)S(1)} async-done(((bf16[32,64,1,128]{3,1,2,0:T(8,128)(2,1)}), bf16[32,64,1,128]{3,1,2,0:T(8,128)(2,1)S(1)}, u32[]{:S(2)}, u32[]{:S(2)}) %all-to-all-start.3) | async-done | bytes 524320 | tf_op jit(solution)/shard_map/all_to_all | solution.py:212
  212.1 0.3 copy.37
  212.4 0.4 copy_bitcast_fusion
  212.8 1.1 maximum_bitcast_fusion
  (39 shorter events, 1.4 us)
Async XLA Ops:
  6.5 11.1 %copy-start.2 = (bf16[1,128,4096]{2,1,0:T(8,128)(2,1)S(1)}, bf16[1,128,4096]{2,1,0:T(8,128)(2,1)}, u32[]{:S(2)}) copy-start(bf16[1,128,4096]{2,1,0:T(8,128)(2,1)} %param.8) | copy-start | bytes 3145732
  6.5 4.6 %collective-permute-start.1 = (bf16[1,128,512]{2,1,0:T(8,128)(2,1)}, bf16[1,128,512]{2,1,0:T(8,128)(2,1)S(1)}, u32[]{:S(2)}, u32[]{:S(2)}) collective-permute-start(bf16[1,128,512]{2,1,0:T(8,128)(2,1)} %param.9), channel_id=1, source_target_pairs={{0,32},{32,64},{64,96},{96,128},{128,160},{160,192},{192,224},{224... | collective-permute-start | bytes 393224 | tf_op jit(solution)/shard_map/ppermute | solution.py:25
  6.5 6.0 %collective-permute-start.2 = (bf16[1,128,512]{2,1,0:T(8,128)(2,1)}, bf16[1,128,512]{2,1,0:T(8,128)(2,1)S(1)}, u32[]{:S(2)}, u32[]{:S(2)}) collective-permute-start(bf16[1,128,512]{2,1,0:T(8,128)(2,1)} %param.10), channel_id=1, source_target_pairs={{0,32},{32,64},{64,96},{96,128},{128,160},{160,192},{192,224},{224... | collective-permute-start | bytes 393224 | tf_op jit(solution)/shard_map/ppermute | solution.py:25
  13.4 11.7 %all-to-all-start.2 = ((bf16[128,4,256]{2,0,1:T(8,128)(2,1)}), bf16[128,4,256]{2,0,1:T(8,128)(2,1)S(1)}, u32[]{:S(2)}, u32[]{:S(2)}) async-start(bf16[128,4,256]{2,0,1:T(8,128)(2,1)} %pad_maximum_fusion.1), calls=%async_computation.2 | async-start | bytes 524288 | tf_op jit(solution)/shard_map/all_to_all | solution.py:202
  17.9 17.8 %copy-start.5 = (bf16[1,1,512,128]{3,2,1,0:T(8,128)(2,1)S(1)}, bf16[1,1,512,128]{3,2,1,0:T(8,128)(2,1)}, u32[]{:S(2)}) copy-start(bf16[1,1,512,128]{3,2,1,0:T(8,128)(2,1)} %param.12) | copy-start | bytes 393220
  17.9 17.8 %copy-start.6 = (bf16[1,1,512,128]{3,2,1,0:T(8,128)(2,1)S(1)}, bf16[1,1,512,128]{3,2,1,0:T(8,128)(2,1)}, u32[]{:S(2)}) copy-start(bf16[1,1,512,128]{3,2,1,0:T(8,128)(2,1)} %param.11) | copy-start | bytes 393220
  25.0 40.4 %copy-start.4 = (bf16[128,4,256]{2,0,1:T(8,128)(2,1)}, bf16[128,4,256]{2,0,1:T(8,128)(2,1)S(1)}, u32[]{:S(2)}) copy-start(bf16[128,4,256]{2,0,1:T(8,128)(2,1)S(1)} %all-to-all-done.2) | copy-start | bytes 786436
  25.0 38.9 %all-to-all-start = ((bf16[128,32,128]{2,0,1:T(8,128)(2,1)}), bf16[128,32,128]{2,0,1:T(8,128)(2,1)S(1)}, u32[]{:S(2)}, u32[]{:S(2)}) async-start(bf16[128,32,128]{2,0,1:T(8,128)(2,1)} %copy.31), calls=%async_computation | async-start | bytes 2097152 | tf_op jit(solution)/shard_map/all_to_all | solution.py:192
  63.9 1.7 copy-start.3
  65.4 5.5 %copy-start.8 = (s32[1,1,11]{2,1,0:T(1,128)S(1)}, s32[1,1,11]{2,1,0:T(1,128)}, u32[]{:S(2)}) copy-start(s32[1,1,11]{2,1,0:T(1,128)} %param.15) | copy-start | bytes 136
  65.4 6.5 %copy-start.7 = (s32[1,1,32]{2,1,0:T(1,128)S(1)}, s32[1,1,32]{2,1,0:T(1,128)}, u32[]{:S(2)}) copy-start(s32[1,1,32]{2,1,0:T(1,128)} %param.13) | copy-start | bytes 388
  65.5 66.1 %all-to-all-start.1 = ((bf16[8,512,256]{2,1,0:T(8,128)(2,1)}), bf16[8,512,256]{2,1,0:T(8,128)(2,1)S(1)}, u32[]{:S(2)}, u32[]{:S(2)}) async-start(bf16[8,512,256]{2,1,0:T(8,128)(2,1)} %broadcast_in_dim.35), calls=%async_computation.1 | async-start | bytes 4194304 | tf_op jit(solution)/shard_map/all_to_all | solution.py:206
  69.6 84.7 %all-gather.2.cloned.1.call-start = ((), (), s32[]{:S(2)}) async-start(), calls=%async_computation.5 | async-start | bytes 2359296 | tf_op jit(solution)/shard_map/all_gather | solution.py:203
  71.1 14.4 %collective-permute-start = (bf16[4096,128]{1,0:T(8,128)(2,1)}, bf16[4096,128]{1,0:T(8,128)(2,1)S(1)}, u32[]{:S(2)}, u32[]{:S(2)}) collective-permute-start(bf16[4096,128]{1,0:T(8,128)(2,1)} %bitcast.68), channel_id=1, source_target_pairs={{0,32},{32,64},{64,96},{96,128},{128,160},{160,192},{192,224},{224... | collective-permute-start | bytes 3145736 | tf_op jit(solution)/shard_map/ppermute | solution.py:25
  85.5 46.1 %copy-start.1 = (bf16[4096,128]{1,0:T(8,128)(2,1)}, bf16[4096,128]{1,0:T(8,128)(2,1)S(1)}, u32[]{:S(2)}) copy-start(bf16[4096,128]{1,0:T(8,128)(2,1)S(1)} %collective-permute-done.q_ref) | copy-start | bytes 3145732
  131.7 1.3 copy-start
  166.4 24.1 %all-to-all-start.4 = ((bf16[32,64,1,128]{3,1,2,0:T(8,128)(2,1)}), bf16[32,64,1,128]{3,1,2,0:T(8,128)(2,1)S(1)}, u32[]{:S(2)}, u32[]{:S(2)}) async-start(bf16[32,64,1,128]{3,1,2,0:T(8,128)(2,1)} %bitcast.62), calls=%async_computation.4 | async-start | bytes 1048576 | tf_op jit(solution)/shard_map/all_to_all | solution.py:212
  190.6 21.5 %all-to-all-start.3 = ((bf16[32,64,1,128]{3,1,2,0:T(8,128)(2,1)}), bf16[32,64,1,128]{3,1,2,0:T(8,128)(2,1)S(1)}, u32[]{:S(2)}, u32[]{:S(2)}) async-start(bf16[32,64,1,128]{3,1,2,0:T(8,128)(2,1)} %bitcast.61), calls=%async_computation.3 | async-start | bytes 1048576 | tf_op jit(solution)/shard_map/all_to_all | solution.py:212
Sparse Core Ops, SparseCore 0:
  72.5 64.5 all-gather.1

commit v9 on v6

--- a/solution.py
+++ b/solution.py
@@ -16,6 +16,7 @@
 NS = 11
 CACHE = 4096
 TQ = 256
+STQ = 512
 
 big_negative = -1e30
 
@@ -53,7 +54,7 @@
 
 def slash_kernel(crow_ref, splane_ref, srow_ref, pick_ref, q_ref, ckv_ref, skv_ref, sbias_ref,
                  acc_ref, top_ref, total_ref, o_ref, kslash, causal_bias, *, parity):
-    nb = TQ // BLK
+    nb = STQ // BLK
     nd = NS + 1
     width = nd * BLK
     tile = pl.program_id(0)
@@ -143,7 +144,7 @@
     srow = ((dev // nz) * tok + (stretch_blk % per_dev) * BLK).reshape(-1)
     sbias = jnp.repeat(jnp.where(valid, 0.0, big_negative).astype(jnp.float32), BLK,
                        axis=1).reshape(nqb, 1, nd * BLK)
-    nb = TQ // BLK
+    nb = STQ // BLK
     width = nd * BLK
     halves = nqb // 2
     q4 = own_query.reshape(halves, 2, BLK, HEAD_SIZE)

time: 172 us -> 169 us (0.983)
  Pallas kernels: 45.7 us -> 43.2 us
    pallas_call x2, Pallas kernels: 24.5 us -> 22 us  [head_attention(): pl.pallas_call(functools.partial(slash_kernel, parity=parity), grid_spec=...]
  transfers between devices with their start and end apart: 8 -> 8, of which waited for: 7 -> 7; matrix products, arithmetic and copies ran while one was open for 4% -> 4% of each run, Pallas kernels for 20% -> 19%
where the time goes in v9:
time: 169 us
  waiting for transfers between devices  60.7 us (36%)
  Pallas kernels  43.2 us (26%)
  starting transfers between devices  27.6 us (16%)
  between operations  14.2 us (8%)
  blocking collectives  11.6 us (7%)
  local copies, waits for them, and re-layouts  6.81 us (4%)
  other arithmetic  4.57 us (3%)
    all_to_all x1, waiting for transfers between devices, per_device(): lax.all_to_all(q_rows, ('gx', 'gz'), split_axis=1, concat_axis=0, tiled=T...  22.3 us
    pallas_call x2, Pallas kernels, head_attention(): pl.pallas_call(functools.partial(slash_kernel, parity=parity), grid_spec=...  22 us
    pallas_call x1, Pallas kernels, vertical_part(): pl.pallas_call(vertical_kernel, grid_spec=grid_spec, out_shape=[jax.Shape...  21.3 us
    ppermute x3, waiting for transfers between devices, from_behind(): return lax.ppermute(x, axis, [(i, (i + by) % peers) for i in range(peers)])  17.2 us
    all_to_all x2, waiting for transfers between devices, per_device(): lax.all_to_all(half[:, :, None, :], ('gx', 'gz'), split_axis=0, concat_ax...  16.8 us
    all_to_all x2, starting transfers between devices, per_device(): lax.all_to_all(half[:, :, None, :], ('gx', 'gz'), split_axis=0, concat_ax...  13.4 us
    all_to_all x1, blocking collectives, per_device(): lax.all_to_all(kv_rows, 'gx', split_axis=1, concat_axis=0, tiled=True)  11.6 us
    all_to_all x1, starting transfers between devices, per_device(): lax.all_to_all(q_rows, ('gx', 'gz'), split_axis=1, concat_axis=0, tiled=T...  11.3 us
  transfers between devices with their start and end apart: 8, of which 7 were waited for; matrix products, arithmetic and copies ran while one was open for 4% of the time, Pallas kernels for 19%

profile of v9, /device:TPU:24, one launch (start us, length us, event | category | flops | bytes accessed | tf_op | source)
XLA Modules:
  0.0 168.7 jit_solution(53894112277577518)
XLA Ops:
  6.5 1.8 %pad_maximum_fusion = bf16[512,256]{1,0:T(8,128)(2,1)} fusion(bf16[512,128]{1,0:T(8,128)(2,1)} %bitcast.67, bf16[512,128]{1,0:T(8,128)(2,1)} %bitcast.68), kind=kLoop, calls=%fused_computation.3 | loop fusion | flops 524288 | bytes 524288 | tf_op jit(solution)/shard_map/concatenate | solution.py:206
  8.5 2.9 %collective-permute-start.2 = (bf16[1,128,512]{2,1,0:T(8,128)(2,1)}, bf16[1,128,512]{2,1,0:T(8,128)(2,1)S(1)}, u32[]{:S(2)}, u32[]{:S(2)}) collective-permute-start(bf16[1,128,512]{2,1,0:T(8,128)(2,1)} %param.10), channel_id=1, source_target_pairs={{0,32},{32,64},{64,96},{96,128},{128,160},{160,192},{192,224},{224... | collective-permute-start | bytes 393224 | tf_op jit(solution)/shard_map/ppermute | solution.py:26
  11.3 1.7 %collective-permute-done.1 = bf16[1,128,512]{2,1,0:T(8,128)(2,1)S(1)} collective-permute-done((bf16[1,128,512]{2,1,0:T(8,128)(2,1)}, bf16[1,128,512]{2,1,0:T(8,128)(2,1)S(1)}, u32[]{:S(2)}, u32[]{:S(2)}) %collective-permute-start.1) | collective-permute-done | bytes 131104 | tf_op jit(solution)/shard_map/ppermute | solution.py:26
  13.1 1.3 collective-permute-done.2
  14.6 11.6 %all_to_all.60 = bf16[128,4,256]{2,0,1:T(8,128)(2,1)} all-to-all(bf16[128,4,256]{2,0,1:T(8,128)(2,1)S(1)} %pad_maximum_fusion.1), channel_id=1, replica_groups=mesh['section'=16,'gx'=4,'gz'=8] {'gx'}, dimensions={1} | all-to-all | bytes 524288 | tf_op jit(solution)/shard_map/all_to_all | solution.py:204
  26.2 14.2 %collective-permute-done = bf16[1,128,4096]{2,1,0:T(8,128)(2,1)S(1)} collective-permute-done((bf16[1,128,4096]{2,1,0:T(8,128)(2,1)S(1)}, bf16[1,128,4096]{2,1,0:T(8,128)(2,1)S(1)}, u32[]{:S(2)}, u32[]{:S(2)}) %collective-permute-start) | collective-permute-done | bytes 1048608 | tf_op jit(solution)/shard_map/ppermute | solution.py:26
  40.4 0.2 copy.41
  40.7 1.4 copy.31
  42.0 11.3 %all-to-all-start = ((bf16[128,32,128]{2,0,1:T(8,128)(2,1)}), bf16[128,32,128]{2,0,1:T(8,128)(2,1)S(1)}, u32[]{:S(2)}, u32[]{:S(2)}) async-start(bf16[128,32,128]{2,0,1:T(8,128)(2,1)} %copy.31), calls=%async_computation | async-start | bytes 2097152 | tf_op jit(solution)/shard_map/all_to_all | solution.py:193
  54.2 0.1 copy.30
  54.3 0.7 reshape.136.pick_ref
  55.1 0.1 and_reduce_fusion
  55.4 0.1 min.17
  55.7 0.7 mul.19.crow_ref
  56.3 0.2 broadcast_in_dim.31
  56.5 0.9 reshape_reshape_reshape.4.sbias_ref
  57.5 0.6 compare_select_fusion.vbias_ref
  58.1 0.6 fusion.6
  58.7 22.3 %all-to-all-done = bf16[128,32,128]{2,0,1:T(8,128)(2,1)S(1)} async-done(((bf16[128,32,128]{2,0,1:T(8,128)(2,1)}), bf16[128,32,128]{2,0,1:T(8,128)(2,1)S(1)}, u32[]{:S(2)}, u32[]{:S(2)}) %all-to-all-start) | async-done | bytes 1048608 | tf_op jit(solution)/shard_map/all_to_all | solution.py:193
  81.0 1.0 copy-done
  82.0 21.3 %shard_map.82 = (f32[4096,128]{1,0:T(8,128)}, f32[4096,1]{1,0:T(8,128)}, f32[4096,1]{1,0:T(8,128)}) custom-call(s32[32]{0:T(128)} %bitcast.69, bf16[4096,128]{1,0:T(8,128)(2,1)} %bitcast.49, bf16[4096,256]{1,0:T(8,128)(2,1)} %all-gather.3.cloned.1.call-done.ckv_ref, f32[1,2048]{1,0:T(1,128)} %compare_select_fusion.vbias_ref), custom_call_target="tpu_custom_call" | custom-call | tf_op jit(solution)/shard_map/pallas_call | solution.py:114
  103.2 4.3 %all-gather.5.cloned.1.call-done.skv_ref = bf16[8,512,256]{2,1,0:T(8,128)(2,1)} async-done(((bf16[1,512,256]{2,1,0:T(8,128)(2,1)}), bf16[8,512,256]{2,1,0:T(8,128)(2,1)}) %all-gather.5.cloned.1.call-update) | async-done | bytes 2097168 | tf_op jit(solution)/shard_map/all_gather | solution.py:205
  107.5 11.0 %shard_map.84 = bf16[32,64,128]{2,1,0:T(8,128)(2,1)} custom-call(s32[768]{0:T(1024)} %mul.19.crow_ref, s32[768]{0:T(1024)} %get-tuple-element.12.splane_ref, s32[768]{0:T(1024)} %get-tuple-element.11.srow_ref, s32[768]{0:T(1024)} %reshape.136.pick_ref, bf16[32,2,64,128]{3,2,1,0:T(8,128)(2,1)} %bitcast.50, ...), custom_call_target="tpu_custom_call" | custom-call | tf_op jit(solution)/shard_map/pallas_call | solution.py:175
  118.5 6.5 %all-to-all-start.3 = ((bf16[32,64,1,128]{3,1,2,0:T(8,128)(2,1)}), bf16[32,64,1,128]{3,1,2,0:T(8,128)(2,1)S(1)}, u32[]{:S(2)}, u32[]{:S(2)}) async-start(bf16[32,64,1,128]{3,1,2,0:T(8,128)(2,1)} %bitcast.60), calls=%async_computation.3 | async-start | bytes 1048576 | tf_op jit(solution)/shard_map/all_to_all | solution.py:212
  125.1 10.9 %shard_map.83 = bf16[32,64,128]{2,1,0:T(8,128)(2,1)} custom-call(s32[768]{0:T(1024)} %mul.19.crow_ref, s32[768]{0:T(1024)} %get-tuple-element.12.splane_ref, s32[768]{0:T(1024)} %get-tuple-element.11.srow_ref, s32[768]{0:T(1024)} %reshape.136.pick_ref, bf16[32,2,64,128]{3,2,1,0:T(8,128)(2,1)} %bitcast.51, ...), custom_call_target="tpu_custom_call" | custom-call | tf_op jit(solution)/shard_map/pallas_call | solution.py:175
  136.0 3.0 %all-to-all-done.3 = bf16[32,64,1,128]{3,1,2,0:T(8,128)(2,1)S(1)} async-done(((bf16[32,64,1,128]{3,1,2,0:T(8,128)(2,1)}), bf16[32,64,1,128]{3,1,2,0:T(8,128)(2,1)S(1)}, u32[]{:S(2)}, u32[]{:S(2)}) %all-to-all-start.3) | async-done | bytes 524320 | tf_op jit(solution)/shard_map/all_to_all | solution.py:212
  139.0 6.8 %all-to-all-start.2 = ((bf16[32,64,1,128]{3,1,2,0:T(8,128)(2,1)}), bf16[32,64,1,128]{3,1,2,0:T(8,128)(2,1)S(1)}, u32[]{:S(2)}, u32[]{:S(2)}) async-start(bf16[32,64,1,128]{3,1,2,0:T(8,128)(2,1)} %bitcast.59), calls=%async_computation.2 | async-start | bytes 1048576 | tf_op jit(solution)/shard_map/all_to_all | solution.py:212
  145.8 0.3 copy.40
  146.2 13.9 %all-to-all-done.2 = bf16[32,64,1,128]{3,1,2,0:T(8,128)(2,1)S(1)} async-done(((bf16[32,64,1,128]{3,1,2,0:T(8,128)(2,1)}), bf16[32,64,1,128]{3,1,2,0:T(8,128)(2,1)S(1)}, u32[]{:S(2)}, u32[]{:S(2)}) %all-to-all-start.2) | async-done | bytes 524320 | tf_op jit(solution)/shard_map/all_to_all | solution.py:212
  160.0 0.3 copy.37
  160.4 0.4 copy_bitcast_fusion
  160.8 1.1 maximum_bitcast_fusion
  (28 shorter events, 0.9 us)
Async XLA Ops:
  6.5 19.6 %copy-start.2 = (bf16[1,128,4096]{2,1,0:T(8,128)(2,1)S(1)}, bf16[1,128,4096]{2,1,0:T(8,128)(2,1)}, u32[]{:S(2)}) copy-start(bf16[1,128,4096]{2,1,0:T(8,128)(2,1)} %param.8) | copy-start | bytes 3145732
  6.5 74.4 %all-gather.3.cloned.1.call-start = ((), (), s32[]{:S(2)}) async-start(), calls=%async_computation.4 | async-start | bytes 2359296 | tf_op jit(solution)/shard_map/all_gather | solution.py:207
  8.4 99.1 %all-gather.5.cloned.1.call-start = ((), (), s32[]{:S(2)}) async-start(), calls=%async_computation.5 | async-start | bytes 2359296 | tf_op jit(solution)/shard_map/all_gather | solution.py:205
  8.4 4.6 %collective-permute-start.1 = (bf16[1,128,512]{2,1,0:T(8,128)(2,1)}, bf16[1,128,512]{2,1,0:T(8,128)(2,1)S(1)}, u32[]{:S(2)}, u32[]{:S(2)}) collective-permute-start(bf16[1,128,512]{2,1,0:T(8,128)(2,1)} %param.9), channel_id=1, source_target_pairs={{0,32},{32,64},{64,96},{96,128},{128,160},{160,192},{192,224},{224... | collective-permute-start | bytes 393224 | tf_op jit(solution)/shard_map/ppermute | solution.py:26
  8.5 6.0 %collective-permute-start.2 = (bf16[1,128,512]{2,1,0:T(8,128)(2,1)}, bf16[1,128,512]{2,1,0:T(8,128)(2,1)S(1)}, u32[]{:S(2)}, u32[]{:S(2)}) collective-permute-start(bf16[1,128,512]{2,1,0:T(8,128)(2,1)} %param.10), channel_id=1, source_target_pairs={{0,32},{32,64},{64,96},{96,128},{128,160},{160,192},{192,224},{224... | collective-permute-start | bytes 393224 | tf_op jit(solution)/shard_map/ppermute | solution.py:26
  26.1 14.2 %collective-permute-start = (bf16[1,128,4096]{2,1,0:T(8,128)(2,1)S(1)}, bf16[1,128,4096]{2,1,0:T(8,128)(2,1)S(1)}, u32[]{:S(2)}, u32[]{:S(2)}) collective-permute-start(bf16[1,128,4096]{2,1,0:T(8,128)(2,1)S(1)} %copy-done.2), channel_id=1, source_target_pairs={{0,32},{32,64},{64,96},{96,128},{128,160},{160,192},{192,224},{224... | collective-permute-start | bytes 3145736 | tf_op jit(solution)/shard_map/ppermute | solution.py:26
  40.6 13.4 %copy-start.3 = (s32[1,1,11]{2,1,0:T(1,128)S(1)}, s32[1,1,11]{2,1,0:T(1,128)}, u32[]{:S(2)}) copy-start(s32[1,1,11]{2,1,0:T(1,128)} %param.15) | copy-start | bytes 136
  40.6 14.4 %copy-start.1 = (s32[1,1,32]{2,1,0:T(1,128)S(1)}, s32[1,1,32]{2,1,0:T(1,128)}, u32[]{:S(2)}) copy-start(s32[1,1,32]{2,1,0:T(1,128)} %param.13) | copy-start | bytes 388
  42.0 38.9 %all-to-all-start = ((bf16[128,32,128]{2,0,1:T(8,128)(2,1)}), bf16[128,32,128]{2,0,1:T(8,128)(2,1)S(1)}, u32[]{:S(2)}, u32[]{:S(2)}) async-start(bf16[128,32,128]{2,0,1:T(8,128)(2,1)} %copy.31), calls=%async_computation | async-start | bytes 2097152 | tf_op jit(solution)/shard_map/all_to_all | solution.py:193
  81.0 1.0 copy-start
  118.5 20.5 %all-to-all-start.3 = ((bf16[32,64,1,128]{3,1,2,0:T(8,128)(2,1)}), bf16[32,64,1,128]{3,1,2,0:T(8,128)(2,1)S(1)}, u32[]{:S(2)}, u32[]{:S(2)}) async-start(bf16[32,64,1,128]{3,1,2,0:T(8,128)(2,1)} %bitcast.60), calls=%async_computation.3 | async-start | bytes 1048576 | tf_op jit(solution)/shard_map/all_to_all | solution.py:212
  139.0 21.0 %all-to-all-start.2 = ((bf16[32,64,1,128]{3,1,2,0:T(8,128)(2,1)}), bf16[32,64,1,128]{3,1,2,0:T(8,128)(2,1)S(1)}, u32[]{:S(2)}, u32[]{:S(2)}) async-start(bf16[32,64,1,128]{3,1,2,0:T(8,128)(2,1)} %bitcast.59), calls=%async_computation.2 | async-start | bytes 1048576 | tf_op jit(solution)/shard_map/all_to_all | solution.py:212
Sparse Core Ops, SparseCore 0:
  9.4 50.8 all-gather.2
  62.4 45.0 all-gather.4

commit v10 on v9

--- a/solution.py
+++ b/solution.py
@@ -16,7 +16,7 @@
 NS = 11
 CACHE = 4096
 TQ = 256
-STQ = 512
+STQ = 1024
 
 big_negative = -1e30
 

time: 169 us -> 170 us (level)
  no operation moved by 1% of the time
where the time goes in v10:
time: 170 us
  waiting for transfers between devices  60.3 us (35%)
  Pallas kernels  44.1 us (26%)
  starting transfers between devices  28.1 us (17%)
  between operations  14.2 us (8%)
  blocking collectives  11.6 us (7%)
  local copies, waits for them, and re-layouts  6.81 us (4%)
  other arithmetic  4.57 us (3%)
    pallas_call x2, Pallas kernels, head_attention(): pl.pallas_call(functools.partial(slash_kernel, parity=parity), grid_spec=...  22.8 us
    all_to_all x1, waiting for transfers between devices, per_device(): lax.all_to_all(q_rows, ('gx', 'gz'), split_axis=1, concat_axis=0, tiled=T...  22.3 us
    pallas_call x1, Pallas kernels, vertical_part(): pl.pallas_call(vertical_kernel, grid_spec=grid_spec, out_shape=[jax.Shape...  21.3 us
    ppermute x3, waiting for transfers between devices, from_behind(): return lax.ppermute(x, axis, [(i, (i + by) % peers) for i in range(peers)])  17.2 us
    all_to_all x2, waiting for transfers between devices, per_device(): lax.all_to_all(half[:, :, None, :], ('gx', 'gz'), split_axis=0, concat_ax...  16.5 us
    all_to_all x2, starting transfers between devices, per_device(): lax.all_to_all(half[:, :, None, :], ('gx', 'gz'), split_axis=0, concat_ax...  13.8 us
    all_to_all x1, blocking collectives, per_device(): lax.all_to_all(kv_rows, 'gx', split_axis=1, concat_axis=0, tiled=True)  11.6 us
    all_to_all x1, starting transfers between devices, per_device(): lax.all_to_all(q_rows, ('gx', 'gz'), split_axis=1, concat_axis=0, tiled=T...  11.3 us
  transfers between devices with their start and end apart: 8, of which 7 were waited for; matrix products, arithmetic and copies ran while one was open for 4% of the time, Pallas kernels for 19%

profile of v10, /device:TPU:24, one launch (start us, length us, event | category | flops | bytes accessed | tf_op | source)
XLA Modules:
  0.0 169.6 jit_solution(4895346170500374801)
XLA Ops:
  6.5 1.8 %pad_maximum_fusion = bf16[512,256]{1,0:T(8,128)(2,1)} fusion(bf16[512,128]{1,0:T(8,128)(2,1)} %bitcast.67, bf16[512,128]{1,0:T(8,128)(2,1)} %bitcast.68), kind=kLoop, calls=%fused_computation.3 | loop fusion | flops 524288 | bytes 524288 | tf_op jit(solution)/shard_map/concatenate | solution.py:206
  8.5 2.9 %collective-permute-start.2 = (bf16[1,128,512]{2,1,0:T(8,128)(2,1)}, bf16[1,128,512]{2,1,0:T(8,128)(2,1)S(1)}, u32[]{:S(2)}, u32[]{:S(2)}) collective-permute-start(bf16[1,128,512]{2,1,0:T(8,128)(2,1)} %param.10), channel_id=1, source_target_pairs={{0,32},{32,64},{64,96},{96,128},{128,160},{160,192},{192,224},{224... | collective-permute-start | bytes 393224 | tf_op jit(solution)/shard_map/ppermute | solution.py:26
  11.3 1.7 %collective-permute-done.1 = bf16[1,128,512]{2,1,0:T(8,128)(2,1)S(1)} collective-permute-done((bf16[1,128,512]{2,1,0:T(8,128)(2,1)}, bf16[1,128,512]{2,1,0:T(8,128)(2,1)S(1)}, u32[]{:S(2)}, u32[]{:S(2)}) %collective-permute-start.1) | collective-permute-done | bytes 131104 | tf_op jit(solution)/shard_map/ppermute | solution.py:26
  13.1 1.3 collective-permute-done.2
  14.6 11.6 %all_to_all.60 = bf16[128,4,256]{2,0,1:T(8,128)(2,1)} all-to-all(bf16[128,4,256]{2,0,1:T(8,128)(2,1)S(1)} %pad_maximum_fusion.1), channel_id=1, replica_groups=mesh['section'=16,'gx'=4,'gz'=8] {'gx'}, dimensions={1} | all-to-all | bytes 524288 | tf_op jit(solution)/shard_map/all_to_all | solution.py:204
  26.2 14.2 %collective-permute-done = bf16[1,128,4096]{2,1,0:T(8,128)(2,1)S(1)} collective-permute-done((bf16[1,128,4096]{2,1,0:T(8,128)(2,1)S(1)}, bf16[1,128,4096]{2,1,0:T(8,128)(2,1)S(1)}, u32[]{:S(2)}, u32[]{:S(2)}) %collective-permute-start) | collective-permute-done | bytes 1048608 | tf_op jit(solution)/shard_map/ppermute | solution.py:26
  40.4 0.2 copy.41
  40.7 1.4 copy.31
  42.0 11.3 %all-to-all-start = ((bf16[128,32,128]{2,0,1:T(8,128)(2,1)}), bf16[128,32,128]{2,0,1:T(8,128)(2,1)S(1)}, u32[]{:S(2)}, u32[]{:S(2)}) async-start(bf16[128,32,128]{2,0,1:T(8,128)(2,1)} %copy.31), calls=%async_computation | async-start | bytes 2097152 | tf_op jit(solution)/shard_map/all_to_all | solution.py:193
  54.2 0.1 copy.30
  54.3 0.7 reshape.136.pick_ref
  55.1 0.1 and_reduce_fusion
  55.4 0.1 min.17
  55.7 0.7 mul.19.crow_ref
  56.3 0.2 broadcast_in_dim.31
  56.5 0.9 reshape_reshape_reshape.4.sbias_ref
  57.5 0.6 compare_select_fusion.vbias_ref
  58.1 0.6 fusion.6
  58.7 22.3 %all-to-all-done = bf16[128,32,128]{2,0,1:T(8,128)(2,1)S(1)} async-done(((bf16[128,32,128]{2,0,1:T(8,128)(2,1)}), bf16[128,32,128]{2,0,1:T(8,128)(2,1)S(1)}, u32[]{:S(2)}, u32[]{:S(2)}) %all-to-all-start) | async-done | bytes 1048608 | tf_op jit(solution)/shard_map/all_to_all | solution.py:193
  81.0 1.0 copy-done
  82.0 21.3 %shard_map.82 = (f32[4096,128]{1,0:T(8,128)}, f32[4096,1]{1,0:T(8,128)}, f32[4096,1]{1,0:T(8,128)}) custom-call(s32[32]{0:T(128)} %bitcast.69, bf16[4096,128]{1,0:T(8,128)(2,1)} %bitcast.49, bf16[4096,256]{1,0:T(8,128)(2,1)} %all-gather.3.cloned.1.call-done.ckv_ref, f32[1,2048]{1,0:T(1,128)} %compare_select_fusion.vbias_ref), custom_call_target="tpu_custom_call" | custom-call | tf_op jit(solution)/shard_map/pallas_call | solution.py:114
  103.2 4.3 %all-gather.5.cloned.1.call-done.skv_ref = bf16[8,512,256]{2,1,0:T(8,128)(2,1)} async-done(((bf16[1,512,256]{2,1,0:T(8,128)(2,1)}), bf16[8,512,256]{2,1,0:T(8,128)(2,1)}) %all-gather.5.cloned.1.call-update) | async-done | bytes 2097168 | tf_op jit(solution)/shard_map/all_gather | solution.py:205
  107.5 11.4 %shard_map.84 = bf16[32,64,128]{2,1,0:T(8,128)(2,1)} custom-call(s32[768]{0:T(1024)} %mul.19.crow_ref, s32[768]{0:T(1024)} %get-tuple-element.12.splane_ref, s32[768]{0:T(1024)} %get-tuple-element.11.srow_ref, s32[768]{0:T(1024)} %reshape.136.pick_ref, bf16[32,2,64,128]{3,2,1,0:T(8,128)(2,1)} %bitcast.50, ...), custom_call_target="tpu_custom_call" | custom-call | tf_op jit(solution)/shard_map/pallas_call | solution.py:175
  118.9 6.5 %all-to-all-start.3 = ((bf16[32,64,1,128]{3,1,2,0:T(8,128)(2,1)}), bf16[32,64,1,128]{3,1,2,0:T(8,128)(2,1)S(1)}, u32[]{:S(2)}, u32[]{:S(2)}) async-start(bf16[32,64,1,128]{3,1,2,0:T(8,128)(2,1)} %bitcast.60), calls=%async_computation.3 | async-start | bytes 1048576 | tf_op jit(solution)/shard_map/all_to_all | solution.py:212
  125.5 11.4 %shard_map.83 = bf16[32,64,128]{2,1,0:T(8,128)(2,1)} custom-call(s32[768]{0:T(1024)} %mul.19.crow_ref, s32[768]{0:T(1024)} %get-tuple-element.12.splane_ref, s32[768]{0:T(1024)} %get-tuple-element.11.srow_ref, s32[768]{0:T(1024)} %reshape.136.pick_ref, bf16[32,2,64,128]{3,2,1,0:T(8,128)(2,1)} %bitcast.51, ...), custom_call_target="tpu_custom_call" | custom-call | tf_op jit(solution)/shard_map/pallas_call | solution.py:175
  136.9 2.5 %all-to-all-done.3 = bf16[32,64,1,128]{3,1,2,0:T(8,128)(2,1)S(1)} async-done(((bf16[32,64,1,128]{3,1,2,0:T(8,128)(2,1)}), bf16[32,64,1,128]{3,1,2,0:T(8,128)(2,1)S(1)}, u32[]{:S(2)}, u32[]{:S(2)}) %all-to-all-start.3) | async-done | bytes 524320 | tf_op jit(solution)/shard_map/all_to_all | solution.py:212
  139.4 7.3 %all-to-all-start.2 = ((bf16[32,64,1,128]{3,1,2,0:T(8,128)(2,1)}), bf16[32,64,1,128]{3,1,2,0:T(8,128)(2,1)S(1)}, u32[]{:S(2)}, u32[]{:S(2)}) async-start(bf16[32,64,1,128]{3,1,2,0:T(8,128)(2,1)} %bitcast.59), calls=%async_computation.2 | async-start | bytes 1048576 | tf_op jit(solution)/shard_map/all_to_all | solution.py:212
  146.7 0.3 copy.40
  147.0 14.0 %all-to-all-done.2 = bf16[32,64,1,128]{3,1,2,0:T(8,128)(2,1)S(1)} async-done(((bf16[32,64,1,128]{3,1,2,0:T(8,128)(2,1)}), bf16[32,64,1,128]{3,1,2,0:T(8,128)(2,1)S(1)}, u32[]{:S(2)}, u32[]{:S(2)}) %all-to-all-start.2) | async-done | bytes 524320 | tf_op jit(solution)/shard_map/all_to_all | solution.py:212
  161.0 0.3 copy.37
  161.3 0.4 copy_bitcast_fusion
  161.7 1.1 maximum_bitcast_fusion
  (28 shorter events, 0.9 us)
Async XLA Ops:
  6.5 19.6 %copy-start.2 = (bf16[1,128,4096]{2,1,0:T(8,128)(2,1)S(1)}, bf16[1,128,4096]{2,1,0:T(8,128)(2,1)}, u32[]{:S(2)}) copy-start(bf16[1,128,4096]{2,1,0:T(8,128)(2,1)} %param.8) | copy-start | bytes 3145732
  6.5 74.4 %all-gather.3.cloned.1.call-start = ((), (), s32[]{:S(2)}) async-start(), calls=%async_computation.4 | async-start | bytes 2359296 | tf_op jit(solution)/shard_map/all_gather | solution.py:207
  8.4 99.1 %all-gather.5.cloned.1.call-start = ((), (), s32[]{:S(2)}) async-start(), calls=%async_computation.5 | async-start | bytes 2359296 | tf_op jit(solution)/shard_map/all_gather | solution.py:205
  8.4 4.6 %collective-permute-start.1 = (bf16[1,128,512]{2,1,0:T(8,128)(2,1)}, bf16[1,128,512]{2,1,0:T(8,128)(2,1)S(1)}, u32[]{:S(2)}, u32[]{:S(2)}) collective-permute-start(bf16[1,128,512]{2,1,0:T(8,128)(2,1)} %param.9), channel_id=1, source_target_pairs={{0,32},{32,64},{64,96},{96,128},{128,160},{160,192},{192,224},{224... | collective-permute-start | bytes 393224 | tf_op jit(solution)/shard_map/ppermute | solution.py:26
  8.5 6.0 %collective-permute-start.2 = (bf16[1,128,512]{2,1,0:T(8,128)(2,1)}, bf16[1,128,512]{2,1,0:T(8,128)(2,1)S(1)}, u32[]{:S(2)}, u32[]{:S(2)}) collective-permute-start(bf16[1,128,512]{2,1,0:T(8,128)(2,1)} %param.10), channel_id=1, source_target_pairs={{0,32},{32,64},{64,96},{96,128},{128,160},{160,192},{192,224},{224... | collective-permute-start | bytes 393224 | tf_op jit(solution)/shard_map/ppermute | solution.py:26
  26.1 14.2 %collective-permute-start = (bf16[1,128,4096]{2,1,0:T(8,128)(2,1)S(1)}, bf16[1,128,4096]{2,1,0:T(8,128)(2,1)S(1)}, u32[]{:S(2)}, u32[]{:S(2)}) collective-permute-start(bf16[1,128,4096]{2,1,0:T(8,128)(2,1)S(1)} %copy-done.2), channel_id=1, source_target_pairs={{0,32},{32,64},{64,96},{96,128},{128,160},{160,192},{192,224},{224... | collective-permute-start | bytes 3145736 | tf_op jit(solution)/shard_map/ppermute | solution.py:26
  40.6 13.4 %copy-start.3 = (s32[1,1,11]{2,1,0:T(1,128)S(1)}, s32[1,1,11]{2,1,0:T(1,128)}, u32[]{:S(2)}) copy-start(s32[1,1,11]{2,1,0:T(1,128)} %param.15) | copy-start | bytes 136
  40.6 14.4 %copy-start.1 = (s32[1,1,32]{2,1,0:T(1,128)S(1)}, s32[1,1,32]{2,1,0:T(1,128)}, u32[]{:S(2)}) copy-start(s32[1,1,32]{2,1,0:T(1,128)} %param.13) | copy-start | bytes 388
  42.0 38.9 %all-to-all-start = ((bf16[128,32,128]{2,0,1:T(8,128)(2,1)}), bf16[128,32,128]{2,0,1:T(8,128)(2,1)S(1)}, u32[]{:S(2)}, u32[]{:S(2)}) async-start(bf16[128,32,128]{2,0,1:T(8,128)(2,1)} %copy.31), calls=%async_computation | async-start | bytes 2097152 | tf_op jit(solution)/shard_map/all_to_all | solution.py:193
  81.0 1.0 copy-start
  118.9 20.5 %all-to-all-start.3 = ((bf16[32,64,1,128]{3,1,2,0:T(8,128)(2,1)}), bf16[32,64,1,128]{3,1,2,0:T(8,128)(2,1)S(1)}, u32[]{:S(2)}, u32[]{:S(2)}) async-start(bf16[32,64,1,128]{3,1,2,0:T(8,128)(2,1)} %bitcast.60), calls=%async_computation.3 | async-start | bytes 1048576 | tf_op jit(solution)/shard_map/all_to_all | solution.py:212
  139.4 21.6 %all-to-all-start.2 = ((bf16[32,64,1,128]{3,1,2,0:T(8,128)(2,1)}), bf16[32,64,1,128]{3,1,2,0:T(8,128)(2,1)S(1)}, u32[]{:S(2)}, u32[]{:S(2)}) async-start(bf16[32,64,1,128]{3,1,2,0:T(8,128)(2,1)} %bitcast.59), calls=%async_computation.2 | async-start | bytes 1048576 | tf_op jit(solution)/shard_map/all_to_all | solution.py:212
Sparse Core Ops, SparseCore 0:
  9.4 50.8 all-gather.2
  62.4 45.0 all-gather.4

commit v11 on v9

--- a/solution.py
+++ b/solution.py
@@ -26,7 +26,7 @@
     return lax.ppermute(x, axis, [(i, (i + by) % peers) for i in range(peers)])
 
 
-def vertical_kernel(verts_ref, q_ref, ckv_ref, vbias_ref, acc_ref, top_ref, total_ref, kvert):
+def vertical_kernel(verts_ref, q_ref, kv_ref, vbias_ref, acc_ref, top_ref, total_ref, kvert):
     tile = pl.program_id(0)
     softmax_scale = 1.0 / math.sqrt(HEAD_SIZE)
     ncb = CACHE // BLK
@@ -35,9 +35,10 @@
     def _():
         def fill(s, carry):
             blk = jnp.clip(verts_ref[s], 0, ncb - 1)
-            src = pl.multiple_of(blk * BLK, BLK)
+            per = kv_ref.shape[1] // BLK
+            src = pl.multiple_of((blk % per) * BLK, BLK)
             dst = pl.multiple_of(s * BLK, BLK)
-            kvert[pl.ds(dst, BLK), :] = ckv_ref[pl.ds(src, BLK), :]
+            kvert[pl.ds(dst, BLK), :] = kv_ref[blk // per, pl.ds(src, BLK), pl.ds(0, 2 * HEAD_SIZE)]
             return carry
 
         lax.fori_loop(0, NVMAX, fill, 0)
@@ -52,7 +53,7 @@
                            preferred_element_type=jnp.float32)
 
 
-def slash_kernel(crow_ref, splane_ref, srow_ref, pick_ref, q_ref, ckv_ref, skv_ref, sbias_ref,
+def slash_kernel(cplane_ref, crow_ref, splane_ref, srow_ref, pick_ref, q_ref, kv_ref, sbias_ref,
                  acc_ref, top_ref, total_ref, o_ref, kslash, causal_bias, *, parity):
     nb = STQ // BLK
     nd = NS + 1
@@ -71,8 +72,10 @@
         qb = 2 * (tile * nb + b) + parity
         for d in range(nd):
             at = qb * nd + d
-            from_cache = ckv_ref[pl.ds(pl.multiple_of(crow_ref[at], BLK), BLK), :]
-            from_stretch = skv_ref[splane_ref[at], pl.ds(pl.multiple_of(srow_ref[at], BLK), BLK), :]
+            from_cache = kv_ref[cplane_ref[at], pl.ds(pl.multiple_of(crow_ref[at], BLK), BLK),
+                                pl.ds(0, 2 * HEAD_SIZE)]
+            from_stretch = kv_ref[splane_ref[at], pl.ds(pl.multiple_of(srow_ref[at], BLK), BLK),
+                                  pl.ds(2 * HEAD_SIZE, 2 * HEAD_SIZE)]
             kslash[b, pl.ds(d * BLK, BLK), :] = jnp.where(pick_ref[at] > 0, from_stretch,
                                                           from_cache)
 
@@ -91,7 +94,7 @@
     o_ref[...] = (acc / total).astype(o_ref.dtype)
 
 
-def vertical_part(own_query, ckv, verts, count):
+def vertical_part(own_query, kv, verts, count):
     prefill_stretch = own_query.shape[0]
     nvc = NVMAX * BLK
     slot = jnp.arange(nvc, dtype=jnp.int32) // BLK
@@ -101,7 +104,7 @@
         grid=(prefill_stretch // TQ,),
         in_specs=[
             pl.BlockSpec((TQ, HEAD_SIZE), lambda i, *_: (i, 0)),
-            pl.BlockSpec(ckv.shape, lambda i, *_: (0, 0)),
+            pl.BlockSpec(kv.shape, lambda i, *_: (0, 0, 0)),
             pl.BlockSpec((1, nvc), lambda i, *_: (0, 0)),
         ],
         out_specs=[
@@ -120,16 +123,17 @@
             jax.ShapeDtypeStruct((prefill_stretch, 1), jnp.float32),
         ],
         compiler_params=pltpu.CompilerParams(dimension_semantics=("arbitrary",)),
-    )(verts, own_query, ckv, vbias)
-
-
-def head_attention(own_query, ckv, skv, verts, count, slashes, tok):
+    )(verts, own_query, kv, vbias)
+
+
+def head_attention(own_query, kv, verts, count, slashes, tok):
     prefill_stretch = own_query.shape[0]
-    nz = skv.shape[0]
+    nz = kv.shape[0]
+    cache_per = kv.shape[1] // BLK
     ncb = CACHE // BLK
     nqb = prefill_stretch // BLK
     nd = NS + 1
-    acc_v, top_v, total_v = vertical_part(own_query, ckv, verts, count)
+    acc_v, top_v, total_v = vertical_part(own_query, kv, verts, count)
     offsets = jnp.concatenate([jnp.zeros((1,), jnp.int32), slashes])
     blocks = ncb + jnp.arange(nqb, dtype=jnp.int32)[:, None] - offsets[None, :]
     used = jnp.arange(NVMAX, dtype=jnp.int32)[None, None, :] < count
@@ -139,7 +143,9 @@
     stretch_blk = jnp.clip(blocks - ncb, 0, nqb - 1)
     dev = stretch_blk // per_dev
     pick = (blocks >= ncb).astype(jnp.int32).reshape(-1)
-    crow = (jnp.clip(blocks, 0, ncb - 1) * BLK).reshape(-1)
+    cache_blk = jnp.clip(blocks, 0, ncb - 1)
+    cplane = (cache_blk // cache_per).reshape(-1)
+    crow = ((cache_blk % cache_per) * BLK).reshape(-1)
     splane = (dev % nz).reshape(-1)
     srow = ((dev // nz) * tok + (stretch_blk % per_dev) * BLK).reshape(-1)
     sbias = jnp.repeat(jnp.where(valid, 0.0, big_negative).astype(jnp.float32), BLK,
@@ -155,12 +161,11 @@
     outs = []
     for parity in range(2):
         grid_spec = pltpu.PrefetchScalarGridSpec(
-            num_scalar_prefetch=4,
+            num_scalar_prefetch=5,
             grid=(halves // nb,),
             in_specs=[
                 pl.BlockSpec((nb, 1, BLK, HEAD_SIZE), lambda i, *_, p=parity: (i, p, 0, 0)),
-                pl.BlockSpec(ckv.shape, lambda i, *_: (0, 0)),
-                pl.BlockSpec(skv.shape, lambda i, *_: (0, 0, 0)),
+                pl.BlockSpec(kv.shape, lambda i, *_: (0, 0, 0)),
                 pl.BlockSpec((nb, 1, 1, width), lambda i, *_, p=parity: (i, p, 0, 0)),
                 pl.BlockSpec((nb, 1, BLK, HEAD_SIZE), lambda i, *_, p=parity: (i, p, 0, 0)),
                 pl.BlockSpec((nb, 1, BLK, 1), lambda i, *_, p=parity: (i, p, 0, 0)),
@@ -177,7 +182,7 @@
             grid_spec=grid_spec,
             out_shape=jax.ShapeDtypeStruct((halves, BLK, HEAD_SIZE), jnp.bfloat16),
             compiler_params=pltpu.CompilerParams(dimension_semantics=("arbitrary",)),
-        )(crow, splane, srow, pick, q4, ckv, skv, sbias4, acc4, top4, total4))
+        )(cplane, crow, splane, srow, pick, q4, kv, sbias4, acc4, top4, total4))
     return outs
 
 
@@ -202,11 +207,11 @@
         axis=2,
     )
     part = lax.all_to_all(kv_rows, "gx", split_axis=1, concat_axis=0, tiled=True)
-    skv = lax.all_gather(part.reshape(nx * tok, 2 * HEAD_SIZE), "gz", axis=0, tiled=False)
-    cache_part = jnp.concatenate([cache_keys[0, 0], cache_values[0, 0]], axis=1)
-    ckv = lax.all_gather(cache_part, "gz", axis=0, tiled=True)
-    halves = head_attention(own_query, ckv, skv, vertical[0, 0], vertical_count[0, 0],
-                            slash[0, 0], tok)
+    shard = jnp.concatenate(
+        [cache_keys[0, 0], cache_values[0, 0], part.reshape(nx * tok, 2 * HEAD_SIZE)], axis=1)
+    kv = lax.all_gather(shard, "gz", axis=0, tiled=False)
+    halves = head_attention(own_query, kv, vertical[0, 0], vertical_count[0, 0], slash[0, 0],
+                            tok)
     pieces = []
     for half in halves:
         moved = lax.all_to_all(half[:, :, None, :], ("gx", "gz"), split_axis=0, concat_axis=2,

time: 169 us -> 198 us (1.17)
  the two profiles are of different devices: /device:TPU:24 before, /device:TPU:8 now
where the time goes in v11:
time: 198 us
  waiting for transfers between devices  91.9 us (46%)
  Pallas kernels  44.2 us (22%)
  starting transfers between devices  25.6 us (13%)
  between operations  14.2 us (7%)
  blocking collectives  10.8 us (5%)
  local copies, waits for them, and re-layouts  7.45 us (4%)
  other arithmetic  3.59 us (2%)
    all_to_all x1, waiting for transfers between devices, per_device(): lax.all_to_all(q_rows, ('gx', 'gz'), split_axis=1, concat_axis=0, tiled=T...  33.7 us
    pallas_call x2, Pallas kernels, head_attention(): pl.pallas_call(functools.partial(slash_kernel, parity=parity), grid_spec=...  22.2 us
    pallas_call x1, Pallas kernels, vertical_part(): pl.pallas_call(vertical_kernel, grid_spec=grid_spec, out_shape=[jax.Shape...  22.1 us
    all_to_all x2, waiting for transfers between devices, per_device(): lax.all_to_all(half[:, :, None, :], ('gx', 'gz'), split_axis=0, concat_ax...  21.8 us
    all_gather x1, waiting for transfers between devices, per_device(): kv = lax.all_gather(shard, 'gz', axis=0, tiled=False)  19.1 us
    ppermute x3, waiting for transfers between devices, from_behind(): return lax.ppermute(x, axis, [(i, (i + by) % peers) for i in range(peers)])  17.3 us
    all_to_all x2, starting transfers between devices, per_device(): lax.all_to_all(half[:, :, None, :], ('gx', 'gz'), split_axis=0, concat_ax...  12.6 us
    all_to_all x1, starting transfers between devices, per_device(): lax.all_to_all(q_rows, ('gx', 'gz'), split_axis=1, concat_axis=0, tiled=T...  11.3 us
  transfers between devices with their start and end apart: 7, of which 7 were waited for; matrix products, arithmetic and copies ran while one was open for 4% of the time, Pallas kernels for 6%

profile of v11, /device:TPU:8, one launch (start us, length us, event | category | flops | bytes accessed | tf_op | source)
XLA Modules:
  0.0 197.7 jit_solution(2724816104280722046)
XLA Ops:
  6.5 1.1 copy.39
  7.7 1.0 copy.38
  8.7 1.7 collective-permute-start.1
  10.4 1.7 collective-permute-done.2
  12.1 1.4 collective-permute-done.1
  13.5 0.1 copy.40
  13.7 10.8 %all_to_all.60 = bf16[128,4,256]{2,0,1:T(8,128)(2,1)S(1)} all-to-all(bf16[128,4,256]{2,0,1:T(8,128)(2,1)S(1)} %copy.40), channel_id=1, replica_groups=mesh['section'=16,'gx'=4,'gz'=8] {'gx'}, dimensions={1} | all-to-all | bytes 524288 | tf_op jit(solution)/shard_map/all_to_all | solution.py:209
  24.4 0.9 pad_maximum_fusion
  25.3 14.2 %collective-permute-done = bf16[1,128,4096]{2,1,0:T(8,128)(2,1)S(1)} collective-permute-done((bf16[1,128,4096]{2,1,0:T(8,128)(2,1)S(1)}, bf16[1,128,4096]{2,1,0:T(8,128)(2,1)S(1)}, u32[]{:S(2)}, u32[]{:S(2)}) %collective-permute-start) | collective-permute-done | bytes 1048608 | tf_op jit(solution)/shard_map/ppermute | solution.py:26
  39.6 0.2 copy.48
  39.8 1.4 copy.37
  41.2 11.3 %all-to-all-start = ((bf16[128,32,128]{2,0,1:T(8,128)(2,1)}), bf16[128,32,128]{2,0,1:T(8,128)(2,1)S(1)}, u32[]{:S(2)}, u32[]{:S(2)}) async-start(bf16[128,32,128]{2,0,1:T(8,128)(2,1)} %copy.37), calls=%async_computation | async-start | bytes 2097152 | tf_op jit(solution)/shard_map/all_to_all | solution.py:198
  53.4 0.7 reshape.141.pick_ref
  54.2 0.1 and_reduce_fusion
  54.9 0.2 broadcast_in_dim.31
  55.1 0.9 reshape_reshape_reshape.4.sbias_ref
  56.1 0.6 compare_select_fusion.vbias_ref
  56.7 0.6 fusion.4
  57.3 33.7 %all-to-all-done = bf16[128,32,128]{2,0,1:T(8,128)(2,1)S(1)} async-done(((bf16[128,32,128]{2,0,1:T(8,128)(2,1)}), bf16[128,32,128]{2,0,1:T(8,128)(2,1)S(1)}, u32[]{:S(2)}, u32[]{:S(2)}) %all-to-all-start) | async-done | bytes 1048608 | tf_op jit(solution)/shard_map/all_to_all | solution.py:198
  91.0 19.1 %all-gather.3.cloned.1.call-done = bf16[4096,512]{1,0:T(8,128)(2,1)} async-done(((bf16[512,512]{1,0:T(8,128)(2,1)}), bf16[4096,512]{1,0:T(8,128)(2,1)}) %all-gather.3.cloned.1.call-update) | async-done | bytes 4194320 | tf_op jit(solution)/shard_map/all_gather | solution.py:212
  110.1 22.1 %shard_map.82 = (f32[4096,128]{1,0:T(8,128)}, f32[4096,1]{1,0:T(8,128)}, f32[4096,1]{1,0:T(8,128)}) custom-call(s32[32]{0:T(128)} %bitcast.81, bf16[4096,128]{1,0:T(8,128)(2,1)} %bitcast.57, bf16[8,512,512]{2,1,0:T(8,128)(2,1)} %bitcast.54, f32[1,2048]{1,0:T(1,128)} %compare_select_fusion.vbias_ref), custom_call_target="tpu_custom_call" | custom-call | tf_op jit(solution)/shard_map/pallas_call | solution.py:117
  132.2 11.1 %shard_map.84 = bf16[32,64,128]{2,1,0:T(8,128)(2,1)} custom-call(s32[768]{0:T(1024)} %get-tuple-element.14.cplane_ref, s32[768]{0:T(1024)} %get-tuple-element.13.crow_ref, s32[768]{0:T(1024)} %get-tuple-element.18.splane_ref, s32[768]{0:T(1024)} %get-tuple-element.19.srow_ref, s32[768]{0:T(1024)} %reshape.141.pick_ref, bf16[32,2,64,128]{3,2,1,0:T(8,128)(2,1)} %bitcast.58, ...), custom_call_target="tpu_custom_call" | custom-call | tf_op jit(solution)/shard_map/pallas_call | solution.py:180
  143.3 7.0 %all-to-all-start.3 = ((bf16[32,64,1,128]{3,1,2,0:T(8,128)(2,1)}), bf16[32,64,1,128]{3,1,2,0:T(8,128)(2,1)S(1)}, u32[]{:S(2)}, u32[]{:S(2)}) async-start(bf16[32,64,1,128]{3,1,2,0:T(8,128)(2,1)} %bitcast.68), calls=%async_computation.3 | async-start | bytes 1048576 | tf_op jit(solution)/shard_map/all_to_all | solution.py:217
  150.2 11.1 %shard_map.83 = bf16[32,64,128]{2,1,0:T(8,128)(2,1)} custom-call(s32[768]{0:T(1024)} %get-tuple-element.14.cplane_ref, s32[768]{0:T(1024)} %get-tuple-element.13.crow_ref, s32[768]{0:T(1024)} %get-tuple-element.18.splane_ref, s32[768]{0:T(1024)} %get-tuple-element.19.srow_ref, s32[768]{0:T(1024)} %reshape.141.pick_ref, bf16[32,2,64,128]{3,2,1,0:T(8,128)(2,1)} %bitcast.59, ...), custom_call_target="tpu_custom_call" | custom-call | tf_op jit(solution)/shard_map/pallas_call | solution.py:180
  161.3 5.8 %all-to-all-done.3 = bf16[32,64,1,128]{3,1,2,0:T(8,128)(2,1)S(1)} async-done(((bf16[32,64,1,128]{3,1,2,0:T(8,128)(2,1)}), bf16[32,64,1,128]{3,1,2,0:T(8,128)(2,1)S(1)}, u32[]{:S(2)}, u32[]{:S(2)}) %all-to-all-start.3) | async-done | bytes 524320 | tf_op jit(solution)/shard_map/all_to_all | solution.py:217
  167.1 5.6 %all-to-all-start.2 = ((bf16[32,64,1,128]{3,1,2,0:T(8,128)(2,1)}), bf16[32,64,1,128]{3,1,2,0:T(8,128)(2,1)S(1)}, u32[]{:S(2)}, u32[]{:S(2)}) async-start(bf16[32,64,1,128]{3,1,2,0:T(8,128)(2,1)} %bitcast.67), calls=%async_computation.2 | async-start | bytes 1048576 | tf_op jit(solution)/shard_map/all_to_all | solution.py:217
  172.7 0.3 copy.47
  173.1 0.2 copy.53
  173.3 16.0 %all-to-all-done.2 = bf16[32,64,1,128]{3,1,2,0:T(8,128)(2,1)S(1)} async-done(((bf16[32,64,1,128]{3,1,2,0:T(8,128)(2,1)}), bf16[32,64,1,128]{3,1,2,0:T(8,128)(2,1)S(1)}, u32[]{:S(2)}, u32[]{:S(2)}) %all-to-all-start.2) | async-done | bytes 524320 | tf_op jit(solution)/shard_map/all_to_all | solution.py:217
  189.3 0.3 copy.44
  189.6 0.2 copy.54
  189.8 1.1 maximum_bitcast_fusion
  (29 shorter events, 1.0 us)
Async XLA Ops:
  6.5 17.9 %copy-start.1 = (bf16[1,1,512,128]{3,2,1,0:T(8,128)(2,1)S(1)}, bf16[1,1,512,128]{3,2,1,0:T(8,128)(2,1)}, u32[]{:S(2)}) copy-start(bf16[1,1,512,128]{3,2,1,0:T(8,128)(2,1)} %param.12) | copy-start | bytes 393220
  6.5 17.9 %copy-start.2 = (bf16[1,1,512,128]{3,2,1,0:T(8,128)(2,1)S(1)}, bf16[1,1,512,128]{3,2,1,0:T(8,128)(2,1)}, u32[]{:S(2)}) copy-start(bf16[1,1,512,128]{3,2,1,0:T(8,128)(2,1)} %param.11) | copy-start | bytes 393220
  6.5 18.8 %copy-start.4 = (bf16[1,128,4096]{2,1,0:T(8,128)(2,1)S(1)}, bf16[1,128,4096]{2,1,0:T(8,128)(2,1)}, u32[]{:S(2)}) copy-start(bf16[1,128,4096]{2,1,0:T(8,128)(2,1)} %param.8) | copy-start | bytes 3145732
  6.5 103.6 %all-gather.3.cloned.1.call-start = ((), (), s32[]{:S(2)}) async-start(), calls=%async_computation.4 | async-start | bytes 4718592 | tf_op jit(solution)/shard_map/all_gather | solution.py:212
  7.7 4.4 %collective-permute-start.2 = (bf16[1,128,512]{1,2,0:T(8,128)(2,1)S(1)}, bf16[1,128,512]{1,2,0:T(8,128)(2,1)S(1)}, u32[]{:S(2)}, u32[]{:S(2)}) collective-permute-start(bf16[1,128,512]{1,2,0:T(8,128)(2,1)S(1)} %copy.39), channel_id=1, source_target_pairs={{0,32},{32,64},{64,96},{96,128},{128,160},{160,192},{192,224},{224... | collective-permute-start | bytes 393224 | tf_op jit(solution)/shard_map/ppermute | solution.py:26
  8.7 4.8 %collective-permute-start.1 = (bf16[1,128,512]{1,2,0:T(8,128)(2,1)S(1)}, bf16[1,128,512]{1,2,0:T(8,128)(2,1)S(1)}, u32[]{:S(2)}, u32[]{:S(2)}) collective-permute-start(bf16[1,128,512]{1,2,0:T(8,128)(2,1)S(1)} %copy.38), channel_id=1, source_target_pairs={{0,32},{32,64},{64,96},{96,128},{128,160},{160,192},{192,224},{224... | collective-permute-start | bytes 393224 | tf_op jit(solution)/shard_map/ppermute | solution.py:26
  25.3 14.2 %collective-permute-start = (bf16[1,128,4096]{2,1,0:T(8,128)(2,1)S(1)}, bf16[1,128,4096]{2,1,0:T(8,128)(2,1)S(1)}, u32[]{:S(2)}, u32[]{:S(2)}) collective-permute-start(bf16[1,128,4096]{2,1,0:T(8,128)(2,1)S(1)} %copy-done.4), channel_id=1, source_target_pairs={{0,32},{32,64},{64,96},{96,128},{128,160},{160,192},{192,224},{224... | collective-permute-start | bytes 3145736 | tf_op jit(solution)/shard_map/ppermute | solution.py:26
  39.8 13.4 %copy-start.5 = (s32[1,1,11]{2,1,0:T(1,128)S(1)}, s32[1,1,11]{2,1,0:T(1,128)}, u32[]{:S(2)}) copy-start(s32[1,1,11]{2,1,0:T(1,128)} %param.15) | copy-start | bytes 136
  39.8 14.4 %copy-start.3 = (s32[1,1,32]{2,1,0:T(1,128)S(1)}, s32[1,1,32]{2,1,0:T(1,128)}, u32[]{:S(2)}) copy-start(s32[1,1,32]{2,1,0:T(1,128)} %param.13) | copy-start | bytes 388
  41.2 49.8 %all-to-all-start = ((bf16[128,32,128]{2,0,1:T(8,128)(2,1)}), bf16[128,32,128]{2,0,1:T(8,128)(2,1)S(1)}, u32[]{:S(2)}, u32[]{:S(2)}) async-start(bf16[128,32,128]{2,0,1:T(8,128)(2,1)} %copy.37), calls=%async_computation | async-start | bytes 2097152 | tf_op jit(solution)/shard_map/all_to_all | solution.py:198
  91.0 19.1 %copy-start = (bf16[128,32,128]{2,0,1:T(8,128)(2,1)}, bf16[128,32,128]{2,0,1:T(8,128)(2,1)S(1)}, u32[]{:S(2)}) copy-start(bf16[128,32,128]{2,0,1:T(8,128)(2,1)S(1)} %all-to-all-done) | copy-start | bytes 3145732
  143.3 23.8 %all-to-all-start.3 = ((bf16[32,64,1,128]{3,1,2,0:T(8,128)(2,1)}), bf16[32,64,1,128]{3,1,2,0:T(8,128)(2,1)S(1)}, u32[]{:S(2)}, u32[]{:S(2)}) async-start(bf16[32,64,1,128]{3,1,2,0:T(8,128)(2,1)} %bitcast.68), calls=%async_computation.3 | async-start | bytes 1048576 | tf_op jit(solution)/shard_map/all_to_all | solution.py:217
  167.1 22.2 %all-to-all-start.2 = ((bf16[32,64,1,128]{3,1,2,0:T(8,128)(2,1)}), bf16[32,64,1,128]{3,1,2,0:T(8,128)(2,1)S(1)}, u32[]{:S(2)}, u32[]{:S(2)}) async-start(bf16[32,64,1,128]{3,1,2,0:T(8,128)(2,1)} %bitcast.67), calls=%async_computation.2 | async-start | bytes 1048576 | tf_op jit(solution)/shard_map/all_to_all | solution.py:217
Sparse Core Ops, SparseCore 0:
  25.4 84.6 all-gather.2

commit v12 on v9

--- a/solution.py
+++ b/solution.py
@@ -52,8 +52,8 @@
                            preferred_element_type=jnp.float32)
 
 
-def slash_kernel(crow_ref, splane_ref, srow_ref, pick_ref, q_ref, ckv_ref, skv_ref, sbias_ref,
-                 acc_ref, top_ref, total_ref, o_ref, kslash, causal_bias, *, parity):
+def slash_kernel(urow_ref, q_ref, ckv_hbm, skv_hbm, sbias_ref, acc_ref, top_ref, total_ref,
+                 o_ref, kslash, causal_bias, kvall, sems, *, parity):
     nb = STQ // BLK
     nd = NS + 1
     width = nd * BLK
@@ -66,15 +66,21 @@
         row = lax.broadcasted_iota(jnp.int32, (BLK, width), 0)
         causal = (col >= BLK) | (col <= row)
         causal_bias[...] = jnp.where(causal, 0.0, big_negative).astype(jnp.float32)
+        cache_rows = ckv_hbm.shape[0]
+        first = pltpu.make_async_copy(ckv_hbm, kvall.at[pl.ds(0, cache_rows)], sems.at[0])
+        second = pltpu.make_async_copy(skv_hbm, kvall.at[pl.ds(cache_rows, skv_hbm.shape[0])],
+                                       sems.at[1])
+        first.start()
+        second.start()
+        first.wait()
+        second.wait()
 
     for b in range(nb):
         qb = 2 * (tile * nb + b) + parity
         for d in range(nd):
             at = qb * nd + d
-            from_cache = ckv_ref[pl.ds(pl.multiple_of(crow_ref[at], BLK), BLK), :]
-            from_stretch = skv_ref[splane_ref[at], pl.ds(pl.multiple_of(srow_ref[at], BLK), BLK), :]
-            kslash[b, pl.ds(d * BLK, BLK), :] = jnp.where(pick_ref[at] > 0, from_stretch,
-                                                          from_cache)
+            kslash[b, pl.ds(d * BLK, BLK), :] = kvall[pl.ds(pl.multiple_of(urow_ref[at], BLK),
+                                                             BLK), :]
 
     q3 = q_ref[...].reshape(nb, BLK, HEAD_SIZE)
     s_s = lax.dot_general(q3, kslash[:, :, :HEAD_SIZE], (((2,), (2,)), ((0,), (0,))),
@@ -138,10 +144,11 @@
     per_dev = tok // BLK
     stretch_blk = jnp.clip(blocks - ncb, 0, nqb - 1)
     dev = stretch_blk // per_dev
-    pick = (blocks >= ncb).astype(jnp.int32).reshape(-1)
-    crow = (jnp.clip(blocks, 0, ncb - 1) * BLK).reshape(-1)
-    splane = (dev % nz).reshape(-1)
-    srow = ((dev // nz) * tok + (stretch_blk % per_dev) * BLK).reshape(-1)
+    cache_rows = ckv.shape[0]
+    part_rows = skv.shape[1]
+    srow = cache_rows + (dev % nz) * part_rows + (dev // nz) * tok + (stretch_blk % per_dev) * BLK
+    urow = jnp.where(blocks >= ncb, srow, jnp.clip(blocks, 0, ncb - 1) * BLK).reshape(-1)
+    flat_skv = skv.reshape(nz * part_rows, 2 * HEAD_SIZE)
     sbias = jnp.repeat(jnp.where(valid, 0.0, big_negative).astype(jnp.float32), BLK,
                        axis=1).reshape(nqb, 1, nd * BLK)
     nb = STQ // BLK
@@ -155,12 +162,12 @@
     outs = []
     for parity in range(2):
         grid_spec = pltpu.PrefetchScalarGridSpec(
-            num_scalar_prefetch=4,
+            num_scalar_prefetch=1,
             grid=(halves // nb,),
             in_specs=[
                 pl.BlockSpec((nb, 1, BLK, HEAD_SIZE), lambda i, *_, p=parity: (i, p, 0, 0)),
-                pl.BlockSpec(ckv.shape, lambda i, *_: (0, 0)),
-                pl.BlockSpec(skv.shape, lambda i, *_: (0, 0, 0)),
+                pl.BlockSpec(memory_space=pl.ANY),
+                pl.BlockSpec(memory_space=pl.ANY),
                 pl.BlockSpec((nb, 1, 1, width), lambda i, *_, p=parity: (i, p, 0, 0)),
                 pl.BlockSpec((nb, 1, BLK, HEAD_SIZE), lambda i, *_, p=parity: (i, p, 0, 0)),
                 pl.BlockSpec((nb, 1, BLK, 1), lambda i, *_, p=parity: (i, p, 0, 0)),
@@ -170,6 +177,8 @@
             scratch_shapes=[
                 pltpu.VMEM((nb, width, 2 * HEAD_SIZE), jnp.bfloat16),
                 pltpu.VMEM((BLK, width), jnp.float32),
+                pltpu.VMEM((ckv.shape[0] + nz * part_rows, 2 * HEAD_SIZE), jnp.bfloat16),
+                pltpu.SemaphoreType.DMA((2,)),
             ],
         )
         outs.append(pl.pallas_call(
@@ -177,7 +186,7 @@
             grid_spec=grid_spec,
             out_shape=jax.ShapeDtypeStruct((halves, BLK, HEAD_SIZE), jnp.bfloat16),
             compiler_params=pltpu.CompilerParams(dimension_semantics=("arbitrary",)),
-        )(crow, splane, srow, pick, q4, ckv, skv, sbias4, acc4, top4, total4))
+        )(urow, q4, ckv, flat_skv, sbias4, acc4, top4, total4))
     return outs
 
 

time: 169 us -> 170 us (level)
  the two profiles are of different devices: /device:TPU:24 before, /device:TPU:88 now
where the time goes in v12:
time: 170 us; the launch traced here: 169 us
  waiting for transfers between devices  62.7 us (37%)
  Pallas kernels  42.9 us (25%)
  starting transfers between devices  25.8 us (15%)
  between operations  14.2 us (8%)
  blocking collectives  11.5 us (7%)
  local copies, waits for them, and re-layouts  7.72 us (5%)
  other arithmetic  4.53 us (3%)
    all_to_all x1, waiting for transfers between devices, per_device(): lax.all_to_all(q_rows, ('gx', 'gz'), split_axis=1, concat_axis=0, tiled=T...  26.6 us
    pallas_call x2, Pallas kernels, head_attention(): pl.pallas_call(functools.partial(slash_kernel, parity=parity), grid_spec=...  21.6 us
    pallas_call x1, Pallas kernels, vertical_part(): pl.pallas_call(vertical_kernel, grid_spec=grid_spec, out_shape=[jax.Shape...  21.3 us
    all_to_all x2, waiting for transfers between devices, per_device(): lax.all_to_all(half[:, :, None, :], ('gx', 'gz'), split_axis=0, concat_ax...  19.9 us
    ppermute x3, waiting for transfers between devices, from_behind(): return lax.ppermute(x, axis, [(i, (i + by) % peers) for i in range(peers)])  16.1 us
    all_to_all x2, starting transfers between devices, per_device(): lax.all_to_all(half[:, :, None, :], ('gx', 'gz'), split_axis=0, concat_ax...  12.1 us
    all_to_all x1, blocking collectives, per_device(): lax.all_to_all(kv_rows, 'gx', split_axis=1, concat_axis=0, tiled=True)  11.5 us
    all_to_all x1, starting transfers between devices, per_device(): lax.all_to_all(q_rows, ('gx', 'gz'), split_axis=1, concat_axis=0, tiled=T...  10.7 us
  transfers between devices with their start and end apart: 8, of which 6 were waited for; matrix products, arithmetic and copies ran while one was open for 5% of the time, Pallas kernels for 19%

profile of v12, /device:TPU:88, one launch (start us, length us, event | category | flops | bytes accessed | tf_op | source)
XLA Modules:
  0.0 169.3 jit_solution(4707832168872156489)
XLA Ops:
  6.5 1.8 %pad_maximum_fusion = bf16[512,256]{1,0:T(8,128)(2,1)} fusion(bf16[512,128]{1,0:T(8,128)(2,1)} %bitcast.72, bf16[512,128]{1,0:T(8,128)(2,1)} %bitcast.73), kind=kLoop, calls=%fused_computation.3 | loop fusion | flops 524288 | bytes 524288 | tf_op jit(solution)/shard_map/concatenate | solution.py:215
  8.4 1.0 copy.39
  9.5 1.0 copy.38
  10.5 2.9 %collective-permute-start.1 = (bf16[1,128,512]{1,2,0:T(8,128)(2,1)S(1)}, bf16[1,128,512]{1,2,0:T(8,128)(2,1)S(1)}, u32[]{:S(2)}, u32[]{:S(2)}) collective-permute-start(bf16[1,128,512]{1,2,0:T(8,128)(2,1)S(1)} %copy.38), channel_id=1, source_target_pairs={{0,32},{32,64},{64,96},{96,128},{128,160},{160,192},{192,224},{224... | collective-permute-start | bytes 393224 | tf_op jit(solution)/shard_map/ppermute | solution.py:26
  13.4 0.5 collective-permute-done.2
  13.8 1.4 collective-permute-done.1
  15.3 0.1 copy.40
  15.4 11.5 %all_to_all.60 = bf16[128,4,256]{2,0,1:T(8,128)(2,1)} all-to-all(bf16[128,4,256]{2,0,1:T(8,128)(2,1)S(1)} %copy.40), channel_id=1, replica_groups=mesh['section'=16,'gx'=4,'gz'=8] {'gx'}, dimensions={1} | all-to-all | bytes 524288 | tf_op jit(solution)/shard_map/all_to_all | solution.py:213
  27.0 14.2 %collective-permute-done = bf16[1,128,4096]{2,1,0:T(8,128)(2,1)S(1)} collective-permute-done((bf16[1,128,4096]{2,1,0:T(8,128)(2,1)S(1)}, bf16[1,128,4096]{2,1,0:T(8,128)(2,1)S(1)}, u32[]{:S(2)}, u32[]{:S(2)}) %collective-permute-start) | collective-permute-done | bytes 1048608 | tf_op jit(solution)/shard_map/ppermute | solution.py:26
  41.2 0.2 copy.48
  41.4 1.4 copy.37
  42.8 10.7 %all-to-all-start = ((bf16[128,32,128]{2,0,1:T(8,128)(2,1)}), bf16[128,32,128]{2,0,1:T(8,128)(2,1)S(1)}, u32[]{:S(2)}, u32[]{:S(2)}) async-start(bf16[128,32,128]{2,0,1:T(8,128)(2,1)} %copy.37), calls=%async_computation | async-start | bytes 2097152 | tf_op jit(solution)/shard_map/all_to_all | solution.py:202
  54.4 0.1 copy.34
  54.5 0.1 ge.12
  54.7 0.1 and_reduce_fusion
  55.4 0.2 broadcast_in_dim.31
  55.6 0.9 reshape_reshape_reshape.4.sbias_ref
  56.5 0.6 compare_select_fusion.vbias_ref
  57.1 0.6 fusion.8.urow_ref
  57.8 26.6 %all-to-all-done = bf16[128,32,128]{2,0,1:T(8,128)(2,1)S(1)} async-done(((bf16[128,32,128]{2,0,1:T(8,128)(2,1)}), bf16[128,32,128]{2,0,1:T(8,128)(2,1)S(1)}, u32[]{:S(2)}, u32[]{:S(2)}) %all-to-all-start) | async-done | bytes 1048608 | tf_op jit(solution)/shard_map/all_to_all | solution.py:202
  84.4 1.0 copy-done
  85.3 21.3 %shard_map.82 = (f32[4096,128]{1,0:T(8,128)}, f32[4096,1]{1,0:T(8,128)}, f32[4096,1]{1,0:T(8,128)}) custom-call(s32[32]{0:T(128)} %bitcast.76, bf16[4096,128]{1,0:T(8,128)(2,1)} %bitcast.52, bf16[4096,256]{1,0:T(8,128)(2,1)} %all-gather.3.cloned.1.call-done.ckv_ref.ckv_hbm, f32[1,2048]{1,0:T(1,128)} %compare_select_fusion.vbias_ref), custom_call_target="tpu_custom_call" | custom-call | tf_op jit(solution)/shard_map/pallas_call | solution.py:120
  106.6 10.8 %shard_map.84 = bf16[32,64,128]{2,1,0:T(8,128)(2,1)} custom-call(s32[768]{0:T(1024)} %fusion.8.urow_ref, bf16[32,2,64,128]{3,2,1,0:T(8,128)(2,1)} %bitcast.53, bf16[4096,256]{1,0:T(8,128)(2,1)} %all-gather.3.cloned.1.call-done.ckv_ref.ckv_hbm, bf16[4096,256]{1,0:T(8,128)(2,1)} %bitcast.55, f32[32,2,1,768]{3,2,1,0:T(1,128)} %reshape_reshape_reshape.4.sbias_ref, ...), custom_call_target="tpu_custom_call" | custom-call | tf_op jit(solution)/shard_map/pallas_call | solution.py:184
  117.4 7.2 %all-to-all-start.3 = ((bf16[32,64,1,128]{3,1,2,0:T(8,128)(2,1)}), bf16[32,64,1,128]{3,1,2,0:T(8,128)(2,1)S(1)}, u32[]{:S(2)}, u32[]{:S(2)}) async-start(bf16[32,64,1,128]{3,1,2,0:T(8,128)(2,1)} %bitcast.65), calls=%async_computation.3 | async-start | bytes 1048576 | tf_op jit(solution)/shard_map/all_to_all | solution.py:221
  124.7 10.8 %shard_map.83 = bf16[32,64,128]{2,1,0:T(8,128)(2,1)} custom-call(s32[768]{0:T(1024)} %fusion.8.urow_ref, bf16[32,2,64,128]{3,2,1,0:T(8,128)(2,1)} %bitcast.54, bf16[4096,256]{1,0:T(8,128)(2,1)} %all-gather.3.cloned.1.call-done.ckv_ref.ckv_hbm, bf16[4096,256]{1,0:T(8,128)(2,1)} %bitcast.56, f32[32,2,1,768]{3,2,1,0:T(1,128)} %reshape_reshape_reshape.4.sbias_ref, ...), custom_call_target="tpu_custom_call" | custom-call | tf_op jit(solution)/shard_map/pallas_call | solution.py:184
  135.5 5.1 %all-to-all-done.3 = bf16[32,64,1,128]{3,1,2,0:T(8,128)(2,1)S(1)} async-done(((bf16[32,64,1,128]{3,1,2,0:T(8,128)(2,1)}), bf16[32,64,1,128]{3,1,2,0:T(8,128)(2,1)S(1)}, u32[]{:S(2)}, u32[]{:S(2)}) %all-to-all-start.3) | async-done | bytes 524320 | tf_op jit(solution)/shard_map/all_to_all | solution.py:221
  140.5 4.8 %all-to-all-start.2 = ((bf16[32,64,1,128]{3,1,2,0:T(8,128)(2,1)}), bf16[32,64,1,128]{3,1,2,0:T(8,128)(2,1)S(1)}, u32[]{:S(2)}, u32[]{:S(2)}) async-start(bf16[32,64,1,128]{3,1,2,0:T(8,128)(2,1)} %bitcast.64), calls=%async_computation.2 | async-start | bytes 1048576 | tf_op jit(solution)/shard_map/all_to_all | solution.py:221
  145.4 0.3 copy.47
  145.7 14.9 %all-to-all-done.2 = bf16[32,64,1,128]{3,1,2,0:T(8,128)(2,1)S(1)} async-done(((bf16[32,64,1,128]{3,1,2,0:T(8,128)(2,1)}), bf16[32,64,1,128]{3,1,2,0:T(8,128)(2,1)S(1)}, u32[]{:S(2)}, u32[]{:S(2)}) %all-to-all-start.2) | async-done | bytes 524320 | tf_op jit(solution)/shard_map/all_to_all | solution.py:221
  160.6 0.3 copy.44
  161.0 0.4 copy_bitcast_fusion
  161.4 1.1 maximum_bitcast_fusion
  (27 shorter events, 1.0 us)
Async XLA Ops:
  6.5 20.4 %copy-start.2 = (bf16[1,128,4096]{2,1,0:T(8,128)(2,1)S(1)}, bf16[1,128,4096]{2,1,0:T(8,128)(2,1)}, u32[]{:S(2)}) copy-start(bf16[1,128,4096]{2,1,0:T(8,128)(2,1)} %param.8) | copy-start | bytes 3145732
  6.5 77.8 %all-gather.3.cloned.1.call-start = ((), (), s32[]{:S(2)}) async-start(), calls=%async_computation.4 | async-start | bytes 2359296 | tf_op jit(solution)/shard_map/all_gather | solution.py:216
  8.4 98.2 %all-gather.5.cloned.1.call-start = ((), (), s32[]{:S(2)}) async-start(), calls=%async_computation.5 | async-start | bytes 2359296 | tf_op jit(solution)/shard_map/all_gather | solution.py:214
  9.4 4.4 %collective-permute-start.2 = (bf16[1,128,512]{1,2,0:T(8,128)(2,1)S(1)}, bf16[1,128,512]{1,2,0:T(8,128)(2,1)S(1)}, u32[]{:S(2)}, u32[]{:S(2)}) collective-permute-start(bf16[1,128,512]{1,2,0:T(8,128)(2,1)S(1)} %copy.39), channel_id=1, source_target_pairs={{0,32},{32,64},{64,96},{96,128},{128,160},{160,192},{192,224},{224... | collective-permute-start | bytes 393224 | tf_op jit(solution)/shard_map/ppermute | solution.py:26
  10.5 4.8 %collective-permute-start.1 = (bf16[1,128,512]{1,2,0:T(8,128)(2,1)S(1)}, bf16[1,128,512]{1,2,0:T(8,128)(2,1)S(1)}, u32[]{:S(2)}, u32[]{:S(2)}) collective-permute-start(bf16[1,128,512]{1,2,0:T(8,128)(2,1)S(1)} %copy.38), channel_id=1, source_target_pairs={{0,32},{32,64},{64,96},{96,128},{128,160},{160,192},{192,224},{224... | collective-permute-start | bytes 393224 | tf_op jit(solution)/shard_map/ppermute | solution.py:26
  26.9 14.2 %collective-permute-start = (bf16[1,128,4096]{2,1,0:T(8,128)(2,1)S(1)}, bf16[1,128,4096]{2,1,0:T(8,128)(2,1)S(1)}, u32[]{:S(2)}, u32[]{:S(2)}) collective-permute-start(bf16[1,128,4096]{2,1,0:T(8,128)(2,1)S(1)} %copy-done.2), channel_id=1, source_target_pairs={{0,32},{32,64},{64,96},{96,128},{128,160},{160,192},{192,224},{224... | collective-permute-start | bytes 3145736 | tf_op jit(solution)/shard_map/ppermute | solution.py:26
  41.4 12.8 %copy-start.3 = (s32[1,1,11]{2,1,0:T(1,128)S(1)}, s32[1,1,11]{2,1,0:T(1,128)}, u32[]{:S(2)}) copy-start(s32[1,1,11]{2,1,0:T(1,128)} %param.15) | copy-start | bytes 136
  41.4 13.3 %copy-start.1 = (s32[1,1,32]{2,1,0:T(1,128)S(1)}, s32[1,1,32]{2,1,0:T(1,128)}, u32[]{:S(2)}) copy-start(s32[1,1,32]{2,1,0:T(1,128)} %param.13) | copy-start | bytes 388
  42.8 41.6 %all-to-all-start = ((bf16[128,32,128]{2,0,1:T(8,128)(2,1)}), bf16[128,32,128]{2,0,1:T(8,128)(2,1)S(1)}, u32[]{:S(2)}, u32[]{:S(2)}) async-start(bf16[128,32,128]{2,0,1:T(8,128)(2,1)} %copy.37), calls=%async_computation | async-start | bytes 2097152 | tf_op jit(solution)/shard_map/all_to_all | solution.py:202
  84.4 1.0 copy-start
  117.4 23.1 %all-to-all-start.3 = ((bf16[32,64,1,128]{3,1,2,0:T(8,128)(2,1)}), bf16[32,64,1,128]{3,1,2,0:T(8,128)(2,1)S(1)}, u32[]{:S(2)}, u32[]{:S(2)}) async-start(bf16[32,64,1,128]{3,1,2,0:T(8,128)(2,1)} %bitcast.65), calls=%async_computation.3 | async-start | bytes 1048576 | tf_op jit(solution)/shard_map/all_to_all | solution.py:221
  140.5 20.1 %all-to-all-start.2 = ((bf16[32,64,1,128]{3,1,2,0:T(8,128)(2,1)}), bf16[32,64,1,128]{3,1,2,0:T(8,128)(2,1)S(1)}, u32[]{:S(2)}, u32[]{:S(2)}) async-start(bf16[32,64,1,128]{3,1,2,0:T(8,128)(2,1)} %bitcast.64), calls=%async_computation.2 | async-start | bytes 1048576 | tf_op jit(solution)/shard_map/all_to_all | solution.py:221
Sparse Core Ops, SparseCore 0:
  9.4 48.3 all-gather.2
  59.9 46.4 all-gather.4

commit v13 on v9

--- a/solution.py
+++ b/solution.py
@@ -209,9 +209,8 @@
                             slash[0, 0], tok)
     pieces = []
     for half in halves:
-        moved = lax.all_to_all(half[:, :, None, :], ("gx", "gz"), split_axis=0, concat_axis=2,
-                               tiled=True)
-        pieces.append(moved.reshape(tok // 2, heads * HEAD_SIZE))
+        moved = lax.all_to_all(half, ("gx", "gz"), split_axis=0, concat_axis=0, tiled=True)
+        pieces.append(moved.transpose(1, 0, 2).reshape(tok // 2, heads * HEAD_SIZE))
     return jnp.concatenate(pieces, axis=0).reshape(1, tok, heads * HEAD_SIZE)
 
 

time: 169 us -> 168 us (level)
  the two profiles are of different devices: /device:TPU:24 before, /device:TPU:88 now
where the time goes in v13:
time: 168 us
  waiting for transfers between devices  60.7 us (36%)
  Pallas kernels  43.2 us (26%)
  starting transfers between devices  27.5 us (16%)
  between operations  14.2 us (8%)
  blocking collectives  11.6 us (7%)
  local copies, waits for them, and re-layouts  5.84 us (3%)
  other arithmetic  4.55 us (3%)
    all_to_all x1, waiting for transfers between devices, per_device(): lax.all_to_all(q_rows, ('gx', 'gz'), split_axis=1, concat_axis=0, tiled=T...  24.5 us
    pallas_call x2, Pallas kernels, head_attention(): pl.pallas_call(functools.partial(slash_kernel, parity=parity), grid_spec=...  21.9 us
    pallas_call x1, Pallas kernels, vertical_part(): pl.pallas_call(vertical_kernel, grid_spec=grid_spec, out_shape=[jax.Shape...  21.3 us
    all_to_all x2, waiting for transfers between devices, per_device(): lax.all_to_all(half, ('gx', 'gz'), split_axis=0, concat_axis=0, tiled=True)  18.2 us
    ppermute x3, waiting for transfers between devices, from_behind(): return lax.ppermute(x, axis, [(i, (i + by) % peers) for i in range(peers)])  17.2 us
    all_to_all x2, starting transfers between devices, per_device(): lax.all_to_all(half, ('gx', 'gz'), split_axis=0, concat_axis=0, tiled=True)  13.8 us
    all_to_all x1, blocking collectives, per_device(): lax.all_to_all(kv_rows, 'gx', split_axis=1, concat_axis=0, tiled=True)  11.6 us
    all_to_all x1, starting transfers between devices, per_device(): lax.all_to_all(q_rows, ('gx', 'gz'), split_axis=1, concat_axis=0, tiled=T...  10.7 us
  transfers between devices with their start and end apart: 8, of which 7 were waited for; matrix products, arithmetic and copies ran while one was open for 4% of the time, Pallas kernels for 19%

profile of v13, /device:TPU:88, one launch (start us, length us, event | category | flops | bytes accessed | tf_op | source)
XLA Modules:
  0.0 167.5 jit_solution(14458758413950553505)
XLA Ops:
  6.5 1.8 %pad_maximum_fusion = bf16[512,256]{1,0:T(8,128)(2,1)} fusion(bf16[512,128]{1,0:T(8,128)(2,1)} %bitcast.51, bf16[512,128]{1,0:T(8,128)(2,1)} %bitcast.52), kind=kLoop, calls=%fused_computation.3 | loop fusion | flops 524288 | bytes 524288 | tf_op jit(solution)/shard_map/concatenate | solution.py:206
  8.4 2.9 %collective-permute-start.2 = (bf16[1,128,512]{2,1,0:T(8,128)(2,1)}, bf16[1,128,512]{2,1,0:T(8,128)(2,1)S(1)}, u32[]{:S(2)}, u32[]{:S(2)}) collective-permute-start(bf16[1,128,512]{2,1,0:T(8,128)(2,1)} %param.10), channel_id=1, source_target_pairs={{0,32},{32,64},{64,96},{96,128},{128,160},{160,192},{192,224},{224... | collective-permute-start | bytes 393224 | tf_op jit(solution)/shard_map/ppermute | solution.py:26
  11.3 1.7 %collective-permute-done.1 = bf16[1,128,512]{2,1,0:T(8,128)(2,1)S(1)} collective-permute-done((bf16[1,128,512]{2,1,0:T(8,128)(2,1)}, bf16[1,128,512]{2,1,0:T(8,128)(2,1)S(1)}, u32[]{:S(2)}, u32[]{:S(2)}) %collective-permute-start.1) | collective-permute-done | bytes 131104 | tf_op jit(solution)/shard_map/ppermute | solution.py:26
  13.1 1.3 collective-permute-done.2
  14.5 11.6 %all_to_all.40 = bf16[128,4,256]{2,0,1:T(8,128)(2,1)} all-to-all(bf16[128,4,256]{2,0,1:T(8,128)(2,1)S(1)} %pad_maximum_fusion.1), channel_id=1, replica_groups=mesh['section'=16,'gx'=4,'gz'=8] {'gx'}, dimensions={1} | all-to-all | bytes 524288 | tf_op jit(solution)/shard_map/all_to_all | solution.py:204
  26.2 14.2 %collective-permute-done = bf16[1,128,4096]{2,1,0:T(8,128)(2,1)S(1)} collective-permute-done((bf16[1,128,4096]{2,1,0:T(8,128)(2,1)S(1)}, bf16[1,128,4096]{2,1,0:T(8,128)(2,1)S(1)}, u32[]{:S(2)}, u32[]{:S(2)}) %collective-permute-start) | collective-permute-done | bytes 1048608 | tf_op jit(solution)/shard_map/ppermute | solution.py:26
  40.4 0.2 copy.39
  40.6 1.4 copy.29
  42.0 10.7 %all-to-all-start = ((bf16[128,32,128]{2,0,1:T(8,128)(2,1)}), bf16[128,32,128]{2,0,1:T(8,128)(2,1)S(1)}, u32[]{:S(2)}, u32[]{:S(2)}) async-start(bf16[128,32,128]{2,0,1:T(8,128)(2,1)} %copy.29), calls=%async_computation | async-start | bytes 2097152 | tf_op jit(solution)/shard_map/all_to_all | solution.py:193
  53.6 0.1 copy.28
  53.7 0.7 reshape.134.pick_ref
  54.5 0.1 and_reduce_fusion
  54.7 0.1 copy.32
  54.8 0.1 copy.27
  54.9 0.1 min.17
  55.0 0.1 copy.26
  55.1 0.7 mul.19.crow_ref
  55.7 0.2 broadcast_in_dim.25
  55.9 0.9 reshape_reshape_reshape.4.sbias_ref
  56.9 0.6 compare_select_fusion.vbias_ref
  57.5 0.6 fusion.6
  58.1 24.5 %all-to-all-done = bf16[128,32,128]{2,0,1:T(8,128)(2,1)S(1)} async-done(((bf16[128,32,128]{2,0,1:T(8,128)(2,1)}), bf16[128,32,128]{2,0,1:T(8,128)(2,1)S(1)}, u32[]{:S(2)}, u32[]{:S(2)}) %all-to-all-start) | async-done | bytes 1048608 | tf_op jit(solution)/shard_map/all_to_all | solution.py:193
  82.6 1.0 copy-done
  83.6 21.3 %shard_map.82 = (f32[4096,128]{1,0:T(8,128)}, f32[4096,1]{1,0:T(8,128)}, f32[4096,1]{1,0:T(8,128)}) custom-call(s32[32]{0:T(128)} %bitcast.53, bf16[4096,128]{1,0:T(8,128)(2,1)} %bitcast.39, bf16[4096,256]{1,0:T(8,128)(2,1)} %all-gather.3.cloned.1.call-done.ckv_ref, f32[1,2048]{1,0:T(1,128)} %compare_select_fusion.vbias_ref), custom_call_target="tpu_custom_call" | custom-call | tf_op jit(solution)/shard_map/pallas_call | solution.py:114
  104.8 0.7 all-gather.5.cloned.1.call-done.skv_ref
  105.6 10.9 %shard_map.83 = bf16[32,64,128]{2,1,0:T(8,128)(2,1)} custom-call(s32[768]{0:T(1024)} %mul.19.crow_ref, s32[768]{0:T(1024)} %get-tuple-element.12.splane_ref, s32[768]{0:T(1024)} %get-tuple-element.11.srow_ref, s32[768]{0:T(1024)} %reshape.134.pick_ref, bf16[32,2,64,128]{3,2,1,0:T(8,128)(2,1)} %bitcast.40, ...), custom_call_target="tpu_custom_call" | custom-call | tf_op jit(solution)/shard_map/pallas_call | solution.py:175
  116.5 7.8 %all-to-all-start.2 = ((bf16[32,64,128]{2,1,0:T(8,128)(2,1)}), bf16[32,64,128]{2,1,0:T(8,128)(2,1)S(1)}, u32[]{:S(2)}, u32[]{:S(2)}) async-start(bf16[32,64,128]{2,1,0:T(8,128)(2,1)} %shard_map.83), calls=%async_computation.2 | async-start | bytes 1048576 | tf_op jit(solution)/shard_map/all_to_all | solution.py:212
  124.3 11.0 %shard_map.84 = bf16[32,64,128]{2,1,0:T(8,128)(2,1)} custom-call(s32[768]{0:T(1024)} %mul.19.crow_ref, s32[768]{0:T(1024)} %get-tuple-element.12.splane_ref, s32[768]{0:T(1024)} %get-tuple-element.11.srow_ref, s32[768]{0:T(1024)} %reshape.134.pick_ref, bf16[32,2,64,128]{3,2,1,0:T(8,128)(2,1)} %bitcast.41, ...), custom_call_target="tpu_custom_call" | custom-call | tf_op jit(solution)/shard_map/pallas_call | solution.py:175
  135.3 3.8 %all-to-all-done.2 = bf16[32,64,128]{2,1,0:T(8,128)(2,1)S(1)} async-done(((bf16[32,64,128]{2,1,0:T(8,128)(2,1)}), bf16[32,64,128]{2,1,0:T(8,128)(2,1)S(1)}, u32[]{:S(2)}, u32[]{:S(2)}) %all-to-all-start.2) | async-done | bytes 524320 | tf_op jit(solution)/shard_map/all_to_all | solution.py:212
  139.1 6.0 %all-to-all-start.3 = ((bf16[32,64,128]{2,1,0:T(8,128)(2,1)}), bf16[32,64,128]{2,1,0:T(8,128)(2,1)S(1)}, u32[]{:S(2)}, u32[]{:S(2)}) async-start(bf16[32,64,128]{2,1,0:T(8,128)(2,1)} %shard_map.84), calls=%async_computation.3 | async-start | bytes 1048576 | tf_op jit(solution)/shard_map/all_to_all | solution.py:212
  145.2 14.4 %all-to-all-done.3 = bf16[32,64,128]{2,1,0:T(8,128)(2,1)S(1)} async-done(((bf16[32,64,128]{2,1,0:T(8,128)(2,1)}), bf16[32,64,128]{2,1,0:T(8,128)(2,1)S(1)}, u32[]{:S(2)}, u32[]{:S(2)}) %all-to-all-start.3) | async-done | bytes 524320 | tf_op jit(solution)/shard_map/all_to_all | solution.py:212
  159.6 1.1 maximum_bitcast_fusion
  (27 shorter events, 0.7 us)
Async XLA Ops:
  6.5 19.6 %copy-start.2 = (bf16[1,128,4096]{2,1,0:T(8,128)(2,1)S(1)}, bf16[1,128,4096]{2,1,0:T(8,128)(2,1)}, u32[]{:S(2)}) copy-start(bf16[1,128,4096]{2,1,0:T(8,128)(2,1)} %param.8) | copy-start | bytes 3145732
  6.5 76.1 %all-gather.3.cloned.1.call-start = ((), (), s32[]{:S(2)}) async-start(), calls=%async_computation.4 | async-start | bytes 2359296 | tf_op jit(solution)/shard_map/all_gather | solution.py:207
  8.4 97.2 %all-gather.5.cloned.1.call-start = ((), (), s32[]{:S(2)}) async-start(), calls=%async_computation.5 | async-start | bytes 2359296 | tf_op jit(solution)/shard_map/all_gather | solution.py:205
  8.4 4.6 %collective-permute-start.1 = (bf16[1,128,512]{2,1,0:T(8,128)(2,1)}, bf16[1,128,512]{2,1,0:T(8,128)(2,1)S(1)}, u32[]{:S(2)}, u32[]{:S(2)}) collective-permute-start(bf16[1,128,512]{2,1,0:T(8,128)(2,1)} %param.9), channel_id=1, source_target_pairs={{0,32},{32,64},{64,96},{96,128},{128,160},{160,192},{192,224},{224... | collective-permute-start | bytes 393224 | tf_op jit(solution)/shard_map/ppermute | solution.py:26
  8.4 6.0 %collective-permute-start.2 = (bf16[1,128,512]{2,1,0:T(8,128)(2,1)}, bf16[1,128,512]{2,1,0:T(8,128)(2,1)S(1)}, u32[]{:S(2)}, u32[]{:S(2)}) collective-permute-start(bf16[1,128,512]{2,1,0:T(8,128)(2,1)} %param.10), channel_id=1, source_target_pairs={{0,32},{32,64},{64,96},{96,128},{128,160},{160,192},{192,224},{224... | collective-permute-start | bytes 393224 | tf_op jit(solution)/shard_map/ppermute | solution.py:26
  26.1 14.2 %collective-permute-start = (bf16[1,128,4096]{2,1,0:T(8,128)(2,1)S(1)}, bf16[1,128,4096]{2,1,0:T(8,128)(2,1)S(1)}, u32[]{:S(2)}, u32[]{:S(2)}) collective-permute-start(bf16[1,128,4096]{2,1,0:T(8,128)(2,1)S(1)} %copy-done.2), channel_id=1, source_target_pairs={{0,32},{32,64},{64,96},{96,128},{128,160},{160,192},{192,224},{224... | collective-permute-start | bytes 3145736 | tf_op jit(solution)/shard_map/ppermute | solution.py:26
  40.6 12.8 %copy-start.3 = (s32[1,1,11]{2,1,0:T(1,128)S(1)}, s32[1,1,11]{2,1,0:T(1,128)}, u32[]{:S(2)}) copy-start(s32[1,1,11]{2,1,0:T(1,128)} %param.15) | copy-start | bytes 136
  40.6 13.8 %copy-start.1 = (s32[1,1,32]{2,1,0:T(1,128)S(1)}, s32[1,1,32]{2,1,0:T(1,128)}, u32[]{:S(2)}) copy-start(s32[1,1,32]{2,1,0:T(1,128)} %param.13) | copy-start | bytes 388
  42.0 40.6 %all-to-all-start = ((bf16[128,32,128]{2,0,1:T(8,128)(2,1)}), bf16[128,32,128]{2,0,1:T(8,128)(2,1)S(1)}, u32[]{:S(2)}, u32[]{:S(2)}) async-start(bf16[128,32,128]{2,0,1:T(8,128)(2,1)} %copy.29), calls=%async_computation | async-start | bytes 2097152 | tf_op jit(solution)/shard_map/all_to_all | solution.py:193
  82.6 1.0 copy-start
  116.5 22.6 %all-to-all-start.2 = ((bf16[32,64,128]{2,1,0:T(8,128)(2,1)}), bf16[32,64,128]{2,1,0:T(8,128)(2,1)S(1)}, u32[]{:S(2)}, u32[]{:S(2)}) async-start(bf16[32,64,128]{2,1,0:T(8,128)(2,1)} %shard_map.83), calls=%async_computation.2 | async-start | bytes 1048576 | tf_op jit(solution)/shard_map/all_to_all | solution.py:212
  139.1 20.4 %all-to-all-start.3 = ((bf16[32,64,128]{2,1,0:T(8,128)(2,1)}), bf16[32,64,128]{2,1,0:T(8,128)(2,1)S(1)}, u32[]{:S(2)}, u32[]{:S(2)}) async-start(bf16[32,64,128]{2,1,0:T(8,128)(2,1)} %shard_map.84), calls=%async_computation.3 | async-start | bytes 1048576 | tf_op jit(solution)/shard_map/all_to_all | solution.py:212
Sparse Core Ops, SparseCore 0:
  9.4 52.5 all-gather.2
  64.1 41.4 all-gather.4

commit v14 on v13

--- a/solution.py
+++ b/solution.py
@@ -35,9 +35,13 @@
     def _():
         def fill(s, carry):
             blk = jnp.clip(verts_ref[s], 0, ncb - 1)
-            src = pl.multiple_of(blk * BLK, BLK)
+            half = ckv_ref.shape[1] // 2
+            per = half // BLK
+            src = pl.multiple_of((blk % per) * BLK, BLK)
             dst = pl.multiple_of(s * BLK, BLK)
-            kvert[pl.ds(dst, BLK), :] = ckv_ref[pl.ds(src, BLK), :]
+            kvert[pl.ds(dst, BLK), pl.ds(0, HEAD_SIZE)] = ckv_ref[blk // per, pl.ds(src, BLK), :]
+            kvert[pl.ds(dst, BLK), pl.ds(HEAD_SIZE, HEAD_SIZE)] = ckv_ref[
+                blk // per, pl.ds(src + half, BLK), :]
             return carry
 
         lax.fori_loop(0, NVMAX, fill, 0)
@@ -52,7 +56,8 @@
                            preferred_element_type=jnp.float32)
 
 
-def slash_kernel(crow_ref, splane_ref, srow_ref, pick_ref, q_ref, ckv_ref, skv_ref, sbias_ref,
+def slash_kernel(cplane_ref, crow_ref, splane_ref, srow_ref, pick_ref, q_ref, ckv_ref, skv_ref,
+                 sbias_ref,
                  acc_ref, top_ref, total_ref, o_ref, kslash, causal_bias, *, parity):
     nb = STQ // BLK
     nd = NS + 1
@@ -71,10 +76,15 @@
         qb = 2 * (tile * nb + b) + parity
         for d in range(nd):
             at = qb * nd + d
-            from_cache = ckv_ref[pl.ds(pl.multiple_of(crow_ref[at], BLK), BLK), :]
+            half = ckv_ref.shape[1] // 2
+            crow = pl.multiple_of(crow_ref[at], BLK)
+            cplane = cplane_ref[at]
+            take = pick_ref[at] > 0
             from_stretch = skv_ref[splane_ref[at], pl.ds(pl.multiple_of(srow_ref[at], BLK), BLK), :]
-            kslash[b, pl.ds(d * BLK, BLK), :] = jnp.where(pick_ref[at] > 0, from_stretch,
-                                                          from_cache)
+            kslash[b, pl.ds(d * BLK, BLK), pl.ds(0, HEAD_SIZE)] = jnp.where(
+                take, from_stretch[:, :HEAD_SIZE], ckv_ref[cplane, pl.ds(crow, BLK), :])
+            kslash[b, pl.ds(d * BLK, BLK), pl.ds(HEAD_SIZE, HEAD_SIZE)] = jnp.where(
+                take, from_stretch[:, HEAD_SIZE:], ckv_ref[cplane, pl.ds(crow + half, BLK), :])
 
     q3 = q_ref[...].reshape(nb, BLK, HEAD_SIZE)
     s_s = lax.dot_general(q3, kslash[:, :, :HEAD_SIZE], (((2,), (2,)), ((0,), (0,))),
@@ -101,7 +111,7 @@
         grid=(prefill_stretch // TQ,),
         in_specs=[
             pl.BlockSpec((TQ, HEAD_SIZE), lambda i, *_: (i, 0)),
-            pl.BlockSpec(ckv.shape, lambda i, *_: (0, 0)),
+            pl.BlockSpec(ckv.shape, lambda i, *_: (0, 0, 0)),
             pl.BlockSpec((1, nvc), lambda i, *_: (0, 0)),
         ],
         out_specs=[
@@ -139,7 +149,10 @@
     stretch_blk = jnp.clip(blocks - ncb, 0, nqb - 1)
     dev = stretch_blk // per_dev
     pick = (blocks >= ncb).astype(jnp.int32).reshape(-1)
-    crow = (jnp.clip(blocks, 0, ncb - 1) * BLK).reshape(-1)
+    cache_per = ckv.shape[1] // 2 // BLK
+    cache_blk = jnp.clip(blocks, 0, ncb - 1)
+    cplane = (cache_blk // cache_per).reshape(-1)
+    crow = ((cache_blk % cache_per) * BLK).reshape(-1)
     splane = (dev % nz).reshape(-1)
     srow = ((dev // nz) * tok + (stretch_blk % per_dev) * BLK).reshape(-1)
     sbias = jnp.repeat(jnp.where(valid, 0.0, big_negative).astype(jnp.float32), BLK,
@@ -155,11 +168,11 @@
     outs = []
     for parity in range(2):
         grid_spec = pltpu.PrefetchScalarGridSpec(
-            num_scalar_prefetch=4,
+            num_scalar_prefetch=5,
             grid=(halves // nb,),
             in_specs=[
                 pl.BlockSpec((nb, 1, BLK, HEAD_SIZE), lambda i, *_, p=parity: (i, p, 0, 0)),
-                pl.BlockSpec(ckv.shape, lambda i, *_: (0, 0)),
+                pl.BlockSpec(ckv.shape, lambda i, *_: (0, 0, 0)),
                 pl.BlockSpec(skv.shape, lambda i, *_: (0, 0, 0)),
                 pl.BlockSpec((nb, 1, 1, width), lambda i, *_, p=parity: (i, p, 0, 0)),
                 pl.BlockSpec((nb, 1, BLK, HEAD_SIZE), lambda i, *_, p=parity: (i, p, 0, 0)),
@@ -177,7 +190,7 @@
             grid_spec=grid_spec,
             out_shape=jax.ShapeDtypeStruct((halves, BLK, HEAD_SIZE), jnp.bfloat16),
             compiler_params=pltpu.CompilerParams(dimension_semantics=("arbitrary",)),
-        )(crow, splane, srow, pick, q4, ckv, skv, sbias4, acc4, top4, total4))
+        )(cplane, crow, splane, srow, pick, q4, ckv, skv, sbias4, acc4, top4, total4))
     return outs
 
 
@@ -203,8 +216,8 @@
     )
     part = lax.all_to_all(kv_rows, "gx", split_axis=1, concat_axis=0, tiled=True)
     skv = lax.all_gather(part.reshape(nx * tok, 2 * HEAD_SIZE), "gz", axis=0, tiled=False)
-    cache_part = jnp.concatenate([cache_keys[0, 0], cache_values[0, 0]], axis=1)
-    ckv = lax.all_gather(cache_part, "gz", axis=0, tiled=True)
+    cache_part = jnp.concatenate([cache_keys[0, 0], cache_values[0, 0]], axis=0)
+    ckv = lax.all_gather(cache_part, "gz", axis=0, tiled=False)
     halves = head_attention(own_query, ckv, skv, vertical[0, 0], vertical_count[0, 0],
                             slash[0, 0], tok)
     pieces = []

time: 168 us -> 175 us (1.042)
  Pallas kernels: 43.2 us -> 49.7 us
  starting transfers between devices: 27.5 us -> 30.5 us
  waiting for transfers between devices: 60.7 us -> 58.3 us
    pallas_call x2, Pallas kernels: 21.9 us -> 28 us  [head_attention(): pl.pallas_call(functools.partial(slash_kernel, parity=parity), grid_spec=...]
    all_to_all x2, starting transfers between devices: 13.8 us -> 16.8 us  [per_device(): lax.all_to_all(half, ('gx', 'gz'), split_axis=0, concat_axis=0, tiled=True)]
    all_to_all x2, waiting for transfers between devices: 18.2 us -> 15.6 us  [per_device(): lax.all_to_all(half, ('gx', 'gz'), split_axis=0, concat_axis=0, tiled=True)]
  transfers between devices with their start and end apart: 8 -> 8, of which waited for: 7 -> 7; matrix products, arithmetic and copies ran while one was open for 4% -> 3% of each run, Pallas kernels for 19% -> 21%
where the time goes in v14:
time: 175 us; the launch traced here: 174 us
  waiting for transfers between devices  58.3 us (33%)
  Pallas kernels  49.7 us (28%)
  starting transfers between devices  30.5 us (17%)
  between operations  14.2 us (8%)
  blocking collectives  11.6 us (7%)
  local copies, waits for them, and re-layouts  5.24 us (3%)
  other arithmetic  4.55 us (3%)
    pallas_call x2, Pallas kernels, head_attention(): pl.pallas_call(functools.partial(slash_kernel, parity=parity), grid_spec=...  28 us
    all_to_all x1, waiting for transfers between devices, per_device(): lax.all_to_all(q_rows, ('gx', 'gz'), split_axis=1, concat_axis=0, tiled=T...  25 us
    pallas_call x1, Pallas kernels, vertical_part(): pl.pallas_call(vertical_kernel, grid_spec=grid_spec, out_shape=[jax.Shape...  21.7 us
    ppermute x3, waiting for transfers between devices, from_behind(): return lax.ppermute(x, axis, [(i, (i + by) % peers) for i in range(peers)])  17.2 us
    all_to_all x2, starting transfers between devices, per_device(): lax.all_to_all(half, ('gx', 'gz'), split_axis=0, concat_axis=0, tiled=True)  16.8 us
    all_to_all x2, waiting for transfers between devices, per_device(): lax.all_to_all(half, ('gx', 'gz'), split_axis=0, concat_axis=0, tiled=True)  15.6 us
    all_to_all x1, blocking collectives, per_device(): lax.all_to_all(kv_rows, 'gx', split_axis=1, concat_axis=0, tiled=True)  11.6 us
    all_to_all x1, starting transfers between devices, per_device(): lax.all_to_all(q_rows, ('gx', 'gz'), split_axis=1, concat_axis=0, tiled=T...  10.7 us
  transfers between devices with their start and end apart: 8, of which 7 were waited for; matrix products, arithmetic and copies ran while one was open for 3% of the time, Pallas kernels for 21%

profile of v14, /device:TPU:88, one launch (start us, length us, event | category | flops | bytes accessed | tf_op | source)
XLA Modules:
  0.0 174.1 jit_solution(10682264689424290003)
XLA Ops:
  6.5 1.8 %pad_maximum_fusion = bf16[1024,128]{1,0:T(8,128)(2,1)} fusion(bf16[512,128]{1,0:T(8,128)(2,1)} %bitcast.55, bf16[512,128]{1,0:T(8,128)(2,1)} %bitcast.56), kind=kLoop, calls=%fused_computation.3 | loop fusion | flops 524288 | bytes 524288 | tf_op jit(solution)/shard_map/concatenate | solution.py:219
  8.4 2.9 %collective-permute-start.2 = (bf16[1,128,512]{2,1,0:T(8,128)(2,1)}, bf16[1,128,512]{2,1,0:T(8,128)(2,1)S(1)}, u32[]{:S(2)}, u32[]{:S(2)}) collective-permute-start(bf16[1,128,512]{2,1,0:T(8,128)(2,1)} %param.10), channel_id=1, source_target_pairs={{0,32},{32,64},{64,96},{96,128},{128,160},{160,192},{192,224},{224... | collective-permute-start | bytes 393224 | tf_op jit(solution)/shard_map/ppermute | solution.py:26
  11.3 1.7 collective-permute-done.1
  13.1 1.3 collective-permute-done.2
  14.5 11.6 %all_to_all.40 = bf16[128,4,256]{2,0,1:T(8,128)(2,1)} all-to-all(bf16[128,4,256]{2,0,1:T(8,128)(2,1)S(1)} %pad_maximum_fusion.1), channel_id=1, replica_groups=mesh['section'=16,'gx'=4,'gz'=8] {'gx'}, dimensions={1} | all-to-all | bytes 524288 | tf_op jit(solution)/shard_map/all_to_all | solution.py:217
  26.1 14.2 %collective-permute-done = bf16[1,128,4096]{2,1,0:T(8,128)(2,1)S(1)} collective-permute-done((bf16[1,128,4096]{2,1,0:T(8,128)(2,1)S(1)}, bf16[1,128,4096]{2,1,0:T(8,128)(2,1)S(1)}, u32[]{:S(2)}, u32[]{:S(2)}) %collective-permute-start) | collective-permute-done | bytes 1048608 | tf_op jit(solution)/shard_map/ppermute | solution.py:26
  40.4 0.2 copy.39
  40.6 1.4 copy.29
  42.0 10.7 %all-to-all-start = ((bf16[128,32,128]{2,0,1:T(8,128)(2,1)}), bf16[128,32,128]{2,0,1:T(8,128)(2,1)S(1)}, u32[]{:S(2)}, u32[]{:S(2)}) async-start(bf16[128,32,128]{2,0,1:T(8,128)(2,1)} %copy.29), calls=%async_computation | async-start | bytes 2097152 | tf_op jit(solution)/shard_map/all_to_all | solution.py:206
  53.6 0.1 copy.28
  53.7 0.7 reshape.135.pick_ref
  54.4 0.1 and_reduce_fusion
  54.6 0.1 copy.32
  54.7 0.1 copy.27
  54.8 0.1 min.20
  54.9 0.1 copy.26
  55.0 0.1 min.18
  55.1 0.2 broadcast_in_dim.25
  55.3 0.9 reshape_reshape_reshape.4.sbias_ref
  56.3 0.6 compare_select_fusion.vbias_ref
  56.9 0.6 fusion.4
  57.5 25.0 %all-to-all-done = bf16[128,32,128]{2,0,1:T(8,128)(2,1)S(1)} async-done(((bf16[128,32,128]{2,0,1:T(8,128)(2,1)}), bf16[128,32,128]{2,0,1:T(8,128)(2,1)S(1)}, u32[]{:S(2)}, u32[]{:S(2)}) %all-to-all-start) | async-done | bytes 1048608 | tf_op jit(solution)/shard_map/all_to_all | solution.py:206
  82.5 1.0 copy-done
  83.5 21.7 %shard_map.82 = (f32[4096,128]{1,0:T(8,128)}, f32[4096,1]{1,0:T(8,128)}, f32[4096,1]{1,0:T(8,128)}) custom-call(s32[32]{0:T(128)} %bitcast.57, bf16[4096,128]{1,0:T(8,128)(2,1)} %bitcast.43, bf16[8,1024,128]{2,1,0:T(8,128)(2,1)} %bitcast.40, f32[1,2048]{1,0:T(1,128)} %compare_select_fusion.vbias_ref), custom_call_target="tpu_custom_call" | custom-call | tf_op jit(solution)/shard_map/pallas_call | solution.py:124
  105.2 0.4 all-gather.4.cloned.1.call-done.skv_ref
  105.6 14.0 %shard_map.83 = bf16[32,64,128]{2,1,0:T(8,128)(2,1)} custom-call(s32[768]{0:T(1024)} %get-tuple-element.14.cplane_ref, s32[768]{0:T(1024)} %get-tuple-element.13.crow_ref, s32[768]{0:T(1024)} %get-tuple-element.18.splane_ref, s32[768]{0:T(1024)} %get-tuple-element.19.srow_ref, s32[768]{0:T(1024)} %reshape.135.pick_ref, bf16[32,2,64,128]{3,2,1,0:T(8,128)(2,1)} %bitcast.44, ...), custom_call_target="tpu_custom_call" | custom-call | tf_op jit(solution)/shard_map/pallas_call | solution.py:188
  119.6 7.9 %all-to-all-start.2 = ((bf16[32,64,128]{2,1,0:T(8,128)(2,1)}), bf16[32,64,128]{2,1,0:T(8,128)(2,1)S(1)}, u32[]{:S(2)}, u32[]{:S(2)}) async-start(bf16[32,64,128]{2,1,0:T(8,128)(2,1)} %shard_map.83), calls=%async_computation.2 | async-start | bytes 1048576 | tf_op jit(solution)/shard_map/all_to_all | solution.py:225
  127.5 14.0 %shard_map.84 = bf16[32,64,128]{2,1,0:T(8,128)(2,1)} custom-call(s32[768]{0:T(1024)} %get-tuple-element.14.cplane_ref, s32[768]{0:T(1024)} %get-tuple-element.13.crow_ref, s32[768]{0:T(1024)} %get-tuple-element.18.splane_ref, s32[768]{0:T(1024)} %get-tuple-element.19.srow_ref, s32[768]{0:T(1024)} %reshape.135.pick_ref, bf16[32,2,64,128]{3,2,1,0:T(8,128)(2,1)} %bitcast.45, ...), custom_call_target="tpu_custom_call" | custom-call | tf_op jit(solution)/shard_map/pallas_call | solution.py:188
  141.5 0.9 all-to-all-done.2
  142.4 8.9 %all-to-all-start.3 = ((bf16[32,64,128]{2,1,0:T(8,128)(2,1)}), bf16[32,64,128]{2,1,0:T(8,128)(2,1)S(1)}, u32[]{:S(2)}, u32[]{:S(2)}) async-start(bf16[32,64,128]{2,1,0:T(8,128)(2,1)} %shard_map.84), calls=%async_computation.3 | async-start | bytes 1048576 | tf_op jit(solution)/shard_map/all_to_all | solution.py:225
  151.4 14.7 %all-to-all-done.3 = bf16[32,64,128]{2,1,0:T(8,128)(2,1)S(1)} async-done(((bf16[32,64,128]{2,1,0:T(8,128)(2,1)}), bf16[32,64,128]{2,1,0:T(8,128)(2,1)S(1)}, u32[]{:S(2)}, u32[]{:S(2)}) %all-to-all-start.3) | async-done | bytes 524320 | tf_op jit(solution)/shard_map/all_to_all | solution.py:225
  166.2 1.1 maximum_bitcast_fusion
  (27 shorter events, 0.7 us)
Async XLA Ops:
  6.5 19.6 %copy-start.2 = (bf16[1,128,4096]{2,1,0:T(8,128)(2,1)S(1)}, bf16[1,128,4096]{2,1,0:T(8,128)(2,1)}, u32[]{:S(2)}) copy-start(bf16[1,128,4096]{2,1,0:T(8,128)(2,1)} %param.8) | copy-start | bytes 3145732
  6.5 76.0 %all-gather.6.cloned.1.call-start = ((), (), s32[]{:S(2)}) async-start(), calls=%async_computation.5 | async-start | bytes 2359296 | tf_op jit(solution)/shard_map/all_gather | solution.py:220
  8.3 97.2 %all-gather.4.cloned.1.call-start = ((), (), s32[]{:S(2)}) async-start(), calls=%async_computation.4 | async-start | bytes 2359296 | tf_op jit(solution)/shard_map/all_gather | solution.py:218
  8.4 4.6 %collective-permute-start.1 = (bf16[1,128,512]{2,1,0:T(8,128)(2,1)}, bf16[1,128,512]{2,1,0:T(8,128)(2,1)S(1)}, u32[]{:S(2)}, u32[]{:S(2)}) collective-permute-start(bf16[1,128,512]{2,1,0:T(8,128)(2,1)} %param.9), channel_id=1, source_target_pairs={{0,32},{32,64},{64,96},{96,128},{128,160},{160,192},{192,224},{224... | collective-permute-start | bytes 393224 | tf_op jit(solution)/shard_map/ppermute | solution.py:26
  8.4 6.0 %collective-permute-start.2 = (bf16[1,128,512]{2,1,0:T(8,128)(2,1)}, bf16[1,128,512]{2,1,0:T(8,128)(2,1)S(1)}, u32[]{:S(2)}, u32[]{:S(2)}) collective-permute-start(bf16[1,128,512]{2,1,0:T(8,128)(2,1)} %param.10), channel_id=1, source_target_pairs={{0,32},{32,64},{64,96},{96,128},{128,160},{160,192},{192,224},{224... | collective-permute-start | bytes 393224 | tf_op jit(solution)/shard_map/ppermute | solution.py:26
  26.1 14.2 %collective-permute-start = (bf16[1,128,4096]{2,1,0:T(8,128)(2,1)S(1)}, bf16[1,128,4096]{2,1,0:T(8,128)(2,1)S(1)}, u32[]{:S(2)}, u32[]{:S(2)}) collective-permute-start(bf16[1,128,4096]{2,1,0:T(8,128)(2,1)S(1)} %copy-done.2), channel_id=1, source_target_pairs={{0,32},{32,64},{64,96},{96,128},{128,160},{160,192},{192,224},{224... | collective-permute-start | bytes 3145736 | tf_op jit(solution)/shard_map/ppermute | solution.py:26
  40.6 12.8 %copy-start.3 = (s32[1,1,11]{2,1,0:T(1,128)S(1)}, s32[1,1,11]{2,1,0:T(1,128)}, u32[]{:S(2)}) copy-start(s32[1,1,11]{2,1,0:T(1,128)} %param.15) | copy-start | bytes 136
  40.6 13.8 %copy-start.1 = (s32[1,1,32]{2,1,0:T(1,128)S(1)}, s32[1,1,32]{2,1,0:T(1,128)}, u32[]{:S(2)}) copy-start(s32[1,1,32]{2,1,0:T(1,128)} %param.13) | copy-start | bytes 388
  42.0 40.5 %all-to-all-start = ((bf16[128,32,128]{2,0,1:T(8,128)(2,1)}), bf16[128,32,128]{2,0,1:T(8,128)(2,1)S(1)}, u32[]{:S(2)}, u32[]{:S(2)}) async-start(bf16[128,32,128]{2,0,1:T(8,128)(2,1)} %copy.29), calls=%async_computation | async-start | bytes 2097152 | tf_op jit(solution)/shard_map/all_to_all | solution.py:206
  82.5 1.0 copy-start
  119.6 22.9 %all-to-all-start.2 = ((bf16[32,64,128]{2,1,0:T(8,128)(2,1)}), bf16[32,64,128]{2,1,0:T(8,128)(2,1)S(1)}, u32[]{:S(2)}, u32[]{:S(2)}) async-start(bf16[32,64,128]{2,1,0:T(8,128)(2,1)} %shard_map.83), calls=%async_computation.2 | async-start | bytes 1048576 | tf_op jit(solution)/shard_map/all_to_all | solution.py:225
  142.4 23.7 %all-to-all-start.3 = ((bf16[32,64,128]{2,1,0:T(8,128)(2,1)}), bf16[32,64,128]{2,1,0:T(8,128)(2,1)S(1)}, u32[]{:S(2)}, u32[]{:S(2)}) async-start(bf16[32,64,128]{2,1,0:T(8,128)(2,1)} %shard_map.84), calls=%async_computation.3 | async-start | bytes 1048576 | tf_op jit(solution)/shard_map/all_to_all | solution.py:225
Sparse Core Ops, SparseCore 0:
  9.4 52.5 all-gather.5
  64.1 41.4 all-gather.3
